TPU v7x, 256 devices: a whole 4x4x8 slice. The times are simulated.
256 devices in a mesh: view: 8 (over x, y_lo), tile: 32 (over z, y_hi, core).
Axes of the slice: x: 4, y: 4 (y_hi: 2, y_lo: 2; y = y_hi * 2 + y_lo), z: 8, core: 2. Of those that a mesh axis runs over, the one named last changes fastest.
Arguments:
- latents: bfloat16 [16, 2048, 1536], P('view', 'tile'), may hold values from -14 to 14
- qkv_weight: bfloat16 [1536, 3072], replicated, may hold values from -0.15625 to 0.15625
- out_weight: bfloat16 [1024, 1536], replicated, may hold values from -0.1875 to 0.1875
- anchor: int32 [1], replicated, may hold values from 0 to 15
- epi_list: int32 [16, 16, 6], P('view'), may hold values from -1 to 31, as said below
Outputs:
- attn_out: bfloat16 [16, 2048, 1536], P('view', 'tile')
Inputs may be any that keep to these rules, and one draw needn't show every extreme that they name: `epi_list`: row (v, b) lists distinct key blocks: an id c < 16 is block c of view (v - 1) mod 16, an id c >= 16 is block c - 16 of view (v + 1) mod 16; unused slots hold -1 and follow the used ones. Every row uses 1 to 6 slots, with a cap that varies from view to view, and some row uses all 6.
All inputs are finite; a program needn't handle non-finite values.
Results may differ from a plain program's by a relative error of at most 0.005.
The roundings to bfloat16 on the way count: a program that leaves them out, or rounds other values in their place, can miss the bound.
Values may be sent and summed in bfloat16 or wider, within the bound.
No kernel may reach another device: no remote copies, remote signals or barrier semaphores. Data moves between devices by JAX's collectives and lax.ppermute only.
A program may use at most 128 MiB of HBM per device.

v0:
```python
import math

import jax
import jax.numpy as jnp
from jax import lax
from jax.sharding import PartitionSpec as P

HEADS = 8
HD = 128
VT = 2048
BLK = 128
NBLK = 16


def spread_2(array, axis, root):
    mine = lax.axis_index(axis) == root
    return lax.psum(jnp.where(mine, array, jnp.zeros_like(array)), axis)


def from_behind(array, axis, by):
    count = lax.axis_size(axis)
    return lax.ppermute(array, axis, [(i, (i + by) % count) for i in range(count)])


def allowed_tokens(epi_rows):
    blocks = jnp.any(
        epi_rows[:, :, None] == jnp.arange(2 * NBLK, dtype=jnp.int32)[None, None, :], axis=1
    )
    nearby = jnp.repeat(jnp.repeat(blocks, BLK, axis=0), BLK, axis=1)
    always = jnp.ones((VT, VT), dtype=bool)
    return jnp.concatenate([always, nearby, always], axis=1)


def attend(queries, keys_part, values_part, allowed):
    scores = jnp.einsum(
        "qd,kd->qk", queries, keys_part, preferred_element_type=jnp.float32
    ) / math.sqrt(HD)
    scores = jnp.where(allowed, scores, -jnp.inf)
    row_peak = jnp.max(scores, axis=1, keepdims=True)
    raised = jnp.exp(scores - row_peak)
    row_total = jnp.sum(raised, axis=1, keepdims=True)
    weights = raised.astype(jnp.bfloat16)
    summed = jnp.einsum("qk,kd->qd", weights, values_part, preferred_element_type=jnp.float32)
    return (summed / row_total).astype(jnp.bfloat16)


def body(latents, qkv_weight, out_weight, anchor, epi_list):
    per_dev, tile_tokens, model_width = latents.shape
    tile_count = lax.axis_size("tile")
    view_tokens = tile_tokens * tile_count
    parts = max(1, tile_count // (per_dev * HEADS))
    units = per_dev * HEADS * parts // tile_count
    part_rows = view_tokens // parts
    per_view = tile_count // per_dev
    shaped = qkv_weight.reshape(model_width, HEADS, 3 * HD)
    projected = jnp.einsum(
        "vtd,dhc->vhtc", latents, shaped, preferred_element_type=jnp.float32
    ).astype(jnp.bfloat16)
    key_values = projected[..., HD:]

    def spread(source):
        wide = jnp.broadcast_to(source[:, :, None], (per_dev, HEADS, parts) + source.shape[2:])
        return wide.reshape(tile_count, units, tile_tokens, source.shape[-1])

    target = anchor[0]
    anchor_tile = lax.dynamic_index_in_dim(key_values, target % per_dev, 0, keepdims=False)
    anchor_tile = spread_2(anchor_tile, "view", target // per_dev)
    anchor_send = spread(jnp.broadcast_to(anchor_tile[None], key_values.shape))
    boundary = [
        from_behind(key_values[per_dev - 1 if offset == 1 else 0], "view", offset)
        for offset in (1, -1)
    ]
    earlier = jnp.concatenate([boundary[0][None], key_values[:-1]], axis=0)
    following = jnp.concatenate([key_values[1:], boundary[1][None]], axis=0)
    resident, anchored, earlier, following = (
        lax.all_to_all(spread(projected), "tile", split_axis=0, concat_axis=2, tiled=True),
        lax.all_to_all(anchor_send, "tile", split_axis=0, concat_axis=2, tiled=True),
        lax.all_to_all(spread(earlier), "tile", split_axis=0, concat_axis=2, tiled=True),
        lax.all_to_all(spread(following), "tile", split_axis=0, concat_axis=2, tiled=True),
    )
    resident, anchored, earlier, following = (resident[0], anchored[0], earlier[0], following[0])
    tile_index = lax.axis_index("tile")
    local_view = tile_index // per_view
    epi_rows = lax.dynamic_index_in_dim(epi_list, local_view, 0, keepdims=False)
    allowed = allowed_tokens(epi_rows)
    joined = jnp.concatenate([resident[..., HD:], earlier, following, anchored], axis=1)
    block_rows = min(512, part_rows)
    block_count = part_rows // block_rows
    part_ids = (tile_index * units + jnp.arange(units, dtype=jnp.int32)) % parts

    def one_unit(unit_items):
        all_queries, keyvals, part_id = unit_items
        start = part_id * part_rows
        queries = lax.dynamic_slice_in_dim(all_queries, start, part_rows, 0).reshape(
            block_count, block_rows, HD
        )
        mask_rows = lax.dynamic_slice_in_dim(allowed, start, part_rows, 0).reshape(
            block_count, block_rows, 4 * view_tokens
        )

        def one_block(block_items):
            query_rows, block_mask = block_items
            return attend(query_rows, keyvals[:, :HD], keyvals[:, HD:], block_mask)

        return lax.map(one_block, (queries, mask_rows)).reshape(part_rows, HD)

    attended = lax.map(one_unit, (resident[..., :HD], joined, part_ids))
    pieces = attended.reshape(units, tile_count // parts, tile_tokens, HD).transpose(1, 0, 2, 3)
    selected = part_ids[None, :] == jnp.arange(parts, dtype=jnp.int32)[:, None]
    outgoing = jnp.where(
        selected[:, None, :, None, None], pieces[None], jnp.zeros((), jnp.bfloat16)
    )
    outgoing = outgoing.reshape(tile_count, units, tile_tokens, HD)
    returned = lax.all_to_all(outgoing, "tile", split_axis=0, concat_axis=1, tiled=True).reshape(
        per_dev, HEADS, parts, tile_tokens, HD
    )
    own_part = tile_index // (tile_count // parts)
    returned = lax.dynamic_index_in_dim(returned, own_part, 2, keepdims=False)
    projected_out = jnp.einsum(
        "vhtc,hcd->vtd",
        returned,
        out_weight.reshape(HEADS, HD, model_width),
        preferred_element_type=jnp.float32,
    )
    return projected_out.astype(jnp.bfloat16)


def solution(mesh):
    return jax.shard_map(
        body,
        mesh=mesh,
        in_specs=(P("view", "tile", None), P(), P(), P(), P("view", None, None)),
        out_specs=P("view", "tile", None),
        check_vma=False,
    )
```

profile of v0, /device:TPU:1, one launch (start us, length us, event | category | flops | bytes accessed | tf_op | source)
XLA Modules:
  0.0 359.8 jit_solution(12178638410884867979)
XLA Ops:
  7.4 9.8 %copy.35 = bf16[192,8,8,384]{3,2,1,0:T(8,128)(2,1)} copy(bf16[192,8,8,384]{3,1,2,0:T(8,128)(2,1)} %bitcast.80) | data formatting | bytes 18874368
  17.1 5.1 %fusion.38 = bf16[2,8,64,384]{3,2,0,1:T(8,128)(2,1)S(1)} fusion(bf16[1536,8,384,1]{2,1,0,3:T(8,128)(2,1)} %bitcast.81, bf16[2,64,1536]{2,1,0:T(8,128)(2,1)S(1)} %copy-done.3), kind=kOutput, calls=%fused_computation.27 | convolution fusion | flops 1208352768 | bytes 10616832 | tf_op jit(solution)/shard_map/vtd,dhc->vhtc/dot_general | solution.py:56
  25.7 78.0 %all-reduce.2.cloned.1.call-done = bf16[8,64,256]{2,1,0:T(8,128)(2,1)} async-done(((bf16[8,64,256]{2,1,0:T(8,128)(2,1)}), bf16[8,64,256]{2,1,0:T(8,128)(2,1)}) %all-reduce.2.cloned.1.call-update) | async-done | bytes 262160 | tf_op jit(solution)/shard_map/psum | solution.py:17
  103.7 2.0 broadcast_in_dim_broadcast_in_dim_broadcast_in_dim.2
  105.7 15.3 %all-to-all-start.3 = ((bf16[32,1,64,256]{3,2,1,0:T(8,128)(2,1)}), bf16[32,1,64,256]{3,2,1,0:T(8,128)(2,1)}, u32[]{:S(2)}, u32[]{:S(2)}) async-start(bf16[32,1,64,256]{3,2,1,0:T(8,128)(2,1)} %bitcast.83), calls=%async_computation.3 | async-start | bytes 2097152 | tf_op jit(solution)/shard_map/all_to_all | solution.py:77
  122.1 1.7 slice_bitcast_fusion.1
  123.8 10.8 %collective-permute-done = bf16[8,64,256]{2,1,0:T(8,128)(2,1)S(1)} collective-permute-done((bf16[8,64,256]{2,1,0:T(8,128)(2,1)S(1)}, bf16[8,64,256]{2,1,0:T(8,128)(2,1)S(1)}, u32[]{:S(2)}, u32[]{:S(2)}) %collective-permute-start) | collective-permute-done | bytes 262176 | tf_op jit(solution)/shard_map/ppermute | solution.py:22
  135.5 13.6 %all-to-all-done.3 = bf16[32,1,64,256]{3,2,1,0:T(8,128)(2,1)} async-done(((bf16[32,1,64,256]{3,2,1,0:T(8,128)(2,1)}), bf16[32,1,64,256]{3,2,1,0:T(8,128)(2,1)}, u32[]{:S(2)}, u32[]{:S(2)}) %all-to-all-start.3) | async-done | bytes 1048608 | tf_op jit(solution)/shard_map/all_to_all | solution.py:77
  149.1 2.1 broadcast_in_dim.92
  151.2 5.9 %all-to-all-start.1 = ((bf16[32,1,64,256]{3,2,1,0:T(8,128)(2,1)}), bf16[32,1,64,256]{3,2,1,0:T(8,128)(2,1)}, u32[]{:S(2)}, u32[]{:S(2)}) async-start(bf16[32,1,64,256]{3,2,1,0:T(8,128)(2,1)} %bitcast.85), calls=%async_computation.1 | async-start | bytes 2097152 | tf_op jit(solution)/shard_map/all_to_all | solution.py:78
  157.1 2.1 copy.26
  159.2 26.0 %all-to-all-done.1 = bf16[32,1,64,256]{3,2,1,0:T(8,128)(2,1)} async-done(((bf16[32,1,64,256]{3,2,1,0:T(8,128)(2,1)}), bf16[32,1,64,256]{3,2,1,0:T(8,128)(2,1)}, u32[]{:S(2)}, u32[]{:S(2)}) %all-to-all-start.1) | async-done | bytes 1048608 | tf_op jit(solution)/shard_map/all_to_all | solution.py:78
  185.2 2.5 broadcast_in_dim.90
  187.8 5.9 %all-to-all-start = ((bf16[32,1,64,384]{3,2,1,0:T(8,128)(2,1)}), bf16[32,1,64,384]{3,2,1,0:T(8,128)(2,1)}, u32[]{:S(2)}, u32[]{:S(2)}) async-start(bf16[32,1,64,384]{3,2,1,0:T(8,128)(2,1)} %bitcast.82), calls=%async_computation | async-start | bytes 3145728 | tf_op jit(solution)/shard_map/all_to_all | solution.py:76
  195.2 11.2 %broadcast_in_dim.89 = pred[2048,32,128]{2,1,0:T(8,128)(4,1)S(1)} broadcast(pred[2048,32]{1,0:T(8,128)(4,1)S(1)} %bitcast.89), dimensions={0,1} | broadcast | bytes 8454144 | tf_op jit(solution)/shard_map/broadcast_in_dim | solution.py:29
  206.5 7.9 %copy.46 = pred[256,8,32,128]{3,1,2,0:T(8,128)(4,1)} copy(pred[256,8,32,128]{3,2,1,0:T(8,128)(4,1)S(1)} %bitcast.79) | data formatting | bytes 16777216
  214.6 1.8 pad_maximum_fusion.1
  216.4 16.6 %all-to-all-done = bf16[32,1,64,384]{3,2,1,0:T(8,128)(2,1)} async-done(((bf16[32,1,64,384]{3,2,1,0:T(8,128)(2,1)}), bf16[32,1,64,384]{3,2,1,0:T(8,128)(2,1)}, u32[]{:S(2)}, u32[]{:S(2)}) %all-to-all-start) | async-done | bytes 1572896 | tf_op jit(solution)/shard_map/all_to_all | solution.py:76
  232.9 2.1 broadcast_in_dim.94
  235.1 6.3 %all-to-all-start.2 = ((bf16[32,1,64,256]{3,2,1,0:T(8,128)(2,1)}), bf16[32,1,64,256]{3,2,1,0:T(8,128)(2,1)}, u32[]{:S(2)}, u32[]{:S(2)}) async-start(bf16[32,1,64,256]{3,2,1,0:T(8,128)(2,1)} %bitcast.84), calls=%async_computation.2 | async-start | bytes 2097152 | tf_op jit(solution)/shard_map/all_to_all | solution.py:79
  242.5 7.9 %fusion.31 = pred[1024,8192]{1,0:T(32,128)(4,1)} fusion(s32[]{:T(128)S(6)} %select_n.67, pred[2048,2048]{1,0:T(32,128)(4,1)S(1)} %broadcast_in_dim.87, pred[2048,4096]{1,0:T(8,128)(4,1)} %bitcast.78), kind=kLoop, calls=%fused_computation.19 | loop fusion | flops 16777216 | bytes 20971524 | tf_op jit(solution)/shard_map/concatenate | solution.py:31
  250.4 2.3 slice.31
  253.8 15.5 %all-to-all-done.2 = bf16[32,1,64,256]{3,2,1,0:T(8,128)(2,1)} async-done(((bf16[32,1,64,256]{3,2,1,0:T(8,128)(2,1)}), bf16[32,1,64,256]{3,2,1,0:T(8,128)(2,1)}, u32[]{:S(2)}, u32[]{:S(2)}) %all-to-all-start.2) | async-done | bytes 1048608 | tf_op jit(solution)/shard_map/all_to_all | solution.py:79
  269.3 3.8 %maximum_bitcast_fusion = bf16[8192,256]{1,0:T(8,128)(2,1)} fusion(bf16[1,2048,256]{2,1,0:T(8,128)(2,1)} %bitcast.26, bf16[1,2048,256]{2,1,0:T(8,128)(2,1)} %bitcast.22, bf16[1,2048,256]{2,1,0:T(8,128)(2,1)} %bitcast.18, bf16[1,2048,256]{2,1,0:T(8,128)(2,1)} %slice.31), kind=kLoop, calls=%fused_computation.23 | loop fusion | flops 16777216 | bytes 8388608 | tf_op jit(solution)/shard_map/while/body/jit(dynamic_index_in_dim)/squeeze | solution.py:107
  273.1 54.6 %while.17 = (s32[]{:T(128)}, bf16[2,512,128]{2,1,0:T(8,128)(2,1)}, pred[2,512,8192]{2,1,0:T(32,128)(4,1)}, bf16[2,512,128]{2,1,0:T(8,128)(2,1)S(1)}, bf16[8192,256]{1,0:T(8,128)(2,1)}, /*index=5*/s32[]{:T(128)}) while((s32[]{:T(128)}, bf16[2,512,128]{2,1,0:T(8,128)(2,1)}, pred[2,512,8192]{2,1,0:T(32,128)(4,1)}, ...), condition=%wide.region_5.6_spmd, body=%wide.region_2.5_spmd.sunk | while | flops 2176973824 | bytes 58994244 | solution.py:105
  273.1 9.8 %fusion.56 = (f32[512]{0:T(512)S(1)}, f32[512,8192]{1,0:T(8,128)}) fusion(bf16[8192,256]{1,0:T(8,128)(2,1)} %get-tuple-element.118, bf16[2,512,128]{2,1,0:T(8,128)(2,1)S(1)} %get-tuple-element.117, s32[]{:T(128)} %get-tuple-element.108, pred[2,512,8192]{2,1,0:T(32,128)(4,1)} %get-tuple-element.116), kind=kOutput, calls=%fused_computation.45.clone.1 | convolution fusion | flops 1086324224 | bytes 23202816 | tf_op jit(solution)/shard_map/while/body/eval_jaxpr/while/body/eval_jaxpr/qd,kd->qk/dot_general | solution.py:35
  282.9 8.1 %fusion.57 = f32[512]{0:T(512)S(1)} fusion(f32[512,8192]{1,0:T(8,128)} %get-tuple-element.100, f32[512]{0:T(512)S(1)} %get-tuple-element.101), kind=kLoop, calls=%fused_computation.2.clone.1 | loop fusion | flops 8388096 | bytes 16781312 | tf_op jit(solution)/shard_map/while/body/eval_jaxpr/while/body/eval_jaxpr/reduce_sum | solution.py:41
  291.0 9.4 %fusion.58 = bf16[2,512,128]{2,1,0:T(8,128)(2,1)} fusion(bf16[2,512,128]{2,1,0:T(8,128)(2,1)} %get-tuple-element.109, s32[]{:T(128)} %get-tuple-element.108, bf16[8192,256]{1,0:T(8,128)(2,1)} %get-tuple-element.118, f32[512,8192]{1,0:T(8,128)} %get-tuple-element.100, f32[512]{0:T(512)S(1)} %get-tuple-element.101, f32[512]{0:T(512)S(1)} %fusion.57), kind=kOutput, calls=%fused_computation.11.clone.1 | convolution fusion | flops 1082261504 | bytes 19010048 | tf_op jit(solution)/shard_map/while/body/eval_jaxpr/while/body/eval_jaxpr/qk,kd->qd/dot_general | solution.py:43
  300.4 9.8 %fusion.56 = (f32[512]{0:T(512)S(1)}, f32[512,8192]{1,0:T(8,128)}) fusion(bf16[8192,256]{1,0:T(8,128)(2,1)} %get-tuple-element.118, bf16[2,512,128]{2,1,0:T(8,128)(2,1)S(1)} %get-tuple-element.117, s32[]{:T(128)} %get-tuple-element.108, pred[2,512,8192]{2,1,0:T(32,128)(4,1)} %get-tuple-element.116), kind=kOutput, calls=%fused_computation.45.clone.1 | convolution fusion | flops 1086324224 | bytes 23202816 | tf_op jit(solution)/shard_map/while/body/eval_jaxpr/while/body/eval_jaxpr/qd,kd->qk/dot_general | solution.py:35
  310.2 8.1 %fusion.57 = f32[512]{0:T(512)S(1)} fusion(f32[512,8192]{1,0:T(8,128)} %get-tuple-element.100, f32[512]{0:T(512)S(1)} %get-tuple-element.101), kind=kLoop, calls=%fused_computation.2.clone.1 | loop fusion | flops 8388096 | bytes 16781312 | tf_op jit(solution)/shard_map/while/body/eval_jaxpr/while/body/eval_jaxpr/reduce_sum | solution.py:41
  318.3 9.4 %fusion.58 = bf16[2,512,128]{2,1,0:T(8,128)(2,1)} fusion(bf16[2,512,128]{2,1,0:T(8,128)(2,1)} %get-tuple-element.109, s32[]{:T(128)} %get-tuple-element.108, bf16[8192,256]{1,0:T(8,128)(2,1)} %get-tuple-element.118, f32[512,8192]{1,0:T(8,128)} %get-tuple-element.100, f32[512]{0:T(512)S(1)} %get-tuple-element.101, f32[512]{0:T(512)S(1)} %fusion.57), kind=kOutput, calls=%fused_computation.11.clone.1 | convolution fusion | flops 1082261504 | bytes 19010048 | tf_op jit(solution)/shard_map/while/body/eval_jaxpr/while/body/eval_jaxpr/qk,kd->qd/dot_general | solution.py:43
  328.9 22.7 %all_to_all.20 = bf16[32,1,64,128]{3,2,1,0:T(8,128)(2,1)S(1)} all-to-all(bf16[32,1,64,128]{3,2,1,0:T(8,128)(2,1)S(1)} %broadcast_select_fusion), channel_id=1, replica_groups=mesh['view'=8,'tile'=32] {'tile'}, dimensions={0} | all-to-all | bytes 1048576 | tf_op jit(solution)/shard_map/all_to_all | solution.py:114
  (31 shorter events, 11.8 us)
Async XLA Ops:
  6.5 345.1 %copy-start = (bf16[1024,1536]{1,0:T(8,128)(2,1)S(1)}, bf16[1024,1536]{1,0:T(8,128)(2,1)}, u32[]{:S(2)}) copy-start(bf16[1024,1536]{1,0:T(8,128)(2,1)} %param.9) | copy-start | bytes 9437188
  6.5 97.1 %all-reduce.2.cloned.1.call-start = ((), (), s32[]{:S(2)}) async-start(), calls=%async_computation.5 | async-start | bytes 524288 | tf_op jit(solution)/shard_map/psum | solution.py:17
  7.4 9.8 %copy-start.3 = (bf16[2,64,1536]{2,1,0:T(8,128)(2,1)S(1)}, bf16[2,64,1536]{2,1,0:T(8,128)(2,1)}, u32[]{:S(2)}) copy-start(bf16[2,64,1536]{2,1,0:T(8,128)(2,1)} %param.7) | copy-start | bytes 1179652
  22.2 0.9 copy-start.1
  25.7 169.3 %copy-start.2 = (s32[2,16,6]{1,0,2:T(2,128)S(1)}, s32[2,16,6]{1,0,2:T(2,128)}, u32[]{:S(2)}) copy-start(s32[2,16,6]{1,0,2:T(2,128)} %param.11) | copy-start | bytes 2308
  105.7 43.4 %all-to-all-start.3 = ((bf16[32,1,64,256]{3,2,1,0:T(8,128)(2,1)}), bf16[32,1,64,256]{3,2,1,0:T(8,128)(2,1)}, u32[]{:S(2)}, u32[]{:S(2)}) async-start(bf16[32,1,64,256]{3,2,1,0:T(8,128)(2,1)} %bitcast.83), calls=%async_computation.3 | async-start | bytes 2097152 | tf_op jit(solution)/shard_map/all_to_all | solution.py:77
  122.0 12.6 %collective-permute-start = (bf16[8,64,256]{2,1,0:T(8,128)(2,1)S(1)}, bf16[8,64,256]{2,1,0:T(8,128)(2,1)S(1)}, u32[]{:S(2)}, u32[]{:S(2)}) collective-permute-start(bf16[8,64,256]{2,1,0:T(8,128)(2,1)S(1)} %get-tuple-element.63), channel_id=1, source_target_pairs={{0,32},{32,64},{64,96},{96,128},{128,160},{160,192},{192,224},{224... | collective-permute-start | bytes 786440 | tf_op jit(solution)/shard_map/ppermute | solution.py:22
  151.2 34.0 %all-to-all-start.1 = ((bf16[32,1,64,256]{3,2,1,0:T(8,128)(2,1)}), bf16[32,1,64,256]{3,2,1,0:T(8,128)(2,1)}, u32[]{:S(2)}, u32[]{:S(2)}) async-start(bf16[32,1,64,256]{3,2,1,0:T(8,128)(2,1)} %bitcast.85), calls=%async_computation.1 | async-start | bytes 2097152 | tf_op jit(solution)/shard_map/all_to_all | solution.py:78
  187.8 45.2 %all-to-all-start = ((bf16[32,1,64,384]{3,2,1,0:T(8,128)(2,1)}), bf16[32,1,64,384]{3,2,1,0:T(8,128)(2,1)}, u32[]{:S(2)}, u32[]{:S(2)}) async-start(bf16[32,1,64,384]{3,2,1,0:T(8,128)(2,1)} %bitcast.82), calls=%async_computation | async-start | bytes 3145728 | tf_op jit(solution)/shard_map/all_to_all | solution.py:76
  193.6 20.9 %collective-permute-start.1 = (bf16[8,64,256]{2,1,0:T(8,128)(2,1)}, bf16[8,64,256]{2,1,0:T(8,128)(2,1)}, u32[]{:S(2)}, u32[]{:S(2)}) collective-permute-start(bf16[8,64,256]{2,1,0:T(8,128)(2,1)} %get-tuple-element.66), channel_id=1, source_target_pairs={{0,224},{32,0},{64,32},{96,64},{128,96},{160,128},{192,160},{224,1... | collective-permute-start | bytes 786440 | tf_op jit(solution)/shard_map/ppermute | solution.py:22
  235.1 34.2 %all-to-all-start.2 = ((bf16[32,1,64,256]{3,2,1,0:T(8,128)(2,1)}), bf16[32,1,64,256]{3,2,1,0:T(8,128)(2,1)}, u32[]{:S(2)}, u32[]{:S(2)}) async-start(bf16[32,1,64,256]{3,2,1,0:T(8,128)(2,1)} %bitcast.84), calls=%async_computation.2 | async-start | bytes 2097152 | tf_op jit(solution)/shard_map/all_to_all | solution.py:79
Sparse Core Ops, SparseCore 0:
  25.8 77.8 all-reduce.1
where the time goes:
time: 361 us; the launch traced here: 360 us
  waiting for transfers between devices  161 us (45%)
  local copies, waits for them, and re-layouts  50 us (14%)
  matrix products  44.8 us (12%)
  starting transfers between devices  34.8 us (10%)
  other arithmetic  32.4 us (9%)
  blocking collectives  22.7 us (6%)
  between operations  14.4 us (4%)
    psum x1, waiting for transfers between devices, spread_2(): return lax.psum(jnp.where(mine, array, jnp.zeros_like(array)), axis)  78 us
    all_to_all x1, waiting for transfers between devices, body(): lax.all_to_all(spread(earlier), 'tile', split_axis=0, concat_axis=2, tile...  26 us
    all_to_all x1, blocking collectives, body(): lax.all_to_all(outgoing, 'tile', split_axis=0, concat_axis=1, tiled=True)  22.7 us
    dot_general x2, matrix products, attend(): jnp.einsum('qd,kd->qk', queries, keys_part, preferred_element_type=jnp.fl...  19.6 us
    dot_general x2, matrix products, attend(): jnp.einsum('qk,kd->qd', weights, values_part, preferred_element_type=jnp....  18.8 us
    unnamed x11, local copies, waits for them, and re-layouts  18.6 us
    all_to_all x1, waiting for transfers between devices, body(): lax.all_to_all(spread(projected), 'tile', split_axis=0, concat_axis=2, ti...  16.6 us
    reduce_sum x2, other arithmetic, attend(): row_total = jnp.sum(raised, axis=1, keepdims=True)  16.2 us
  transfers between devices with their start and end apart: 7, of which 6 were waited for; matrix products, arithmetic and copies ran while one was open for 11% of the time, Pallas kernels for 0%

commit v1 on v0

v1 whole, which is shorter than its diff:
```python
import math

import jax
import jax.numpy as jnp
from jax import lax
from jax.sharding import Mesh
from jax.sharding import PartitionSpec as P

HEADS = 8
HD = 128
VT = 2048
BLK = 128
NBLK = 16

SUB = ("zh", "zl", "yhi", "core")
HALF = ("zl", "yhi", "core")


def allowed_tokens(epi_rows, rows):
    blocks = jnp.any(
        epi_rows[:, :, None] == jnp.arange(2 * NBLK, dtype=jnp.int32)[None, None, :], axis=1
    )
    nearby = jnp.repeat(jnp.repeat(blocks, BLK, axis=0), BLK, axis=1)
    always = jnp.ones((rows, VT), dtype=bool)
    return jnp.concatenate([always, nearby, always], axis=1)


def attend(queries, keys_part, values_part, allowed):
    scores = jnp.einsum(
        "qd,kd->qk", queries, keys_part, preferred_element_type=jnp.float32
    ) / math.sqrt(HD)
    scores = jnp.where(allowed, scores, -jnp.inf)
    row_peak = jnp.max(scores, axis=1, keepdims=True)
    raised = jnp.exp(scores - row_peak)
    row_total = jnp.sum(raised, axis=1, keepdims=True)
    weights = raised.astype(jnp.bfloat16)
    summed = jnp.einsum("qk,kd->qd", weights, values_part, preferred_element_type=jnp.float32)
    return (summed / row_total).astype(jnp.bfloat16)


def broadcast_view(value, root, count):
    me = lax.axis_index("view")
    dist = (me - root) % count
    held = jnp.where(dist == 0, value, jnp.zeros_like(value))
    step = 1
    while step < count:
        got = lax.ppermute(held, "view", [(i, (i + step) % count) for i in range(count)])
        held = jnp.where((dist >= step) & (dist < 2 * step), got, held)
        step *= 2
    return held


def body(latents, qkv_weight, out_weight, anchor, epi_list):
    per_dev, tile_tokens, model_width = latents.shape
    views_n = lax.axis_size("view")
    half_n = lax.axis_size(HALF)
    tile_n = lax.axis_size(SUB)
    part_rows = tile_tokens * half_n
    core_n = lax.axis_size("core")
    slot = lax.axis_index("core")
    half = lax.axis_index("zh")

    shaped = qkv_weight.reshape(model_width, HEADS, 3 * HD)
    projected = jnp.einsum(
        "vtd,dhc->hvtc", latents, shaped, preferred_element_type=jnp.float32
    ).astype(jnp.bfloat16)
    queries = projected[..., :HD]
    key_values = projected[..., HD:]

    target = anchor[0]
    anchor_tile = lax.dynamic_index_in_dim(key_values, target % per_dev, 1, keepdims=False)
    anchor_tile = broadcast_view(anchor_tile, target // per_dev, views_n)

    q_send = queries.reshape(HEADS * per_dev, tile_tokens, HD)
    q_mine = lax.all_to_all(q_send, HALF, 0, 0, tiled=True).reshape(part_rows, HD)

    kv_send = jnp.concatenate(
        [key_values, jnp.broadcast_to(anchor_tile[:, None], key_values.shape)], axis=-1
    ).reshape(HEADS * per_dev, tile_tokens, 4 * HD)
    kv_send = jnp.broadcast_to(kv_send[None], (tile_n // (HEADS * per_dev),) + kv_send.shape)
    kv_send = kv_send.reshape(tile_n, tile_tokens, 4 * HD)
    kv_all = lax.all_to_all(kv_send, SUB, 0, 0, tiled=True).reshape(tile_n * tile_tokens, 4 * HD)
    own_kv = kv_all[:, : 2 * HD]
    anchored = kv_all[:, 2 * HD :]

    other = lax.ppermute(own_kv, "core", [(0, 1), (1, 0)])
    pairs = []
    for v in range(views_n):
        for c in range(core_n):
            dest_view = (v + 1) % views_n if c == 1 else (v - 1) % views_n
            pairs.append((v * core_n + c, dest_view * core_n + (1 - c)))
    far = lax.ppermute(own_kv, ("view", "core"), pairs)
    earlier = jnp.where(slot == 1, other, far)
    following = jnp.where(slot == 1, far, other)

    epi_rows = lax.dynamic_index_in_dim(epi_list, slot, 0, keepdims=False)
    epi_rows = lax.dynamic_slice_in_dim(epi_rows, half * (part_rows // BLK), part_rows // BLK, 0)
    allowed = allowed_tokens(epi_rows, part_rows)
    joined = jnp.concatenate([own_kv, earlier, following, anchored], axis=0)

    block_rows = min(512, part_rows)
    block_count = part_rows // block_rows
    q_blocks = q_mine.reshape(block_count, block_rows, HD)
    mask_blocks = allowed.reshape(block_count, block_rows, 4 * VT)

    def one_block(items):
        query_rows, block_mask = items
        return attend(query_rows, joined[:, :HD], joined[:, HD:], block_mask)

    attended = lax.map(one_block, (q_blocks, mask_blocks)).reshape(half_n, tile_tokens, HD)
    returned = lax.all_to_all(attended, HALF, 0, 0, tiled=True)
    returned = returned.reshape(HEADS, per_dev, tile_tokens, HD)
    projected_out = jnp.einsum(
        "hvtc,hcd->vtd",
        returned,
        out_weight.reshape(HEADS, HD, model_width),
        preferred_element_type=jnp.float32,
    )
    return projected_out.astype(jnp.bfloat16)


def solution(mesh):
    views_n, tile_n = mesh.devices.shape
    fine = Mesh(
        mesh.devices.reshape(views_n, 2, tile_n // 8, 2, 2),
        ("view",) + SUB,
    )
    return jax.shard_map(
        body,
        mesh=fine,
        in_specs=(P("view", SUB, None), P(), P(), P(), P("view", None, None)),
        out_specs=P("view", SUB, None),
        check_vma=False,
    )
```

time: 361 us -> 230 us (0.64)
  waiting for transfers between devices: 161 us -> 63.1 us
  between operations: 14.4 us -> 0.96 us
  local copies, waits for them, and re-layouts: 50 us -> 39.7 us
  blocking collectives: 22.7 us -> 18.3 us
  starting transfers between devices: 34.8 us -> 31 us
    psum x1 -> x0, waiting for transfers between devices: 78 us -> none  [spread_2(): return lax.psum(jnp.where(mine, array, jnp.zeros_like(array)), axis)]
    all_to_all x4 -> x2, waiting for transfers between devices: 71.8 us -> 27.1 us  [the longest x1 27.1 us: body(): lax.all_to_all(kv_send, SUB, 0, 0, tiled=True)]
    ppermute x2 -> x5, waiting for transfers between devices: 10.9 us -> 36 us  [the longest x1 20.9 us: body(): far = lax.ppermute(own_kv, ('view', 'core'), pairs)]
    concatenate x0 -> x1, local copies, waits for them, and re-layouts: none -> 12 us  [allowed_tokens(): return jnp.concatenate([always, nearby, always], axis=1)]
    all_to_all x4 -> x2, starting transfers between devices: 33.4 us -> 22.7 us  [the longest x1 16.5 us: body(): lax.all_to_all(kv_send, SUB, 0, 0, tiled=True)]
    unnamed x11, local copies, waits for them, and re-layouts: 18.6 us -> 10.6 us
    broadcast_in_dim x7 -> x3, local copies, waits for them, and re-layouts: 9.09 us -> 2.18 us  [the longest x1 1.59 us: body(): jnp.broadcast_to(kv_send[None], (tile_n // (HEADS * per_dev),) + kv_send....]
    ppermute x2 -> x5, starting transfers between devices: 1.48 us -> 8.28 us  [the longest x3 8.17 us: broadcast_view(): lax.ppermute(held, 'view', [(i, (i + step) % count) for i in range(count)])]
  transfers between devices with their start and end apart: 7 -> 7, of which waited for: 6 -> 5; matrix products, arithmetic and copies ran while one was open for 11% -> 16% of each run, Pallas kernels for 0% -> 0%
where the time goes in v1:
time: 230 us; the launch traced here: 228 us
  waiting for transfers between devices  63.1 us (27%)
  matrix products  44.8 us (19%)
  local copies, waits for them, and re-layouts  39.7 us (17%)
  starting transfers between devices  31 us (13%)
  other arithmetic  29.9 us (13%)
  blocking collectives  18.3 us (8%)
    all_to_all x1, waiting for transfers between devices, body(): lax.all_to_all(kv_send, SUB, 0, 0, tiled=True)  27.1 us
    ppermute x1, waiting for transfers between devices, body(): far = lax.ppermute(own_kv, ('view', 'core'), pairs)  20.9 us
    dot_general x2, matrix products, attend(): jnp.einsum('qd,kd->qk', queries, keys_part, preferred_element_type=jnp.fl...  19.6 us
    dot_general x2, matrix products, attend(): jnp.einsum('qk,kd->qd', weights, values_part, preferred_element_type=jnp....  18.8 us
    all_to_all x1, blocking collectives, body(): returned = lax.all_to_all(attended, HALF, 0, 0, tiled=True)  18.3 us
    all_to_all x1, starting transfers between devices, body(): lax.all_to_all(kv_send, SUB, 0, 0, tiled=True)  16.5 us
    reduce_sum x2, other arithmetic, attend(): row_total = jnp.sum(raised, axis=1, keepdims=True)  16.2 us
    ppermute x3, waiting for transfers between devices, broadcast_view(): lax.ppermute(held, 'view', [(i, (i + step) % count) for i in range(count)])  15.1 us
  transfers between devices with their start and end apart: 7, of which 5 were waited for; matrix products, arithmetic and copies ran while one was open for 16% of the time, Pallas kernels for 0%

profile of v1, /device:TPU:1, one launch (start us, length us, event | category | flops | bytes accessed | tf_op | source)
XLA Modules:
  0.0 227.7 jit_solution(15731606136216869912)
XLA Ops:
  0.9 9.7 %copy.20 = bf16[192,8,8,384]{3,2,1,0:T(8,128)(2,1)} copy(bf16[192,8,8,384]{3,1,2,0:T(8,128)(2,1)} %bitcast.57) | data formatting | bytes 18874368
  10.6 5.1 %fusion.36 = bf16[8,2,64,384]{3,2,1,0:T(8,128)(2,1)S(1)} fusion(bf16[1536,8,384,1]{2,1,0,3:T(8,128)(2,1)} %bitcast.58, bf16[2,64,1536]{2,1,0:T(8,128)(2,1)S(1)} %copy-done.4), kind=kOutput, calls=%fused_computation.22 | convolution fusion | flops 1208352768 | bytes 10616832 | tf_op jit(solution)/shard_map/vtd,dhc->hvtc/dot_general | solution.py:64
  17.4 1.0 select_bitcast_fusion
  18.4 2.2 collective-permute-start
  20.6 6.1 %collective-permute-done = bf16[8,64,256]{2,1,0:T(8,128)(2,1)} collective-permute-done((bf16[8,64,256]{2,1,0:T(8,128)(2,1)S(1)}, bf16[8,64,256]{2,1,0:T(8,128)(2,1)}, u32[]{:S(2)}, u32[]{:S(2)}) %collective-permute-start) | collective-permute-done | bytes 262176 | tf_op jit(solution)/shard_map/ppermute | solution.py:47
  26.6 1.0 broadcast_select_fusion.2
  27.6 2.2 collective-permute-start.1
  29.8 5.1 %collective-permute-done.1 = bf16[8,64,256]{2,1,0:T(8,128)(2,1)} collective-permute-done((bf16[8,64,256]{2,1,0:T(8,128)(2,1)S(1)}, bf16[8,64,256]{2,1,0:T(8,128)(2,1)}, u32[]{:S(2)}, u32[]{:S(2)}) %collective-permute-start.1) | collective-permute-done | bytes 262176 | tf_op jit(solution)/shard_map/ppermute | solution.py:47
  35.6 3.8 %collective-permute-start.2 = (bf16[8,64,256]{2,1,0:T(8,128)(2,1)}, bf16[8,64,256]{2,1,0:T(8,128)(2,1)S(1)}, u32[]{:S(2)}, u32[]{:S(2)}) collective-permute-start(bf16[8,64,256]{2,1,0:T(8,128)(2,1)} %broadcast_select_fusion.3), channel_id=1, source_target_pairs={{0,128},{32,160},{64,192},{96,224},{128,0},{160,32},{192,64},{224,... | collective-permute-start | bytes 786440 | tf_op jit(solution)/shard_map/ppermute | solution.py:47
  39.4 4.0 %collective-permute-done.2 = bf16[8,64,256]{2,1,0:T(8,128)(2,1)S(1)} collective-permute-done((bf16[8,64,256]{2,1,0:T(8,128)(2,1)}, bf16[8,64,256]{2,1,0:T(8,128)(2,1)S(1)}, u32[]{:S(2)}, u32[]{:S(2)}) %collective-permute-start.2) | collective-permute-done | bytes 262176 | tf_op jit(solution)/shard_map/ppermute | solution.py:47
  43.5 1.1 pad_maximum_fusion.1
  44.6 1.6 broadcast_in_dim.47
  46.2 16.5 %all-to-all-start.1 = ((bf16[32,64,512]{2,1,0:T(8,128)(2,1)}), bf16[32,64,512]{2,1,0:T(8,128)(2,1)}, u32[]{:S(2)}, u32[]{:S(2)}) async-start(bf16[32,64,512]{2,1,0:T(8,128)(2,1)} %bitcast.59), calls=%async_computation.1 | async-start | bytes 4194304 | tf_op jit(solution)/shard_map/all_to_all | solution.py:82
  62.7 1.7 slice.22
  64.6 9.1 %broadcast_in_dim.43 = pred[1024,32,128]{2,1,0:T(32,128)(4,1)} broadcast(pred[1024,32]{1,0:T(8,128)(4,1)S(1)} %bitcast.64), dimensions={0,1} | broadcast | bytes 4227072 | tf_op jit(solution)/shard_map/broadcast_in_dim | solution.py:23
  73.7 12.0 %concatenate.12 = pred[2,512,4096]{2,1,0:T(32,128)(4,1)} reshape(pred[1024,32,128]{2,1,0:T(32,128)(4,1)} %broadcast_in_dim.43) | data formatting | bytes 8388608 | tf_op jit(solution)/shard_map/concatenate | solution.py:25
  85.7 27.1 %all-to-all-done.1 = bf16[32,64,512]{2,1,0:T(8,128)(2,1)} async-done(((bf16[32,64,512]{2,1,0:T(8,128)(2,1)}), bf16[32,64,512]{2,1,0:T(8,128)(2,1)}, u32[]{:S(2)}, u32[]{:S(2)}) %all-to-all-start.1) | async-done | bytes 2097184 | tf_op jit(solution)/shard_map/all_to_all | solution.py:82
  112.8 6.2 %all-to-all-start = ((bf16[16,64,128]{2,1,0:T(8,128)(2,1)}), bf16[16,64,128]{2,1,0:T(8,128)(2,1)S(1)}, u32[]{:S(2)}, u32[]{:S(2)}) async-start(bf16[16,64,128]{2,1,0:T(8,128)(2,1)} %bitcast.63), calls=%async_computation | async-start | bytes 524288 | tf_op jit(solution)/shard_map/all_to_all | solution.py:75
  119.0 3.1 %fusion.42 = (bf16[2048,256]{1,0:T(8,128)(2,1)}, bf16[2048,256]{1,0:T(8,128)(2,1)}) fusion(bf16[2048,512]{1,0:T(8,128)(2,1)} %bitcast.14), kind=kLoop, calls=%fused_computation.36 | loop fusion | bytes 4194304 | tf_op jit(solution)/shard_map/slice | solution.py:83
  122.8 4.6 %pad_add_fusion = pred[2,512,8192]{2,1,0:T(32,128)(4,1)} fusion(pred[2,512,2048]{2,1,0:T(32,128)(4,1)S(1)} %broadcast_in_dim.41, pred[2,512,4096]{2,1,0:T(32,128)(4,1)S(1)} %copy-done.1), kind=kLoop, calls=%fused_computation.15 | loop fusion | flops 16777216 | bytes 14680064 | tf_op jit(solution)/shard_map/concatenate | solution.py:25
  127.5 20.9 %collective-permute-done.4 = bf16[2048,256]{1,0:T(8,128)(2,1)} collective-permute-done((bf16[2048,256]{1,0:T(8,128)(2,1)}, bf16[2048,256]{1,0:T(8,128)(2,1)}, u32[]{:S(2)}, u32[]{:S(2)}) %collective-permute-start.4) | collective-permute-done | bytes 1048608 | tf_op jit(solution)/shard_map/ppermute | solution.py:92
  148.3 1.7 broadcast_select_fusion.1
  150.0 3.4 %pad_maximum_fusion = bf16[8192,256]{1,0:T(8,128)(2,1)} fusion(bf16[2048,256]{1,0:T(8,128)(2,1)} %get-tuple-element.48, bf16[2048,256]{1,0:T(8,128)(2,1)S(1)} %get-tuple-element.46, bf16[2048,256]{1,0:T(8,128)(2,1)S(1)} %get-tuple-element.45, bf16[2048,256]{1,0:T(8,128)(2,1)} %get-tuple-element.47), kind=kLoop, calls=%fused_computation.18 | loop fusion | flops 16777216 | bytes 8388608 | tf_op jit(solution)/shard_map/concatenate | solution.py:99
  153.4 54.6 %while.10 = (s32[]{:T(128)}, bf16[2,512,128]{2,1,0:T(8,128)(2,1)}, pred[2,512,8192]{2,1,0:T(32,128)(4,1)}, bf16[2,512,128]{2,1,0:T(8,128)(2,1)S(1)}, bf16[8192,256]{1,0:T(8,128)(2,1)}, /*index=5*/s32[]{:T(128)}) while((s32[]{:T(128)}, bf16[2,512,128]{2,1,0:T(8,128)(2,1)}, pred[2,512,8192]{2,1,0:T(32,128)(4,1)}, ...), condition=%wide.region_4.5_spmd, body=%wide.region_1.4_spmd.sunk | while | flops 2176973824 | bytes 58994244 | solution.py:110
  153.4 9.8 %fusion.52 = (f32[512]{0:T(512)S(1)}, f32[512,8192]{1,0:T(8,128)}) fusion(bf16[8192,256]{1,0:T(8,128)(2,1)} %get-tuple-element.100, bf16[2,512,128]{2,1,0:T(8,128)(2,1)S(1)} %get-tuple-element.99, s32[]{:T(128)} %get-tuple-element.90, pred[2,512,8192]{2,1,0:T(32,128)(4,1)} %get-tuple-element.98), kind=kOutput, calls=%fused_computation.35.clone.1 | convolution fusion | flops 1086324224 | bytes 23202816 | tf_op jit(solution)/shard_map/while/body/eval_jaxpr/qd,kd->qk/dot_general | solution.py:29
  163.2 8.1 %fusion.53 = f32[512]{0:T(512)S(1)} fusion(f32[512,8192]{1,0:T(8,128)} %get-tuple-element.82, f32[512]{0:T(512)S(1)} %get-tuple-element.83), kind=kLoop, calls=%fused_computation.2.clone.1 | loop fusion | flops 8388096 | bytes 16781312 | tf_op jit(solution)/shard_map/while/body/eval_jaxpr/reduce_sum | solution.py:35
  171.3 9.4 %fusion.54 = bf16[2,512,128]{2,1,0:T(8,128)(2,1)} fusion(bf16[2,512,128]{2,1,0:T(8,128)(2,1)} %get-tuple-element.91, s32[]{:T(128)} %get-tuple-element.90, bf16[8192,256]{1,0:T(8,128)(2,1)} %get-tuple-element.100, f32[512,8192]{1,0:T(8,128)} %get-tuple-element.82, f32[512]{0:T(512)S(1)} %get-tuple-element.83, f32[512]{0:T(512)S(1)} %fusion.53), kind=kOutput, calls=%fused_computation.11.clone.1 | convolution fusion | flops 1082261504 | bytes 19010048 | tf_op jit(solution)/shard_map/while/body/eval_jaxpr/qk,kd->qd/dot_general | solution.py:37
  180.8 9.8 %fusion.52 = (f32[512]{0:T(512)S(1)}, f32[512,8192]{1,0:T(8,128)}) fusion(bf16[8192,256]{1,0:T(8,128)(2,1)} %get-tuple-element.100, bf16[2,512,128]{2,1,0:T(8,128)(2,1)S(1)} %get-tuple-element.99, s32[]{:T(128)} %get-tuple-element.90, pred[2,512,8192]{2,1,0:T(32,128)(4,1)} %get-tuple-element.98), kind=kOutput, calls=%fused_computation.35.clone.1 | convolution fusion | flops 1086324224 | bytes 23202816 | tf_op jit(solution)/shard_map/while/body/eval_jaxpr/qd,kd->qk/dot_general | solution.py:29
  190.5 8.1 %fusion.53 = f32[512]{0:T(512)S(1)} fusion(f32[512,8192]{1,0:T(8,128)} %get-tuple-element.82, f32[512]{0:T(512)S(1)} %get-tuple-element.83), kind=kLoop, calls=%fused_computation.2.clone.1 | loop fusion | flops 8388096 | bytes 16781312 | tf_op jit(solution)/shard_map/while/body/eval_jaxpr/reduce_sum | solution.py:35
  198.7 9.4 %fusion.54 = bf16[2,512,128]{2,1,0:T(8,128)(2,1)} fusion(bf16[2,512,128]{2,1,0:T(8,128)(2,1)} %get-tuple-element.91, s32[]{:T(128)} %get-tuple-element.90, bf16[8192,256]{1,0:T(8,128)(2,1)} %get-tuple-element.100, f32[512,8192]{1,0:T(8,128)} %get-tuple-element.82, f32[512]{0:T(512)S(1)} %get-tuple-element.83, f32[512]{0:T(512)S(1)} %fusion.53), kind=kOutput, calls=%fused_computation.11.clone.1 | convolution fusion | flops 1082261504 | bytes 19010048 | tf_op jit(solution)/shard_map/while/body/eval_jaxpr/qk,kd->qd/dot_general | solution.py:37
  208.1 18.3 %all_to_all.15 = bf16[16,64,128]{2,1,0:T(8,128)(2,1)S(1)} all-to-all(bf16[16,64,128]{2,1,0:T(8,128)(2,1)} %bitcast.15), channel_id=1, replica_groups=mesh['view'=8,'zh'=2,'zl'=4,'yhi'=2,'core'=2] {'zl','yhi','core'}, dimensions={0} | all-to-all | bytes 524288 | tf_op jit(solution)/shard_map/all_to_all | solution.py:111
  226.3 1.3 fusion.32
  (24 shorter events, 3.4 us)
Async XLA Ops:
  0.0 226.3 %copy-start = (bf16[1024,1536]{1,0:T(8,128)(2,1)S(1)}, bf16[1024,1536]{1,0:T(8,128)(2,1)}, u32[]{:S(2)}) copy-start(bf16[1024,1536]{1,0:T(8,128)(2,1)} %param.9) | copy-start | bytes 9437188
  0.9 9.7 %copy-start.4 = (bf16[2,64,1536]{2,1,0:T(8,128)(2,1)S(1)}, bf16[2,64,1536]{2,1,0:T(8,128)(2,1)}, u32[]{:S(2)}) copy-start(bf16[2,64,1536]{2,1,0:T(8,128)(2,1)} %param.7) | copy-start | bytes 1179652
  15.7 0.9 copy-start.2
  16.6 47.8 %copy-start.3 = (s32[2,16,6]{1,0,2:T(2,128)S(1)}, s32[2,16,6]{1,0,2:T(2,128)}, u32[]{:S(2)}) copy-start(s32[2,16,6]{1,0,2:T(2,128)} %param.11) | copy-start | bytes 2308
  18.4 8.3 %collective-permute-start = (bf16[8,64,256]{2,1,0:T(8,128)(2,1)S(1)}, bf16[8,64,256]{2,1,0:T(8,128)(2,1)}, u32[]{:S(2)}, u32[]{:S(2)}) collective-permute-start(bf16[8,64,256]{2,1,0:T(8,128)(2,1)S(1)} %select_bitcast_fusion), channel_id=1, source_target_pairs={{0,32},{32,64},{64,96},{96,128},{128,160},{160,192},{192,224},{224... | collective-permute-start | bytes 786440 | tf_op jit(solution)/shard_map/ppermute | solution.py:47
  27.6 7.3 %collective-permute-start.1 = (bf16[8,64,256]{2,1,0:T(8,128)(2,1)S(1)}, bf16[8,64,256]{2,1,0:T(8,128)(2,1)}, u32[]{:S(2)}, u32[]{:S(2)}) collective-permute-start(bf16[8,64,256]{2,1,0:T(8,128)(2,1)S(1)} %broadcast_select_fusion.2), channel_id=1, source_target_pairs={{0,64},{32,96},{64,128},{96,160},{128,192},{160,224},{192,0},{224,... | collective-permute-start | bytes 786440 | tf_op jit(solution)/shard_map/ppermute | solution.py:47
  35.6 7.8 %collective-permute-start.2 = (bf16[8,64,256]{2,1,0:T(8,128)(2,1)}, bf16[8,64,256]{2,1,0:T(8,128)(2,1)S(1)}, u32[]{:S(2)}, u32[]{:S(2)}) collective-permute-start(bf16[8,64,256]{2,1,0:T(8,128)(2,1)} %broadcast_select_fusion.3), channel_id=1, source_target_pairs={{0,128},{32,160},{64,192},{96,224},{128,0},{160,32},{192,64},{224,... | collective-permute-start | bytes 786440 | tf_op jit(solution)/shard_map/ppermute | solution.py:47
  46.2 66.6 %all-to-all-start.1 = ((bf16[32,64,512]{2,1,0:T(8,128)(2,1)}), bf16[32,64,512]{2,1,0:T(8,128)(2,1)}, u32[]{:S(2)}, u32[]{:S(2)}) async-start(bf16[32,64,512]{2,1,0:T(8,128)(2,1)} %bitcast.59), calls=%async_computation.1 | async-start | bytes 4194304 | tf_op jit(solution)/shard_map/all_to_all | solution.py:82
  112.8 40.6 %all-to-all-start = ((bf16[16,64,128]{2,1,0:T(8,128)(2,1)}), bf16[16,64,128]{2,1,0:T(8,128)(2,1)S(1)}, u32[]{:S(2)}, u32[]{:S(2)}) async-start(bf16[16,64,128]{2,1,0:T(8,128)(2,1)} %bitcast.63), calls=%async_computation | async-start | bytes 524288 | tf_op jit(solution)/shard_map/all_to_all | solution.py:75
  119.0 3.8 %copy-start.1 = (pred[2,512,4096]{2,1,0:T(32,128)(4,1)S(1)}, pred[2,512,4096]{2,1,0:T(32,128)(4,1)}, u32[]{:S(2)}) copy-start(pred[2,512,4096]{2,1,0:T(32,128)(4,1)} %concatenate.12) | copy-start | bytes 12582916
  122.2 5.3 %collective-permute-start.3 = (bf16[2048,256]{1,0:T(8,128)(2,1)}, bf16[2048,256]{1,0:T(8,128)(2,1)}, u32[]{:S(2)}, u32[]{:S(2)}) collective-permute-start(bf16[2048,256]{1,0:T(8,128)(2,1)} %get-tuple-element.47), channel_id=1, source_target_pairs={{0,1},{1,0},{2,3},{3,2},{4,5},{5,4},{6,7},{7,6},{8,9},{9,8},{10,11... | collective-permute-start | bytes 3145736 | tf_op jit(solution)/shard_map/ppermute | solution.py:86
  122.3 26.0 %collective-permute-start.4 = (bf16[2048,256]{1,0:T(8,128)(2,1)}, bf16[2048,256]{1,0:T(8,128)(2,1)}, u32[]{:S(2)}, u32[]{:S(2)}) collective-permute-start(bf16[2048,256]{1,0:T(8,128)(2,1)} %get-tuple-element.47), channel_id=1, source_target_pairs={{0,225},{1,32},{32,1},{33,64},{64,33},{65,96},{96,65},{97,128},{12... | collective-permute-start | bytes 3145736 | tf_op jit(solution)/shard_map/ppermute | solution.py:92

commit v2 on v1

v2 whole, which is shorter than its diff:
```python
import math

import jax
import jax.numpy as jnp
from jax import lax
from jax.experimental import pallas as pl
from jax.experimental.pallas import tpu as pltpu
from jax.sharding import Mesh
from jax.sharding import PartitionSpec as P

HEADS = 8
HD = 128
VT = 2048
BLK = 128
NBLK = 16

SUB = ("zh", "zl", "yhi", "core")
HALF = ("zl", "yhi", "core")


def attention_kernel(epi_ref, q_ref, own_ref, anc_ref, *rest):
    block = pl.program_id(0)
    nb_refs, o_ref = rest[:-1], rest[-1]
    queries = q_ref[...]
    scale = math.sqrt(HD)

    def scores_of(keyvals):
        return lax.dot_general(
            queries, keyvals[:, :HD], (((1,), (1,)), ((), ())),
            preferred_element_type=jnp.float32,
        ) / scale

    parts = []
    for ref in (own_ref, anc_ref):
        keyvals = ref[...]
        parts.append((scores_of(keyvals), keyvals))
    for slot, nb_ref in enumerate(nb_refs):
        index = epi_ref[block, slot]
        keyvals = nb_ref[...]
        scores = jnp.where(index >= 0, scores_of(keyvals), -jnp.inf)
        parts.append((scores, keyvals))
    peak = parts[0][0].max(axis=1, keepdims=True)
    for scores, _ in parts[1:]:
        peak = jnp.maximum(peak, scores.max(axis=1, keepdims=True))
    total = None
    summed = None
    for scores, keyvals in parts:
        raised = jnp.exp(scores - peak)
        row = raised.sum(axis=1, keepdims=True)
        prod = jnp.dot(raised.astype(jnp.bfloat16), keyvals[:, HD:], preferred_element_type=jnp.float32)
        total = row if total is None else total + row
        summed = prod if summed is None else summed + prod
    o_ref[...] = (summed / total).astype(o_ref.dtype)


def attention(epi_rows, queries, own, anchored, nearby):
    rows = queries.shape[0]
    spec_full = lambda n: pl.BlockSpec((n, 2 * HD), lambda b, epi: (0, 0))

    def spec_slot(slot):
        return pl.BlockSpec(
            (BLK, 2 * HD), lambda b, epi: (jnp.clip(epi[b, slot], 0, 2 * NBLK - 1), 0)
        )

    slots = epi_rows.shape[1]
    return pl.pallas_call(
        attention_kernel,
        out_shape=jax.ShapeDtypeStruct((rows, HD), jnp.bfloat16),
        grid_spec=pltpu.PrefetchScalarGridSpec(
            num_scalar_prefetch=1,
            grid=(rows // BLK,),
            in_specs=[
                pl.BlockSpec((BLK, HD), lambda b, epi: (b, 0)),
                spec_full(own.shape[0]),
                spec_full(anchored.shape[0]),
            ] + [spec_slot(e) for e in range(slots)],
            out_specs=pl.BlockSpec((BLK, HD), lambda b, epi: (b, 0)),
        ),
    )(epi_rows, queries, own, anchored, *([nearby] * slots))


def broadcast_view(value, root, count):
    me = lax.axis_index("view")
    dist = (me - root) % count
    held = jnp.where(dist == 0, value, jnp.zeros_like(value))
    step = 1
    while step < count:
        got = lax.ppermute(held, "view", [(i, (i + step) % count) for i in range(count)])
        held = jnp.where((dist >= step) & (dist < 2 * step), got, held)
        step *= 2
    return held


def body(latents, qkv_weight, out_weight, anchor, epi_list):
    per_dev, tile_tokens, model_width = latents.shape
    views_n = lax.axis_size("view")
    half_n = lax.axis_size(HALF)
    tile_n = lax.axis_size(SUB)
    part_rows = tile_tokens * half_n
    core_n = lax.axis_size("core")
    slot = lax.axis_index("core")
    half = lax.axis_index("zh")

    flat = jnp.dot(
        latents.reshape(per_dev * tile_tokens, model_width), qkv_weight,
        preferred_element_type=jnp.float32,
    ).astype(jnp.bfloat16)
    projected = flat.reshape(per_dev, tile_tokens, HEADS, 3 * HD).transpose(2, 0, 1, 3)
    queries = projected[..., :HD]
    key_values = projected[..., HD:]

    target = anchor[0]
    anchor_tile = lax.dynamic_index_in_dim(key_values, target % per_dev, 1, keepdims=False)
    anchor_tile = broadcast_view(anchor_tile, target // per_dev, views_n)

    q_send = queries.reshape(HEADS * per_dev, tile_tokens, HD)
    q_mine = lax.all_to_all(q_send, HALF, 0, 0, tiled=True).reshape(part_rows, HD)

    def to_units(source):
        wide = jnp.broadcast_to(source[None], (tile_n // (HEADS * per_dev),) + source.shape)
        wide = wide.reshape(tile_n, tile_tokens, 2 * HD)
        return lax.all_to_all(wide, SUB, 0, 0, tiled=True).reshape(tile_n * tile_tokens, 2 * HD)

    own_kv = to_units(key_values.reshape(HEADS * per_dev, tile_tokens, 2 * HD))
    anchored = to_units(
        jnp.broadcast_to(anchor_tile[:, None], key_values.shape).reshape(
            HEADS * per_dev, tile_tokens, 2 * HD
        )
    )

    other = lax.ppermute(own_kv, "core", [(0, 1), (1, 0)])
    pairs = []
    for v in range(views_n):
        for c in range(core_n):
            dest_view = (v + 1) % views_n if c == 1 else (v - 1) % views_n
            pairs.append((v * core_n + c, dest_view * core_n + (1 - c)))
    far = lax.ppermute(own_kv, ("view", "core"), pairs)
    nearby = jnp.where(
        slot == 1,
        jnp.concatenate([other, far], axis=0),
        jnp.concatenate([far, other], axis=0),
    )

    epi_rows = lax.dynamic_index_in_dim(epi_list, slot, 0, keepdims=False)
    epi_rows = lax.dynamic_slice_in_dim(epi_rows, half * (part_rows // BLK), part_rows // BLK, 0)
    attended = attention(epi_rows, q_mine, own_kv, anchored, nearby)
    attended = attended.reshape(half_n, tile_tokens, HD)
    returned = lax.all_to_all(attended, HALF, 0, 0, tiled=True)
    returned = returned.reshape(HEADS, per_dev, tile_tokens, HD)
    projected_out = jnp.einsum(
        "hvtc,hcd->vtd",
        returned,
        out_weight.reshape(HEADS, HD, model_width),
        preferred_element_type=jnp.float32,
    )
    return projected_out.astype(jnp.bfloat16)


def solution(mesh):
    views_n, tile_n = mesh.devices.shape
    fine = Mesh(
        mesh.devices.reshape(views_n, 2, tile_n // 8, 2, 2),
        ("view",) + SUB,
    )
    return jax.shard_map(
        body,
        mesh=fine,
        in_specs=(P("view", SUB, None), P(), P(), P(), P("view", None, None)),
        out_specs=P("view", SUB, None),
        check_vma=False,
    )
```

time: 230 us -> 165 us (0.72)
  matrix products: 44.8 us -> 6.67 us
  local copies, waits for them, and re-layouts: 39.7 us -> 8.93 us
  other arithmetic: 29.9 us -> 11 us
  Pallas kernels: 0 us -> 16.3 us
  starting transfers between devices: 31 us -> 35 us
  waiting for transfers between devices: 63.1 us -> 66.8 us
    dot_general x5 -> x1, matrix products: 43.5 us -> 5.34 us  [body(): jnp.dot(latents.reshape(per_dev * tile_tokens, model_width), qkv_weight,...]
    all_to_all x1 -> x2, waiting for transfers between devices: 27.1 us -> 0.01 us  [to_units(): lax.all_to_all(wide, SUB, 0, 0, tiled=True)]
    pallas_call x0 -> x1, Pallas kernels: none -> 16.3 us  [attention(): pl.pallas_call(attention_kernel, out_shape=jax.ShapeDtypeStruct((rows, HD...]
    reduce_sum x2 -> x0, other arithmetic: 16.2 us -> none  [attend(): row_total = jnp.sum(raised, axis=1, keepdims=True)]
    concatenate x1 -> x0, local copies, waits for them, and re-layouts: 12 us -> none  [allowed_tokens(): return jnp.concatenate([always, nearby, always], axis=1)]
    ppermute x1, waiting for transfers between devices: 20.9 us -> 32.5 us  [body(): far = lax.ppermute(own_kv, ('view', 'core'), pairs)]
    ppermute x3, waiting for transfers between devices: 15.1 us -> 25.2 us  [broadcast_view(): lax.ppermute(held, 'view', [(i, (i + step) % count) for i in range(count)])]
    concatenate x3 -> x0, other arithmetic: 9.19 us -> none  [the longest x1 4.63 us: allowed_tokens(): return jnp.concatenate([always, nearby, always], axis=1)]
  transfers between devices with their start and end apart: 7 -> 8, of which waited for: 5 -> 5; matrix products, arithmetic and copies ran while one was open for 16% -> 8% of each run, Pallas kernels for 0% -> 0%
where the time goes in v2:
time: 165 us; the launch traced here: 164 us
  waiting for transfers between devices  66.8 us (40%)
  starting transfers between devices  35 us (21%)
  blocking collectives  18.9 us (11%)
  Pallas kernels  16.3 us (10%)
  other arithmetic  11 us (7%)
  local copies, waits for them, and re-layouts  8.93 us (5%)
  matrix products  6.67 us (4%)
    ppermute x1, waiting for transfers between devices, body(): far = lax.ppermute(own_kv, ('view', 'core'), pairs)  32.5 us
    ppermute x3, waiting for transfers between devices, broadcast_view(): lax.ppermute(held, 'view', [(i, (i + step) % count) for i in range(count)])  25.2 us
    all_to_all x1, blocking collectives, body(): returned = lax.all_to_all(attended, HALF, 0, 0, tiled=True)  18.9 us
    all_to_all x2, starting transfers between devices, to_units(): lax.all_to_all(wide, SUB, 0, 0, tiled=True)  18.2 us
    pallas_call x1, Pallas kernels, attention(): pl.pallas_call(attention_kernel, out_shape=jax.ShapeDtypeStruct((rows, HD...  16.3 us
    all_to_all x1, starting transfers between devices, body(): lax.all_to_all(q_send, HALF, 0, 0, tiled=True).reshape(part_rows, HD)  10 us
    all_to_all x1, waiting for transfers between devices, body(): lax.all_to_all(q_send, HALF, 0, 0, tiled=True).reshape(part_rows, HD)  9.1 us
    dot_general x1, matrix products, body(): jnp.dot(latents.reshape(per_dev * tile_tokens, model_width), qkv_weight,...  5.34 us
  transfers between devices with their start and end apart: 8, of which 5 were waited for; matrix products, arithmetic and copies ran while one was open for 8% of the time, Pallas kernels for 0%

profile of v2, /device:TPU:1, one launch (start us, length us, event | category | flops | bytes accessed | tf_op | source)
XLA Modules:
  0.0 164.4 jit_solution(16363414275530705969)
XLA Ops:
  0.0 5.3 %convolution_convert_fusion = bf16[128,3072]{1,0:T(8,128)(2,1)S(1)} fusion(bf16[128,1536]{1,0:T(8,128)(2,1)} %bitcast.50, bf16[1536,3072]{1,0:T(8,128)(2,1)} %param.6), kind=kOutput, calls=%fused_computation | convolution fusion | flops 1208352768 | bytes 10616832 | tf_op jit(solution)/shard_map/dot_general | solution.py:104
  5.4 0.1 copy.15
  5.5 0.1 copy.17
  5.6 0.9 copy-done.1
  6.5 0.8 slice.8
  7.3 10.0 %all-to-all-start = ((bf16[16,64,128]{2,1,0:T(8,128)(2,1)}), bf16[16,64,128]{2,1,0:T(8,128)(2,1)S(1)}, u32[]{:S(2)}, u32[]{:S(2)}) async-start(bf16[16,64,128]{2,1,0:T(8,128)(2,1)} %bitcast.53), calls=%async_computation | async-start | bytes 524288 | tf_op jit(solution)/shard_map/all_to_all | solution.py:117
  17.3 1.9 %slice.9 = bf16[8,2,64,256]{3,2,1,0:T(8,128)(2,1)} slice(bf16[8,2,64,384]{3,2,1,0:T(8,128)(2,1)} %bitcast.46), slice={[0:8], [0:2], [0:64], [128:384]} | slice | bytes 1048576 | tf_op jit(solution)/shard_map/slice | solution.py:110
  19.2 9.1 %all-to-all-done = bf16[16,64,128]{2,1,0:T(8,128)(2,1)S(1)} async-done(((bf16[16,64,128]{2,1,0:T(8,128)(2,1)}), bf16[16,64,128]{2,1,0:T(8,128)(2,1)S(1)}, u32[]{:S(2)}, u32[]{:S(2)}) %all-to-all-start) | async-done | bytes 262176 | tf_op jit(solution)/shard_map/all_to_all | solution.py:117
  28.3 2.2 %broadcast_in_dim.24 = bf16[2,16,64,256]{3,2,1,0:T(8,128)(2,1)} broadcast(bf16[16,64,256]{2,1,0:T(8,128)(2,1)} %bitcast.41), dimensions={1,2,3} | broadcast | bytes 1572864 | tf_op jit(solution)/shard_map/broadcast_in_dim | solution.py:120
  30.6 6.6 %all-to-all-start.1 = ((bf16[32,64,256]{2,1,0:T(8,128)(2,1)}), bf16[32,64,256]{2,1,0:T(8,128)(2,1)}, u32[]{:S(2)}, u32[]{:S(2)}) async-start(bf16[32,64,256]{2,1,0:T(8,128)(2,1)} %bitcast.42), calls=%async_computation.1 | async-start | bytes 2097152 | tf_op jit(solution)/shard_map/all_to_all | solution.py:122
  37.9 1.7 %select_bitcast_fusion = bf16[8,64,256]{2,1,0:T(8,128)(2,1)} fusion(bf16[8,2,64,256]{3,2,1,0:T(8,128)(2,1)} %slice.9, s32[]{:T(128)S(6)} %select_n.78, pred[]{:T(512)S(6)} %eq.9), kind=kLoop, calls=%fused_computation.5 | loop fusion | flops 131072 | bytes 524293 | tf_op jit(solution)/shard_map/jit(_where)/select_n | solution.py:85
  39.6 0.4 collective-permute-start
  40.0 12.7 %collective-permute-done = bf16[8,64,256]{2,1,0:T(8,128)(2,1)} collective-permute-done((bf16[8,64,256]{2,1,0:T(8,128)(2,1)}, bf16[8,64,256]{2,1,0:T(8,128)(2,1)}, u32[]{:S(2)}, u32[]{:S(2)}) %collective-permute-start) | collective-permute-done | bytes 262176 | tf_op jit(solution)/shard_map/ppermute | solution.py:88
  52.7 1.7 %broadcast_select_fusion = bf16[8,64,256]{2,1,0:T(8,128)(2,1)} fusion(bf16[8,64,256]{2,1,0:T(8,128)(2,1)} %collective-permute-done, pred[]{:T(512)S(6)} %and.30, bf16[8,2,64,256]{3,2,1,0:T(8,128)(2,1)} %slice.9, s32[]{:T(128)S(6)} %select_n.78, pred[]{:T(512)S(6)} %eq.9), kind=kLoop, calls=%fused_computation.6 | loop fusion | flops 262144 | bytes 786438 | tf_op jit(solution)/shard_map/jit(_where)/select_n | solution.py:89
  54.4 1.0 collective-permute-start.1
  55.4 6.7 %collective-permute-done.1 = bf16[8,64,256]{2,1,0:T(8,128)(2,1)} collective-permute-done((bf16[8,64,256]{2,1,0:T(8,128)(2,1)}, bf16[8,64,256]{2,1,0:T(8,128)(2,1)}, u32[]{:S(2)}, u32[]{:S(2)}) %collective-permute-start.1) | collective-permute-done | bytes 262176 | tf_op jit(solution)/shard_map/ppermute | solution.py:88
  62.1 1.7 %broadcast_select_fusion.1 = bf16[8,64,256]{2,1,0:T(8,128)(2,1)} fusion(bf16[8,64,256]{2,1,0:T(8,128)(2,1)} %collective-permute-done.1, bf16[8,64,256]{2,1,0:T(8,128)(2,1)} %broadcast_select_fusion, pred[]{:T(512)S(6)} %and.29), kind=kLoop, calls=%fused_computation.7 | loop fusion | flops 131072 | bytes 786433 | tf_op jit(solution)/shard_map/jit(_where)/select_n | solution.py:89
  63.8 1.3 collective-permute-start.2
  65.1 5.8 %collective-permute-done.2 = bf16[8,64,256]{2,1,0:T(8,128)(2,1)} collective-permute-done((bf16[8,64,256]{2,1,0:T(8,128)(2,1)}, bf16[8,64,256]{2,1,0:T(8,128)(2,1)}, u32[]{:S(2)}, u32[]{:S(2)}) %collective-permute-start.2) | collective-permute-done | bytes 262176 | tf_op jit(solution)/shard_map/ppermute | solution.py:88
  70.9 1.7 %broadcast_select_fusion.2 = bf16[8,64,256]{2,1,0:T(8,128)(2,1)} fusion(bf16[8,64,256]{2,1,0:T(8,128)(2,1)} %collective-permute-done.2, bf16[8,64,256]{2,1,0:T(8,128)(2,1)} %broadcast_select_fusion.1, pred[]{:T(512)S(6)} %and.28), kind=kLoop, calls=%fused_computation.8 | loop fusion | flops 131072 | bytes 786433 | tf_op jit(solution)/shard_map/jit(_where)/select_n | solution.py:89
  72.6 1.0 broadcast_in_dim.26
  73.6 1.1 broadcast_in_dim.28
  74.7 11.7 %all-to-all-start.2 = ((bf16[32,64,256]{2,1,0:T(8,128)(2,1)}), bf16[32,64,256]{2,1,0:T(8,128)(2,1)}, u32[]{:S(2)}, u32[]{:S(2)}) async-start(bf16[32,64,256]{2,1,0:T(8,128)(2,1)} %bitcast.43), calls=%async_computation.2 | async-start | bytes 2097152 | tf_op jit(solution)/shard_map/all_to_all | solution.py:122
  86.3 2.8 %collective-permute-start.4 = (bf16[2048,256]{1,0:T(8,128)(2,1)}, bf16[2048,256]{1,0:T(8,128)(2,1)}, u32[]{:S(2)}, u32[]{:S(2)}) collective-permute-start(bf16[2048,256]{1,0:T(8,128)(2,1)} %bitcast.7.own_ref), channel_id=1, source_target_pairs={{0,225},{1,32},{32,1},{33,64},{64,33},{65,96},{96,65},{97,128},{12... | collective-permute-start | bytes 3145736 | tf_op jit(solution)/shard_map/ppermute | solution.py:137
  89.2 1.3 collective-permute-start.3
  90.5 0.1 constant_dynamic-slice_fusion
  90.5 0.7 copy.14
  91.2 32.5 %collective-permute-done.4 = bf16[2048,256]{1,0:T(8,128)(2,1)} collective-permute-done((bf16[2048,256]{1,0:T(8,128)(2,1)}, bf16[2048,256]{1,0:T(8,128)(2,1)}, u32[]{:S(2)}, u32[]{:S(2)}) %collective-permute-start.4) | collective-permute-done | bytes 1048608 | tf_op jit(solution)/shard_map/ppermute | solution.py:137
  123.7 4.2 %maximum_select_fusion.rest_0_.rest_1_.rest_2_.rest_3_.rest_4_.rest_5_ = bf16[4096,256]{1,0:T(8,128)(2,1)} fusion(bf16[2048,256]{1,0:T(8,128)(2,1)} %collective-permute-done.4, bf16[2048,256]{1,0:T(8,128)(2,1)} %collective-permute-done.3, pred[]{:T(512)S(6)} %eq.10), kind=kLoop, calls=%fused_computation.3 | loop fusion | flops 9437184 | bytes 4194305 | tf_op jit(solution)/shard_map/jit(_where)/select_n | solution.py:138
  127.9 16.3 %shard_map.55 = bf16[1024,128]{1,0:T(8,128)(2,1)} custom-call(s32[8,6]{1,0:T(8,128)} %bitcast.54, bf16[1024,128]{1,0:T(8,128)(2,1)} %bitcast.51, bf16[2048,256]{1,0:T(8,128)(2,1)} %bitcast.7.own_ref, bf16[2048,256]{1,0:T(8,128)(2,1)} %bitcast.12.anc_ref, bf16[4096,256]{1,0:T(8,128)(2,1)} %maximum_select_fusion.rest_0_.rest_1_.rest_2_.rest_3_.rest_4_.rest_5_, ...), custom_call_target="tpu_custom_call" | custom-call | tf_op jit(solution)/shard_map/pallas_call | solution.py:66
  144.2 18.9 %all_to_all.20 = bf16[16,64,128]{2,1,0:T(8,128)(2,1)S(1)} all-to-all(bf16[16,64,128]{2,1,0:T(8,128)(2,1)} %bitcast.52), channel_id=1, replica_groups=mesh['view'=8,'zh'=2,'zl'=4,'yhi'=2,'core'=2] {'zl','yhi','core'}, dimensions={0} | all-to-all | bytes 524288 | tf_op jit(solution)/shard_map/all_to_all | solution.py:148
  163.1 1.3 fusion
  (10 shorter events, 0.0 us)
Async XLA Ops:
  0.0 163.1 %copy-start = (bf16[1024,1536]{1,0:T(8,128)(2,1)S(1)}, bf16[1024,1536]{1,0:T(8,128)(2,1)}, u32[]{:S(2)}) copy-start(bf16[1024,1536]{1,0:T(8,128)(2,1)} %param.7) | copy-start | bytes 9437188
  5.6 0.9 copy-start.1
  7.3 21.1 %all-to-all-start = ((bf16[16,64,128]{2,1,0:T(8,128)(2,1)}), bf16[16,64,128]{2,1,0:T(8,128)(2,1)S(1)}, u32[]{:S(2)}, u32[]{:S(2)}) async-start(bf16[16,64,128]{2,1,0:T(8,128)(2,1)} %bitcast.53), calls=%async_computation | async-start | bytes 524288 | tf_op jit(solution)/shard_map/all_to_all | solution.py:117
  28.3 44.2 %copy-start.2 = (bf16[16,64,128]{2,1,0:T(8,128)(2,1)}, bf16[16,64,128]{2,1,0:T(8,128)(2,1)S(1)}, u32[]{:S(2)}) copy-start(bf16[16,64,128]{2,1,0:T(8,128)(2,1)S(1)} %all-to-all-done) | copy-start | bytes 786436
  30.6 42.0 %all-to-all-start.1 = ((bf16[32,64,256]{2,1,0:T(8,128)(2,1)}), bf16[32,64,256]{2,1,0:T(8,128)(2,1)}, u32[]{:S(2)}, u32[]{:S(2)}) async-start(bf16[32,64,256]{2,1,0:T(8,128)(2,1)} %bitcast.42), calls=%async_computation.1 | async-start | bytes 2097152 | tf_op jit(solution)/shard_map/all_to_all | solution.py:122
  39.6 13.1 %collective-permute-start = (bf16[8,64,256]{2,1,0:T(8,128)(2,1)}, bf16[8,64,256]{2,1,0:T(8,128)(2,1)}, u32[]{:S(2)}, u32[]{:S(2)}) collective-permute-start(bf16[8,64,256]{2,1,0:T(8,128)(2,1)} %select_bitcast_fusion), channel_id=1, source_target_pairs={{0,32},{32,64},{64,96},{96,128},{128,160},{160,192},{192,224},{224... | collective-permute-start | bytes 786440 | tf_op jit(solution)/shard_map/ppermute | solution.py:88
  54.4 36.0 %copy-start.3 = (s32[2,16,6]{1,0,2:T(2,128)S(1)}, s32[2,16,6]{1,0,2:T(2,128)}, u32[]{:S(2)}) copy-start(s32[2,16,6]{1,0,2:T(2,128)} %param.9) | copy-start | bytes 2308
  54.4 7.7 %collective-permute-start.1 = (bf16[8,64,256]{2,1,0:T(8,128)(2,1)}, bf16[8,64,256]{2,1,0:T(8,128)(2,1)}, u32[]{:S(2)}, u32[]{:S(2)}) collective-permute-start(bf16[8,64,256]{2,1,0:T(8,128)(2,1)} %broadcast_select_fusion), channel_id=1, source_target_pairs={{0,64},{32,96},{64,128},{96,160},{128,192},{160,224},{192,0},{224,... | collective-permute-start | bytes 786440 | tf_op jit(solution)/shard_map/ppermute | solution.py:88
  63.8 7.0 %collective-permute-start.2 = (bf16[8,64,256]{2,1,0:T(8,128)(2,1)}, bf16[8,64,256]{2,1,0:T(8,128)(2,1)}, u32[]{:S(2)}, u32[]{:S(2)}) collective-permute-start(bf16[8,64,256]{2,1,0:T(8,128)(2,1)} %broadcast_select_fusion.1), channel_id=1, source_target_pairs={{0,128},{32,160},{64,192},{96,224},{128,0},{160,32},{192,64},{224,... | collective-permute-start | bytes 786440 | tf_op jit(solution)/shard_map/ppermute | solution.py:88
  74.7 53.2 %all-to-all-start.2 = ((bf16[32,64,256]{2,1,0:T(8,128)(2,1)}), bf16[32,64,256]{2,1,0:T(8,128)(2,1)}, u32[]{:S(2)}, u32[]{:S(2)}) async-start(bf16[32,64,256]{2,1,0:T(8,128)(2,1)} %bitcast.43), calls=%async_computation.2 | async-start | bytes 2097152 | tf_op jit(solution)/shard_map/all_to_all | solution.py:122
  86.3 37.4 %collective-permute-start.4 = (bf16[2048,256]{1,0:T(8,128)(2,1)}, bf16[2048,256]{1,0:T(8,128)(2,1)}, u32[]{:S(2)}, u32[]{:S(2)}) collective-permute-start(bf16[2048,256]{1,0:T(8,128)(2,1)} %bitcast.7.own_ref), channel_id=1, source_target_pairs={{0,225},{1,32},{32,1},{33,64},{64,33},{65,96},{96,65},{97,128},{12... | collective-permute-start | bytes 3145736 | tf_op jit(solution)/shard_map/ppermute | solution.py:137
  89.2 34.5 %collective-permute-start.3 = (bf16[2048,256]{1,0:T(8,128)(2,1)}, bf16[2048,256]{1,0:T(8,128)(2,1)}, u32[]{:S(2)}, u32[]{:S(2)}) collective-permute-start(bf16[2048,256]{1,0:T(8,128)(2,1)} %bitcast.7.own_ref), channel_id=1, source_target_pairs={{0,1},{1,0},{2,3},{3,2},{4,5},{5,4},{6,7},{7,6},{8,9},{9,8},{10,11... | collective-permute-start | bytes 3145736 | tf_op jit(solution)/shard_map/ppermute | solution.py:131

commit v3 on v2

--- a/solution.py
+++ b/solution.py
@@ -83,11 +83,15 @@
     me = lax.axis_index("view")
     dist = (me - root) % count
     held = jnp.where(dist == 0, value, jnp.zeros_like(value))
-    step = 1
-    while step < count:
-        got = lax.ppermute(held, "view", [(i, (i + step) % count) for i in range(count)])
-        held = jnp.where((dist >= step) & (dist < 2 * step), got, held)
-        step *= 2
+    reach = 0
+    while 2 * reach + 1 < count:
+        step = 2 * reach + 1
+        up = lax.ppermute(held, "view", [(i, (i + step) % count) for i in range(count)])
+        down = lax.ppermute(held, "view", [(i, (i - step) % count) for i in range(count)])
+        lo = (dist >= reach + 1) & (dist <= reach + step)
+        hi = (dist >= count - reach - step) & (dist <= count - reach - 1)
+        held = jnp.where(lo, up, jnp.where(hi, down, held))
+        reach += step
     return held
 
 
@@ -106,22 +110,21 @@
         preferred_element_type=jnp.float32,
     ).astype(jnp.bfloat16)
     projected = flat.reshape(per_dev, tile_tokens, HEADS, 3 * HD).transpose(2, 0, 1, 3)
-    queries = projected[..., :HD]
     key_values = projected[..., HD:]
 
     target = anchor[0]
     anchor_tile = lax.dynamic_index_in_dim(key_values, target % per_dev, 1, keepdims=False)
     anchor_tile = broadcast_view(anchor_tile, target // per_dev, views_n)
 
-    q_send = queries.reshape(HEADS * per_dev, tile_tokens, HD)
-    q_mine = lax.all_to_all(q_send, HALF, 0, 0, tiled=True).reshape(part_rows, HD)
+    def to_units(source):
+        width = source.shape[-1]
+        wide = jnp.broadcast_to(source[None], (tile_n // (HEADS * per_dev),) + source.shape)
+        wide = wide.reshape(tile_n, tile_tokens, width)
+        return lax.all_to_all(wide, SUB, 0, 0, tiled=True).reshape(tile_n * tile_tokens, width)
 
-    def to_units(source):
-        wide = jnp.broadcast_to(source[None], (tile_n // (HEADS * per_dev),) + source.shape)
-        wide = wide.reshape(tile_n, tile_tokens, 2 * HD)
-        return lax.all_to_all(wide, SUB, 0, 0, tiled=True).reshape(tile_n * tile_tokens, 2 * HD)
-
-    own_kv = to_units(key_values.reshape(HEADS * per_dev, tile_tokens, 2 * HD))
+    resident = to_units(projected.reshape(HEADS * per_dev, tile_tokens, 3 * HD))
+    q_mine = lax.dynamic_slice_in_dim(resident[:, :HD], half * part_rows, part_rows, 0)
+    own_kv = resident[:, HD:]
     anchored = to_units(
         jnp.broadcast_to(anchor_tile[:, None], key_values.shape).reshape(
             HEADS * per_dev, tile_tokens, 2 * HD

time: 165 us -> 157 us (0.952)
  waiting for transfers between devices: 66.8 us -> 62.5 us
  other arithmetic: 11 us -> 7.16 us
  starting transfers between devices: 35 us -> 32.9 us
    ppermute x0 -> x2, waiting for transfers between devices: none -> 27.7 us  [broadcast_view(): lax.ppermute(held, 'view', [(i, (i - step) % count) for i in range(count)])]
    ppermute x3 -> x2, waiting for transfers between devices: 25.2 us -> 5.6 us  [broadcast_view(): lax.ppermute(held, 'view', [(i, (i + step) % count) for i in range(count)])]
    all_to_all x1 -> x0, starting transfers between devices: 10 us -> none  [body(): lax.all_to_all(q_send, HALF, 0, 0, tiled=True).reshape(part_rows, HD)]
    all_to_all x1 -> x0, waiting for transfers between devices: 9.1 us -> none  [body(): lax.all_to_all(q_send, HALF, 0, 0, tiled=True).reshape(part_rows, HD)]
    ppermute x0 -> x2, starting transfers between devices: none -> 7.85 us  [broadcast_view(): lax.ppermute(held, 'view', [(i, (i - step) % count) for i in range(count)])]
    all_to_all x2, starting transfers between devices: 18.2 us -> 21.8 us  [to_units(): lax.all_to_all(wide, SUB, 0, 0, tiled=True)]
    ppermute x1, waiting for transfers between devices: 32.5 us -> 29.2 us  [body(): far = lax.ppermute(own_kv, ('view', 'core'), pairs)]
    select_n x3 -> x2, other arithmetic: 5.11 us -> 2.06 us  [broadcast_view(): held = jnp.where(lo, up, jnp.where(hi, down, held))]
  transfers between devices with their start and end apart: 8 -> 8, of which waited for: 5 -> 4; matrix products, arithmetic and copies ran while one was open for 8% -> 9% of each run, Pallas kernels for 0% -> 0%
where the time goes in v3:
time: 157 us; the launch traced here: 156 us
  waiting for transfers between devices  62.5 us (40%)
  starting transfers between devices  32.9 us (21%)
  blocking collectives  19.1 us (12%)
  Pallas kernels  16.3 us (10%)
  local copies, waits for them, and re-layouts  10.4 us (7%)
  other arithmetic  7.16 us (5%)
  matrix products  6.67 us (4%)
    ppermute x1, waiting for transfers between devices, body(): far = lax.ppermute(own_kv, ('view', 'core'), pairs)  29.2 us
    ppermute x2, waiting for transfers between devices, broadcast_view(): lax.ppermute(held, 'view', [(i, (i - step) % count) for i in range(count)])  27.7 us
    all_to_all x2, starting transfers between devices, to_units(): lax.all_to_all(wide, SUB, 0, 0, tiled=True)  21.8 us
    all_to_all x1, blocking collectives, body(): returned = lax.all_to_all(attended, HALF, 0, 0, tiled=True)  19.1 us
    pallas_call x1, Pallas kernels, attention(): pl.pallas_call(attention_kernel, out_shape=jax.ShapeDtypeStruct((rows, HD...  16.3 us
    ppermute x2, starting transfers between devices, broadcast_view(): lax.ppermute(held, 'view', [(i, (i - step) % count) for i in range(count)])  7.85 us
    ppermute x2, waiting for transfers between devices, broadcast_view(): lax.ppermute(held, 'view', [(i, (i + step) % count) for i in range(count)])  5.6 us
    dot_general x1, matrix products, body(): jnp.dot(latents.reshape(per_dev * tile_tokens, model_width), qkv_weight,...  5.34 us
  transfers between devices with their start and end apart: 8, of which 4 were waited for; matrix products, arithmetic and copies ran while one was open for 9% of the time, Pallas kernels for 0%

profile of v3, /device:TPU:1, one launch (start us, length us, event | category | flops | bytes accessed | tf_op | source)
XLA Modules:
  0.0 155.9 jit_solution(342443171270533275)
XLA Ops:
  0.0 5.3 %convolution_convert_fusion = bf16[128,3072]{1,0:T(8,128)(2,1)S(1)} fusion(bf16[128,1536]{1,0:T(8,128)(2,1)} %bitcast.48, bf16[1536,3072]{1,0:T(8,128)(2,1)} %param.6), kind=kOutput, calls=%fused_computation | convolution fusion | flops 1208352768 | bytes 10616832 | tf_op jit(solution)/shard_map/dot_general | solution.py:108
  5.4 0.1 copy.14
  5.5 0.1 copy.17
  5.6 0.9 copy-done.1
  6.5 1.4 broadcast_in_dim.24
  7.9 12.8 %all-to-all-start = ((bf16[32,64,384]{2,1,0:T(8,128)(2,1)}), bf16[32,64,384]{2,1,0:T(8,128)(2,1)}, u32[]{:S(2)}, u32[]{:S(2)}) async-start(bf16[32,64,384]{2,1,0:T(8,128)(2,1)} %bitcast.40), calls=%async_computation | async-start | bytes 3145728 | tf_op jit(solution)/shard_map/all_to_all | solution.py:123
  21.4 1.9 %slice.14 = bf16[8,2,64,256]{3,2,1,0:T(8,128)(2,1)} slice(bf16[8,2,64,384]{3,2,1,0:T(8,128)(2,1)} %bitcast.42), slice={[0:8], [0:2], [0:64], [128:384]} | slice | bytes 1048576 | tf_op jit(solution)/shard_map/slice | solution.py:113
  23.3 1.0 select_bitcast_fusion
  24.3 2.7 %collective-permute-start.1 = (bf16[8,64,256]{2,1,0:T(8,128)(2,1)S(1)}, bf16[8,64,256]{2,1,0:T(8,128)(2,1)}, u32[]{:S(2)}, u32[]{:S(2)}) collective-permute-start(bf16[8,64,256]{2,1,0:T(8,128)(2,1)S(1)} %select_bitcast_fusion), channel_id=1, source_target_pairs={{0,224},{32,0},{64,32},{96,64},{128,96},{160,128},{192,160},{224,1... | collective-permute-start | bytes 786440 | tf_op jit(solution)/shard_map/ppermute | solution.py:90
  26.9 0.0 collective-permute-start
  26.9 19.8 %collective-permute-done.1 = bf16[8,64,256]{2,1,0:T(8,128)(2,1)} collective-permute-done((bf16[8,64,256]{2,1,0:T(8,128)(2,1)S(1)}, bf16[8,64,256]{2,1,0:T(8,128)(2,1)}, u32[]{:S(2)}, u32[]{:S(2)}) %collective-permute-start.1) | collective-permute-done | bytes 262176 | tf_op jit(solution)/shard_map/ppermute | solution.py:90
  46.8 1.1 select_select_fusion.1
  47.8 0.0 copy-start.2
  47.9 5.2 %collective-permute-start.3 = (bf16[8,64,256]{2,1,0:T(8,128)(2,1)S(1)}, bf16[8,64,256]{2,1,0:T(8,128)(2,1)}, u32[]{:S(2)}, u32[]{:S(2)}) collective-permute-start(bf16[8,64,256]{2,1,0:T(8,128)(2,1)S(1)} %select_select_fusion.1), channel_id=1, source_target_pairs={{0,160},{32,192},{64,224},{96,0},{128,32},{160,64},{192,96},{224,1... | collective-permute-start | bytes 786440 | tf_op jit(solution)/shard_map/ppermute | solution.py:90
  53.0 7.9 %collective-permute-done.3 = bf16[8,64,256]{2,1,0:T(8,128)(2,1)} collective-permute-done((bf16[8,64,256]{2,1,0:T(8,128)(2,1)S(1)}, bf16[8,64,256]{2,1,0:T(8,128)(2,1)}, u32[]{:S(2)}, u32[]{:S(2)}) %collective-permute-start.3) | collective-permute-done | bytes 262176 | tf_op jit(solution)/shard_map/ppermute | solution.py:90
  60.9 5.6 %collective-permute-done.2 = bf16[8,64,256]{2,1,0:T(8,128)(2,1)} collective-permute-done((bf16[8,64,256]{2,1,0:T(8,128)(2,1)S(1)}, bf16[8,64,256]{2,1,0:T(8,128)(2,1)}, u32[]{:S(2)}, u32[]{:S(2)}) %collective-permute-start.2) | collective-permute-done | bytes 262176 | tf_op jit(solution)/shard_map/ppermute | solution.py:89
  66.5 1.0 select_select_fusion
  67.5 0.0 copy-start.3
  67.6 1.1 broadcast_in_dim.28
  68.7 9.0 %all-to-all-start.1 = ((bf16[32,64,256]{2,1,0:T(8,128)(2,1)}), bf16[32,64,256]{2,1,0:T(8,128)(2,1)}, u32[]{:S(2)}, u32[]{:S(2)}) async-start(bf16[32,64,256]{2,1,0:T(8,128)(2,1)} %bitcast.43), calls=%async_computation.1 | async-start | bytes 2097152 | tf_op jit(solution)/shard_map/all_to_all | solution.py:123
  77.7 2.3 %slice.13.own_ref = bf16[2048,256]{1,0:T(8,128)(2,1)} slice(bf16[2048,384]{1,0:T(8,128)(2,1)} %bitcast.5), slice={[0:2048], [128:384]} | slice | bytes 2097152 | tf_op jit(solution)/shard_map/slice | solution.py:127
  80.0 1.7 %collective-permute-start.5 = (bf16[2048,256]{1,0:T(8,128)(2,1)}, bf16[2048,256]{1,0:T(8,128)(2,1)}, u32[]{:S(2)}, u32[]{:S(2)}) collective-permute-start(bf16[2048,256]{1,0:T(8,128)(2,1)} %slice.13.own_ref), channel_id=1, source_target_pairs={{0,225},{1,32},{32,1},{33,64},{64,33},{65,96},{96,65},{97,128},{12... | collective-permute-start | bytes 3145736 | tf_op jit(solution)/shard_map/ppermute | solution.py:140
  81.7 1.5 collective-permute-start.4
  83.2 0.1 constant_dynamic-slice_fusion.1
  83.3 0.7 copy.13
  84.0 1.1 slice.12
  85.0 0.7 constant_dynamic-slice_fusion.q_ref
  85.8 29.2 %collective-permute-done.5 = bf16[2048,256]{1,0:T(8,128)(2,1)} collective-permute-done((bf16[2048,256]{1,0:T(8,128)(2,1)}, bf16[2048,256]{1,0:T(8,128)(2,1)}, u32[]{:S(2)}, u32[]{:S(2)}) %collective-permute-start.5) | collective-permute-done | bytes 1048608 | tf_op jit(solution)/shard_map/ppermute | solution.py:140
  115.0 4.1 %maximum_select_fusion.rest_0_.rest_1_.rest_2_.rest_3_.rest_4_.rest_5_ = bf16[4096,256]{1,0:T(8,128)(2,1)} fusion(bf16[2048,256]{1,0:T(8,128)(2,1)} %collective-permute-done.5, bf16[2048,256]{1,0:T(8,128)(2,1)} %collective-permute-done.4, pred[]{:T(512)S(6)} %eq.10), kind=kLoop, calls=%fused_computation.3 | loop fusion | flops 9437184 | bytes 4194305 | tf_op jit(solution)/shard_map/jit(_where)/select_n | solution.py:141
  119.1 16.3 %shard_map.55 = bf16[1024,128]{1,0:T(8,128)(2,1)} custom-call(s32[8,6]{1,0:T(8,128)} %bitcast.50, bf16[1024,128]{1,0:T(8,128)(2,1)} %constant_dynamic-slice_fusion.q_ref, bf16[2048,256]{1,0:T(8,128)(2,1)} %slice.13.own_ref, bf16[2048,256]{1,0:T(8,128)(2,1)} %bitcast.10.anc_ref, ...), custom_call_target="tpu_custom_call" | custom-call | tf_op jit(solution)/shard_map/pallas_call | solution.py:66
  135.4 19.1 %all_to_all.15 = bf16[16,64,128]{2,1,0:T(8,128)(2,1)S(1)} all-to-all(bf16[16,64,128]{2,1,0:T(8,128)(2,1)} %bitcast.49), channel_id=1, replica_groups=mesh['view'=8,'zh'=2,'zl'=4,'yhi'=2,'core'=2] {'zl','yhi','core'}, dimensions={0} | all-to-all | bytes 524288 | tf_op jit(solution)/shard_map/all_to_all | solution.py:151
  154.5 1.3 fusion
  (11 shorter events, 0.1 us)
Async XLA Ops:
  0.0 154.5 %copy-start = (bf16[1024,1536]{1,0:T(8,128)(2,1)S(1)}, bf16[1024,1536]{1,0:T(8,128)(2,1)}, u32[]{:S(2)}) copy-start(bf16[1024,1536]{1,0:T(8,128)(2,1)} %param.7) | copy-start | bytes 9437188
  5.6 0.9 copy-start.1
  7.9 59.6 %all-to-all-start = ((bf16[32,64,384]{2,1,0:T(8,128)(2,1)}), bf16[32,64,384]{2,1,0:T(8,128)(2,1)}, u32[]{:S(2)}, u32[]{:S(2)}) async-start(bf16[32,64,384]{2,1,0:T(8,128)(2,1)} %bitcast.40), calls=%async_computation | async-start | bytes 3145728 | tf_op jit(solution)/shard_map/all_to_all | solution.py:123
  24.3 22.5 %collective-permute-start.1 = (bf16[8,64,256]{2,1,0:T(8,128)(2,1)S(1)}, bf16[8,64,256]{2,1,0:T(8,128)(2,1)}, u32[]{:S(2)}, u32[]{:S(2)}) collective-permute-start(bf16[8,64,256]{2,1,0:T(8,128)(2,1)S(1)} %select_bitcast_fusion), channel_id=1, source_target_pairs={{0,224},{32,0},{64,32},{96,64},{128,96},{160,128},{192,160},{224,1... | collective-permute-start | bytes 786440 | tf_op jit(solution)/shard_map/ppermute | solution.py:90
  26.9 19.8 %collective-permute-start = (bf16[8,64,256]{2,1,0:T(8,128)(2,1)S(1)}, bf16[8,64,256]{2,1,0:T(8,128)(2,1)}, u32[]{:S(2)}, u32[]{:S(2)}) collective-permute-start(bf16[8,64,256]{2,1,0:T(8,128)(2,1)S(1)} %select_bitcast_fusion), channel_id=1, source_target_pairs={{0,32},{32,64},{64,96},{96,128},{128,160},{160,192},{192,224},{224... | collective-permute-start | bytes 786440 | tf_op jit(solution)/shard_map/ppermute | solution.py:89
  47.8 13.1 %copy-start.2 = (bf16[8,64,256]{2,1,0:T(8,128)(2,1)}, bf16[8,64,256]{2,1,0:T(8,128)(2,1)S(1)}, u32[]{:S(2)}) copy-start(bf16[8,64,256]{2,1,0:T(8,128)(2,1)S(1)} %select_select_fusion.1) | copy-start | bytes 786436
  47.9 13.1 %collective-permute-start.3 = (bf16[8,64,256]{2,1,0:T(8,128)(2,1)S(1)}, bf16[8,64,256]{2,1,0:T(8,128)(2,1)}, u32[]{:S(2)}, u32[]{:S(2)}) collective-permute-start(bf16[8,64,256]{2,1,0:T(8,128)(2,1)S(1)} %select_select_fusion.1), channel_id=1, source_target_pairs={{0,160},{32,192},{64,224},{96,0},{128,32},{160,64},{192,96},{224,1... | collective-permute-start | bytes 786440 | tf_op jit(solution)/shard_map/ppermute | solution.py:90
  53.0 13.5 %collective-permute-start.2 = (bf16[8,64,256]{2,1,0:T(8,128)(2,1)S(1)}, bf16[8,64,256]{2,1,0:T(8,128)(2,1)}, u32[]{:S(2)}, u32[]{:S(2)}) collective-permute-start(bf16[8,64,256]{2,1,0:T(8,128)(2,1)S(1)} %select_select_fusion.1), channel_id=1, source_target_pairs={{0,96},{32,128},{64,160},{96,192},{128,224},{160,0},{192,32},{224,... | collective-permute-start | bytes 786440 | tf_op jit(solution)/shard_map/ppermute | solution.py:89
  67.5 15.7 %copy-start.3 = (s32[2,16,6]{1,0,2:T(2,128)S(1)}, s32[2,16,6]{1,0,2:T(2,128)}, u32[]{:S(2)}) copy-start(s32[2,16,6]{1,0,2:T(2,128)} %param.9) | copy-start | bytes 2308
  68.7 50.4 %all-to-all-start.1 = ((bf16[32,64,256]{2,1,0:T(8,128)(2,1)}), bf16[32,64,256]{2,1,0:T(8,128)(2,1)}, u32[]{:S(2)}, u32[]{:S(2)}) async-start(bf16[32,64,256]{2,1,0:T(8,128)(2,1)} %bitcast.43), calls=%async_computation.1 | async-start | bytes 2097152 | tf_op jit(solution)/shard_map/all_to_all | solution.py:123
  80.0 35.0 %collective-permute-start.5 = (bf16[2048,256]{1,0:T(8,128)(2,1)}, bf16[2048,256]{1,0:T(8,128)(2,1)}, u32[]{:S(2)}, u32[]{:S(2)}) collective-permute-start(bf16[2048,256]{1,0:T(8,128)(2,1)} %slice.13.own_ref), channel_id=1, source_target_pairs={{0,225},{1,32},{32,1},{33,64},{64,33},{65,96},{96,65},{97,128},{12... | collective-permute-start | bytes 3145736 | tf_op jit(solution)/shard_map/ppermute | solution.py:140
  81.7 33.3 %collective-permute-start.4 = (bf16[2048,256]{1,0:T(8,128)(2,1)}, bf16[2048,256]{1,0:T(8,128)(2,1)}, u32[]{:S(2)}, u32[]{:S(2)}) collective-permute-start(bf16[2048,256]{1,0:T(8,128)(2,1)} %slice.13.own_ref), channel_id=1, source_target_pairs={{0,1},{1,0},{2,3},{3,2},{4,5},{5,4},{6,7},{7,6},{8,9},{9,8},{10,11... | collective-permute-start | bytes 3145736 | tf_op jit(solution)/shard_map/ppermute | solution.py:134

commit v4 on v3

--- a/solution.py
+++ b/solution.py
@@ -6,11 +6,11 @@
 from jax.experimental import pallas as pl
 from jax.experimental.pallas import tpu as pltpu
 from jax.sharding import Mesh
+
 from jax.sharding import PartitionSpec as P
 
 HEADS = 8
 HD = 128
-VT = 2048
 BLK = 128
 NBLK = 16
 
@@ -95,7 +95,7 @@
     return held
 
 
-def body(latents, qkv_weight, out_weight, anchor, epi_list):
+def layer(latents, qkv_weight, out_weight, anchor, epi_list):
     per_dev, tile_tokens, model_width = latents.shape
     views_n = lax.axis_size("view")
     half_n = lax.axis_size(HALF)
@@ -105,6 +105,10 @@
     slot = lax.axis_index("core")
     half = lax.axis_index("zh")
 
+    target = anchor[0]
+    anchor_latents = lax.dynamic_index_in_dim(latents, target % per_dev, 0, keepdims=False)
+    anchor_latents = broadcast_view(anchor_latents, target // per_dev, views_n)
+
     flat = jnp.dot(
         latents.reshape(per_dev * tile_tokens, model_width), qkv_weight,
         preferred_element_type=jnp.float32,
@@ -112,9 +116,10 @@
     projected = flat.reshape(per_dev, tile_tokens, HEADS, 3 * HD).transpose(2, 0, 1, 3)
     key_values = projected[..., HD:]
 
-    target = anchor[0]
-    anchor_tile = lax.dynamic_index_in_dim(key_values, target % per_dev, 1, keepdims=False)
-    anchor_tile = broadcast_view(anchor_tile, target // per_dev, views_n)
+    anchor_tile = jnp.dot(
+        anchor_latents, qkv_weight, preferred_element_type=jnp.float32
+    ).astype(jnp.bfloat16)
+    anchor_tile = anchor_tile.reshape(tile_tokens, HEADS, 3 * HD)[..., HD:].transpose(1, 0, 2)
 
     def to_units(source):
         width = source.shape[-1]
@@ -166,7 +171,7 @@
         ("view",) + SUB,
     )
     return jax.shard_map(
-        body,
+        layer,
         mesh=fine,
         in_specs=(P("view", SUB, None), P(), P(), P(), P("view", None, None)),
         out_specs=P("view", SUB, None),

time: 157 us -> 153 us (0.975)
  waiting for transfers between devices: 62.5 us -> 55.5 us
  matrix products: 6.67 us -> 12.2 us
  starting transfers between devices: 32.9 us -> 35.9 us
  local copies, waits for them, and re-layouts: 10.4 us -> 7.78 us
  other arithmetic: 7.16 us -> 5.56 us
    ppermute x2, waiting for transfers between devices: 27.7 us -> 21.9 us  [broadcast_view(): lax.ppermute(held, 'view', [(i, (i - step) % count) for i in range(count)])]
    dot_general x2 -> x3, matrix products: 6.67 us -> 12.2 us  [the longest x1 5.51 us: layer(): jnp.dot(anchor_latents, qkv_weight, preferred_element_type=jnp.float32)]
    slice x3 -> x2, local copies, waits for them, and re-layouts: 5.24 us -> 3.37 us  [the longest x1 2.29 us: layer(): own_kv = resident[:, HD:]]
    all_to_all x2, starting transfers between devices: 21.8 us -> 23.6 us  [to_units(): lax.all_to_all(wide, SUB, 0, 0, tiled=True)]
  transfers between devices with their start and end apart: 8 -> 8, of which waited for: 4 -> 4; matrix products, arithmetic and copies ran while one was open for 9% -> 11% of each run, Pallas kernels for 0% -> 0%
where the time goes in v4:
time: 153 us
  waiting for transfers between devices  55.5 us (36%)
  starting transfers between devices  35.9 us (23%)
  blocking collectives  18.7 us (12%)
  Pallas kernels  16.3 us (11%)
  matrix products  12.2 us (8%)
  local copies, waits for them, and re-layouts  7.78 us (5%)
  other arithmetic  5.56 us (4%)
    ppermute x1, waiting for transfers between devices, layer(): far = lax.ppermute(own_kv, ('view', 'core'), pairs)  28.2 us
    all_to_all x2, starting transfers between devices, to_units(): lax.all_to_all(wide, SUB, 0, 0, tiled=True)  23.6 us
    ppermute x2, waiting for transfers between devices, broadcast_view(): lax.ppermute(held, 'view', [(i, (i - step) % count) for i in range(count)])  21.9 us
    all_to_all x1, blocking collectives, layer(): returned = lax.all_to_all(attended, HALF, 0, 0, tiled=True)  18.7 us
    pallas_call x1, Pallas kernels, attention(): pl.pallas_call(attention_kernel, out_shape=jax.ShapeDtypeStruct((rows, HD...  16.3 us
    ppermute x2, starting transfers between devices, broadcast_view(): lax.ppermute(held, 'view', [(i, (i - step) % count) for i in range(count)])  8.14 us
    dot_general x1, matrix products, layer(): jnp.dot(anchor_latents, qkv_weight, preferred_element_type=jnp.float32)  5.51 us
    ppermute x2, waiting for transfers between devices, broadcast_view(): lax.ppermute(held, 'view', [(i, (i + step) % count) for i in range(count)])  5.38 us
  transfers between devices with their start and end apart: 8, of which 4 were waited for; matrix products, arithmetic and copies ran while one was open for 11% of the time, Pallas kernels for 0%

profile of v4, /device:TPU:1, one launch (start us, length us, event | category | flops | bytes accessed | tf_op | source)
XLA Modules:
  0.0 152.7 jit_solution(14727779476941099912)
XLA Ops:
  0.0 5.3 %convolution_convert_fusion = bf16[128,3072]{1,0:T(8,128)(2,1)S(1)} fusion(bf16[128,1536]{1,0:T(8,128)(2,1)} %bitcast.48, bf16[1536,3072]{1,0:T(8,128)(2,1)} %param.6), kind=kOutput, calls=%fused_computation | convolution fusion | flops 1208352768 | bytes 10616832 | tf_op jit(solution)/shard_map/dot_general | solution.py:112
  5.4 0.1 copy.15
  5.5 0.1 copy.9
  5.6 0.0 copy-start.1
  5.6 1.4 broadcast_in_dim.24
  7.0 12.8 %all-to-all-start = ((bf16[32,64,384]{2,1,0:T(8,128)(2,1)}), bf16[32,64,384]{2,1,0:T(8,128)(2,1)}, u32[]{:S(2)}, u32[]{:S(2)}) async-start(bf16[32,64,384]{2,1,0:T(8,128)(2,1)} %bitcast.43), calls=%async_computation | async-start | bytes 3145728 | tf_op jit(solution)/shard_map/all_to_all | solution.py:128
  20.5 0.7 select_bitcast_fusion
  21.2 2.6 %collective-permute-start.1 = (bf16[64,1536]{1,0:T(8,128)(2,1)}, bf16[64,1536]{1,0:T(8,128)(2,1)}, u32[]{:S(2)}, u32[]{:S(2)}) collective-permute-start(bf16[64,1536]{1,0:T(8,128)(2,1)} %select_bitcast_fusion), channel_id=1, source_target_pairs={{0,224},{32,0},{64,32},{96,64},{128,96},{160,128},{192,160},{224,1... | collective-permute-start | bytes 589832 | tf_op jit(solution)/shard_map/ppermute | solution.py:90
  23.8 15.2 %collective-permute-done.1 = bf16[64,1536]{1,0:T(8,128)(2,1)} collective-permute-done((bf16[64,1536]{1,0:T(8,128)(2,1)}, bf16[64,1536]{1,0:T(8,128)(2,1)}, u32[]{:S(2)}, u32[]{:S(2)}) %collective-permute-start.1) | collective-permute-done | bytes 196640 | tf_op jit(solution)/shard_map/ppermute | solution.py:90
  39.0 0.0 collective-permute-done
  39.0 0.7 select_select_fusion
  39.8 5.6 %collective-permute-start.3 = (bf16[64,1536]{1,0:T(8,128)(2,1)}, bf16[64,1536]{1,0:T(8,128)(2,1)S(1)}, u32[]{:S(2)}, u32[]{:S(2)}) collective-permute-start(bf16[64,1536]{1,0:T(8,128)(2,1)} %select_select_fusion), channel_id=1, source_target_pairs={{0,160},{32,192},{64,224},{96,0},{128,32},{160,64},{192,96},{224,1... | collective-permute-start | bytes 589832 | tf_op jit(solution)/shard_map/ppermute | solution.py:90
  45.3 0.0 collective-permute-start.2
  45.3 6.7 %collective-permute-done.3 = bf16[64,1536]{1,0:T(8,128)(2,1)S(1)} collective-permute-done((bf16[64,1536]{1,0:T(8,128)(2,1)}, bf16[64,1536]{1,0:T(8,128)(2,1)S(1)}, u32[]{:S(2)}, u32[]{:S(2)}) %collective-permute-start.3) | collective-permute-done | bytes 196640 | tf_op jit(solution)/shard_map/ppermute | solution.py:90
  52.0 5.4 %collective-permute-done.2 = bf16[64,1536]{1,0:T(8,128)(2,1)S(1)} collective-permute-done((bf16[64,1536]{1,0:T(8,128)(2,1)}, bf16[64,1536]{1,0:T(8,128)(2,1)S(1)}, u32[]{:S(2)}, u32[]{:S(2)}) %collective-permute-start.2) | collective-permute-done | bytes 196640 | tf_op jit(solution)/shard_map/ppermute | solution.py:89
  57.3 5.5 %convolution_convert_fusion.1 = bf16[64,3072]{1,0:T(8,128)(2,1)S(1)} fusion(bf16[1536,3072]{1,0:T(8,128)(2,1)} %param.6, bf16[64,1536]{1,0:T(8,128)(2,1)S(1)} %collective-permute-done.2, bf16[64,1536]{1,0:T(8,128)(2,1)S(1)} %collective-permute-done.3, bf16[64,1536]{1,0:T(8,128)(2,1)} %select_select_fusion, pred[]{:T(512)S(6)} %and.35, pred[]{:T(512)S(6)} %and.31), kind=kOutput, calls=%fused_computation.1 | convolution fusion | flops 604372992 | bytes 10420226 | tf_op jit(solution)/shard_map/dot_general | solution.py:119
  62.9 0.1 copy.16
  63.0 0.0 copy-start.2
  63.1 1.1 broadcast_in_dim.28
  64.2 10.8 %all-to-all-start.1 = ((bf16[32,64,256]{2,1,0:T(8,128)(2,1)}), bf16[32,64,256]{2,1,0:T(8,128)(2,1)}, u32[]{:S(2)}, u32[]{:S(2)}) async-start(bf16[32,64,256]{2,1,0:T(8,128)(2,1)} %bitcast.44), calls=%async_computation.1 | async-start | bytes 2097152 | tf_op jit(solution)/shard_map/all_to_all | solution.py:128
  75.0 2.3 %slice.13.own_ref = bf16[2048,256]{1,0:T(8,128)(2,1)} slice(bf16[2048,384]{1,0:T(8,128)(2,1)} %bitcast.5), slice={[0:2048], [128:384]} | slice | bytes 2097152 | tf_op jit(solution)/shard_map/slice | solution.py:132
  77.3 1.2 collective-permute-start.5
  78.5 2.9 %collective-permute-start.4 = (bf16[2048,256]{1,0:T(8,128)(2,1)}, bf16[2048,256]{1,0:T(8,128)(2,1)}, u32[]{:S(2)}, u32[]{:S(2)}) collective-permute-start(bf16[2048,256]{1,0:T(8,128)(2,1)} %slice.13.own_ref), channel_id=1, source_target_pairs={{0,1},{1,0},{2,3},{3,2},{4,5},{5,4},{6,7},{7,6},{8,9},{9,8},{10,11... | collective-permute-start | bytes 3145736 | tf_op jit(solution)/shard_map/ppermute | solution.py:139
  81.4 0.1 constant_dynamic-slice_fusion.1
  81.5 0.7 copy.14
  82.2 1.1 slice.12
  83.2 0.7 constant_dynamic-slice_fusion.q_ref
  84.0 28.2 %collective-permute-done.5 = bf16[2048,256]{1,0:T(8,128)(2,1)} collective-permute-done((bf16[2048,256]{1,0:T(8,128)(2,1)}, bf16[2048,256]{1,0:T(8,128)(2,1)}, u32[]{:S(2)}, u32[]{:S(2)}) %collective-permute-start.5) | collective-permute-done | bytes 1048608 | tf_op jit(solution)/shard_map/ppermute | solution.py:145
  112.2 4.1 %maximum_select_fusion.rest_0_.rest_1_.rest_2_.rest_3_.rest_4_.rest_5_ = bf16[4096,256]{1,0:T(8,128)(2,1)} fusion(bf16[2048,256]{1,0:T(8,128)(2,1)} %collective-permute-done.5, bf16[2048,256]{1,0:T(8,128)(2,1)} %collective-permute-done.4, pred[]{:T(512)S(6)} %eq.10), kind=kLoop, calls=%fused_computation.4 | loop fusion | flops 9437184 | bytes 4194305 | tf_op jit(solution)/shard_map/jit(_where)/select_n | solution.py:146
  116.4 16.3 %shard_map.55 = bf16[1024,128]{1,0:T(8,128)(2,1)} custom-call(s32[8,6]{1,0:T(8,128)} %bitcast.54, bf16[1024,128]{1,0:T(8,128)(2,1)} %constant_dynamic-slice_fusion.q_ref, bf16[2048,256]{1,0:T(8,128)(2,1)} %slice.13.own_ref, bf16[2048,256]{1,0:T(8,128)(2,1)} %bitcast.11.anc_ref, ...), custom_call_target="tpu_custom_call" | custom-call | tf_op jit(solution)/shard_map/pallas_call | solution.py:66
  132.7 18.7 %all_to_all.15 = bf16[16,64,128]{2,1,0:T(8,128)(2,1)S(1)} all-to-all(bf16[16,64,128]{2,1,0:T(8,128)(2,1)} %bitcast.53), channel_id=1, replica_groups=mesh['view'=8,'zh'=2,'zl'=4,'yhi'=2,'core'=2] {'zl','yhi','core'}, dimensions={0} | all-to-all | bytes 524288 | tf_op jit(solution)/shard_map/all_to_all | solution.py:156
  151.3 1.3 fusion
  (11 shorter events, 0.1 us)
Async XLA Ops:
  0.0 151.3 %copy-start = (bf16[1024,1536]{1,0:T(8,128)(2,1)S(1)}, bf16[1024,1536]{1,0:T(8,128)(2,1)}, u32[]{:S(2)}) copy-start(bf16[1024,1536]{1,0:T(8,128)(2,1)} %param.7) | copy-start | bytes 9437188
  5.6 14.9 %copy-start.1 = (bf16[2,64,1536]{2,1,0:T(8,128)(2,1)S(1)}, bf16[2,64,1536]{2,1,0:T(8,128)(2,1)}, u32[]{:S(2)}) copy-start(bf16[2,64,1536]{2,1,0:T(8,128)(2,1)} %param.5) | copy-start | bytes 1179652
  7.0 56.0 %all-to-all-start = ((bf16[32,64,384]{2,1,0:T(8,128)(2,1)}), bf16[32,64,384]{2,1,0:T(8,128)(2,1)}, u32[]{:S(2)}, u32[]{:S(2)}) async-start(bf16[32,64,384]{2,1,0:T(8,128)(2,1)} %bitcast.43), calls=%async_computation | async-start | bytes 3145728 | tf_op jit(solution)/shard_map/all_to_all | solution.py:128
  21.2 17.8 %collective-permute-start.1 = (bf16[64,1536]{1,0:T(8,128)(2,1)}, bf16[64,1536]{1,0:T(8,128)(2,1)}, u32[]{:S(2)}, u32[]{:S(2)}) collective-permute-start(bf16[64,1536]{1,0:T(8,128)(2,1)} %select_bitcast_fusion), channel_id=1, source_target_pairs={{0,224},{32,0},{64,32},{96,64},{128,96},{160,128},{192,160},{224,1... | collective-permute-start | bytes 589832 | tf_op jit(solution)/shard_map/ppermute | solution.py:90
  23.8 15.2 %collective-permute-start = (bf16[64,1536]{1,0:T(8,128)(2,1)}, bf16[64,1536]{1,0:T(8,128)(2,1)}, u32[]{:S(2)}, u32[]{:S(2)}) collective-permute-start(bf16[64,1536]{1,0:T(8,128)(2,1)} %select_bitcast_fusion), channel_id=1, source_target_pairs={{0,32},{32,64},{64,96},{96,128},{128,160},{160,192},{192,224},{224... | collective-permute-start | bytes 589832 | tf_op jit(solution)/shard_map/ppermute | solution.py:89
  39.8 12.2 %collective-permute-start.3 = (bf16[64,1536]{1,0:T(8,128)(2,1)}, bf16[64,1536]{1,0:T(8,128)(2,1)S(1)}, u32[]{:S(2)}, u32[]{:S(2)}) collective-permute-start(bf16[64,1536]{1,0:T(8,128)(2,1)} %select_select_fusion), channel_id=1, source_target_pairs={{0,160},{32,192},{64,224},{96,0},{128,32},{160,64},{192,96},{224,1... | collective-permute-start | bytes 589832 | tf_op jit(solution)/shard_map/ppermute | solution.py:90
  45.3 12.0 %collective-permute-start.2 = (bf16[64,1536]{1,0:T(8,128)(2,1)}, bf16[64,1536]{1,0:T(8,128)(2,1)S(1)}, u32[]{:S(2)}, u32[]{:S(2)}) collective-permute-start(bf16[64,1536]{1,0:T(8,128)(2,1)} %select_select_fusion), channel_id=1, source_target_pairs={{0,96},{32,128},{64,160},{96,192},{128,224},{160,0},{192,32},{224,... | collective-permute-start | bytes 589832 | tf_op jit(solution)/shard_map/ppermute | solution.py:89
  63.0 18.4 %copy-start.2 = (s32[2,16,6]{1,0,2:T(2,128)S(1)}, s32[2,16,6]{1,0,2:T(2,128)}, u32[]{:S(2)}) copy-start(s32[2,16,6]{1,0,2:T(2,128)} %param.9) | copy-start | bytes 2308
  64.2 52.2 %all-to-all-start.1 = ((bf16[32,64,256]{2,1,0:T(8,128)(2,1)}), bf16[32,64,256]{2,1,0:T(8,128)(2,1)}, u32[]{:S(2)}, u32[]{:S(2)}) async-start(bf16[32,64,256]{2,1,0:T(8,128)(2,1)} %bitcast.44), calls=%async_computation.1 | async-start | bytes 2097152 | tf_op jit(solution)/shard_map/all_to_all | solution.py:128
  77.3 34.9 %collective-permute-start.5 = (bf16[2048,256]{1,0:T(8,128)(2,1)}, bf16[2048,256]{1,0:T(8,128)(2,1)}, u32[]{:S(2)}, u32[]{:S(2)}) collective-permute-start(bf16[2048,256]{1,0:T(8,128)(2,1)} %slice.13.own_ref), channel_id=1, source_target_pairs={{0,225},{1,32},{32,1},{33,64},{64,33},{65,96},{96,65},{97,128},{12... | collective-permute-start | bytes 3145736 | tf_op jit(solution)/shard_map/ppermute | solution.py:145
  78.5 33.7 %collective-permute-start.4 = (bf16[2048,256]{1,0:T(8,128)(2,1)}, bf16[2048,256]{1,0:T(8,128)(2,1)}, u32[]{:S(2)}, u32[]{:S(2)}) collective-permute-start(bf16[2048,256]{1,0:T(8,128)(2,1)} %slice.13.own_ref), channel_id=1, source_target_pairs={{0,1},{1,0},{2,3},{3,2},{4,5},{5,4},{6,7},{7,6},{8,9},{9,8},{10,11... | collective-permute-start | bytes 3145736 | tf_op jit(solution)/shard_map/ppermute | solution.py:139

commit v5 on v4

--- a/solution.py
+++ b/solution.py
@@ -18,65 +18,70 @@
 HALF = ("zl", "yhi", "core")
 
 
-def attention_kernel(epi_ref, q_ref, own_ref, anc_ref, *rest):
+def attention_kernel(epi_ref, flag_ref, q_ref, own_ref, anc_ref, *rest):
     block = pl.program_id(0)
-    nb_refs, o_ref = rest[:-1], rest[-1]
+    slots = epi_ref.shape[1]
+    other_refs, far_refs, o_ref = rest[:slots], rest[slots:-1], rest[-1]
     queries = q_ref[...]
     scale = math.sqrt(HD)
 
-    def scores_of(keyvals):
+    def scores_of(keys):
         return lax.dot_general(
-            queries, keyvals[:, :HD], (((1,), (1,)), ((), ())),
+            queries, keys, (((1,), (1,)), ((), ())),
             preferred_element_type=jnp.float32,
         ) / scale
 
-    parts = []
-    for ref in (own_ref, anc_ref):
-        keyvals = ref[...]
-        parts.append((scores_of(keyvals), keyvals))
-    for slot, nb_ref in enumerate(nb_refs):
+    own = own_ref[...]
+    anc = anc_ref[...]
+    parts = [
+        (scores_of(own[:, HD : 2 * HD]), own[:, 2 * HD :]),
+        (scores_of(anc[:, :HD]), anc[:, HD:]),
+    ]
+    for slot in range(slots):
         index = epi_ref[block, slot]
-        keyvals = nb_ref[...]
-        scores = jnp.where(index >= 0, scores_of(keyvals), -jnp.inf)
-        parts.append((scores, keyvals))
+        use_other = (index < NBLK) == (flag_ref[0] == 1)
+        keyvals = jnp.where(use_other, other_refs[slot][...], far_refs[slot][...])
+        scores = jnp.where(index >= 0, scores_of(keyvals[:, :HD]), -jnp.inf)
+        parts.append((scores, keyvals[:, HD:]))
     peak = parts[0][0].max(axis=1, keepdims=True)
     for scores, _ in parts[1:]:
         peak = jnp.maximum(peak, scores.max(axis=1, keepdims=True))
     total = None
     summed = None
-    for scores, keyvals in parts:
+    for scores, values in parts:
         raised = jnp.exp(scores - peak)
         row = raised.sum(axis=1, keepdims=True)
-        prod = jnp.dot(raised.astype(jnp.bfloat16), keyvals[:, HD:], preferred_element_type=jnp.float32)
+        prod = jnp.dot(raised.astype(jnp.bfloat16), values, preferred_element_type=jnp.float32)
         total = row if total is None else total + row
         summed = prod if summed is None else summed + prod
     o_ref[...] = (summed / total).astype(o_ref.dtype)
 
 
-def attention(epi_rows, queries, own, anchored, nearby):
-    rows = queries.shape[0]
-    spec_full = lambda n: pl.BlockSpec((n, 2 * HD), lambda b, epi: (0, 0))
+def attention(epi_rows, flags, resident, anchored, other, far, rows):
+    slots = epi_rows.shape[1]
 
     def spec_slot(slot):
         return pl.BlockSpec(
-            (BLK, 2 * HD), lambda b, epi: (jnp.clip(epi[b, slot], 0, 2 * NBLK - 1), 0)
+            (BLK, 2 * HD),
+            lambda b, epi, flag: (jnp.clip(epi[b, slot], 0, 2 * NBLK - 1) % NBLK, 0),
         )
 
-    slots = epi_rows.shape[1]
     return pl.pallas_call(
         attention_kernel,
         out_shape=jax.ShapeDtypeStruct((rows, HD), jnp.bfloat16),
         grid_spec=pltpu.PrefetchScalarGridSpec(
-            num_scalar_prefetch=1,
+            num_scalar_prefetch=2,
             grid=(rows // BLK,),
             in_specs=[
-                pl.BlockSpec((BLK, HD), lambda b, epi: (b, 0)),
-                spec_full(own.shape[0]),
-                spec_full(anchored.shape[0]),
-            ] + [spec_slot(e) for e in range(slots)],
-            out_specs=pl.BlockSpec((BLK, HD), lambda b, epi: (b, 0)),
+                pl.BlockSpec((BLK, HD), lambda b, epi, flag: (flag[1] + b, 0)),
+                pl.BlockSpec(resident.shape, lambda b, epi, flag: (0, 0)),
+                pl.BlockSpec(anchored.shape, lambda b, epi, flag: (0, 0)),
+            ]
+            + [spec_slot(e) for e in range(slots)]
+            + [spec_slot(e) for e in range(slots)],
+            out_specs=pl.BlockSpec((BLK, HD), lambda b, epi, flag: (b, 0)),
         ),
-    )(epi_rows, queries, own, anchored, *([nearby] * slots))
+    )(epi_rows, flags, resident, resident, anchored, *([other] * slots), *([far] * slots))
 
 
 def broadcast_view(value, root, count):
@@ -128,7 +133,6 @@
         return lax.all_to_all(wide, SUB, 0, 0, tiled=True).reshape(tile_n * tile_tokens, width)
 
     resident = to_units(projected.reshape(HEADS * per_dev, tile_tokens, 3 * HD))
-    q_mine = lax.dynamic_slice_in_dim(resident[:, :HD], half * part_rows, part_rows, 0)
     own_kv = resident[:, HD:]
     anchored = to_units(
         jnp.broadcast_to(anchor_tile[:, None], key_values.shape).reshape(
@@ -143,15 +147,10 @@
             dest_view = (v + 1) % views_n if c == 1 else (v - 1) % views_n
             pairs.append((v * core_n + c, dest_view * core_n + (1 - c)))
     far = lax.ppermute(own_kv, ("view", "core"), pairs)
-    nearby = jnp.where(
-        slot == 1,
-        jnp.concatenate([other, far], axis=0),
-        jnp.concatenate([far, other], axis=0),
-    )
-
     epi_rows = lax.dynamic_index_in_dim(epi_list, slot, 0, keepdims=False)
     epi_rows = lax.dynamic_slice_in_dim(epi_rows, half * (part_rows // BLK), part_rows // BLK, 0)
-    attended = attention(epi_rows, q_mine, own_kv, anchored, nearby)
+    flags = jnp.stack([slot, half * (part_rows // BLK)]).astype(jnp.int32)
+    attended = attention(epi_rows, flags, resident, anchored, other, far, part_rows)
     attended = attended.reshape(half_n, tile_tokens, HD)
     returned = lax.all_to_all(attended, HALF, 0, 0, tiled=True)
     returned = returned.reshape(HEADS, per_dev, tile_tokens, HD)

time: 153 us -> 151 us (0.987)
  other arithmetic: 5.56 us -> 2.05 us
  Pallas kernels: 16.3 us -> 18.5 us
  local copies, waits for them, and re-layouts: 7.78 us -> 6.01 us
    all_to_all x2, waiting for transfers between devices: 0.01 us -> 20.3 us  [to_units(): lax.all_to_all(wide, SUB, 0, 0, tiled=True)]
    ppermute x1, waiting for transfers between devices: 28.2 us -> 9.07 us  [layer(): far = lax.ppermute(own_kv, ('view', 'core'), pairs)]
    select_n x1 -> x0, other arithmetic: 4.15 us -> none  [layer(): jnp.where(slot == 1, jnp.concatenate([other, far], axis=0), jnp.concatena...]
    pallas_call x1, Pallas kernels: 16.3 us -> 18.5 us  [attention(): pl.pallas_call(attention_kernel, out_shape=jax.ShapeDtypeStruct((rows, HD...]
  transfers between devices with their start and end apart: 8 -> 8, of which waited for: 4 -> 5; matrix products, arithmetic and copies ran while one was open for 11% -> 7% of each run, Pallas kernels for 0% -> 0%
where the time goes in v5:
time: 151 us
  waiting for transfers between devices  56.7 us (38%)
  starting transfers between devices  35.9 us (24%)
  blocking collectives  18.7 us (12%)
  Pallas kernels  18.5 us (12%)
  matrix products  12.2 us (8%)
  local copies, waits for them, and re-layouts  6.01 us (4%)
  other arithmetic  2.05 us (1%)
    all_to_all x2, starting transfers between devices, to_units(): lax.all_to_all(wide, SUB, 0, 0, tiled=True)  23.6 us
    ppermute x2, waiting for transfers between devices, broadcast_view(): lax.ppermute(held, 'view', [(i, (i - step) % count) for i in range(count)])  21.9 us
    all_to_all x2, waiting for transfers between devices, to_units(): lax.all_to_all(wide, SUB, 0, 0, tiled=True)  20.3 us
    all_to_all x1, blocking collectives, layer(): returned = lax.all_to_all(attended, HALF, 0, 0, tiled=True)  18.7 us
    pallas_call x1, Pallas kernels, attention(): pl.pallas_call(attention_kernel, out_shape=jax.ShapeDtypeStruct((rows, HD...  18.5 us
    ppermute x1, waiting for transfers between devices, layer(): far = lax.ppermute(own_kv, ('view', 'core'), pairs)  9.07 us
    ppermute x2, starting transfers between devices, broadcast_view(): lax.ppermute(held, 'view', [(i, (i - step) % count) for i in range(count)])  8.14 us
    dot_general x1, matrix products, layer(): jnp.dot(anchor_latents, qkv_weight, preferred_element_type=jnp.float32)  5.51 us
  transfers between devices with their start and end apart: 8, of which 5 were waited for; matrix products, arithmetic and copies ran while one was open for 7% of the time, Pallas kernels for 0%

profile of v5, /device:TPU:1, one launch (start us, length us, event | category | flops | bytes accessed | tf_op | source)
XLA Modules:
  0.0 150.8 jit_solution(5539043371765357835)
XLA Ops:
  0.0 5.3 %convolution_convert_fusion = bf16[128,3072]{1,0:T(8,128)(2,1)S(1)} fusion(bf16[128,1536]{1,0:T(8,128)(2,1)} %bitcast.50, bf16[1536,3072]{1,0:T(8,128)(2,1)} %param.6), kind=kOutput, calls=%fused_computation | convolution fusion | flops 1208352768 | bytes 10616832 | tf_op jit(solution)/shard_map/dot_general | solution.py:117
  5.4 0.1 copy.15
  5.5 0.1 copy.9
  5.6 1.4 broadcast_in_dim.24
  7.0 12.8 %all-to-all-start = ((bf16[32,64,384]{2,1,0:T(8,128)(2,1)}), bf16[32,64,384]{2,1,0:T(8,128)(2,1)}, u32[]{:S(2)}, u32[]{:S(2)}) async-start(bf16[32,64,384]{2,1,0:T(8,128)(2,1)} %bitcast.45), calls=%async_computation | async-start | bytes 3145728 | tf_op jit(solution)/shard_map/all_to_all | solution.py:133
  20.5 0.7 select_bitcast_fusion
  21.2 2.6 %collective-permute-start.1 = (bf16[64,1536]{1,0:T(8,128)(2,1)}, bf16[64,1536]{1,0:T(8,128)(2,1)}, u32[]{:S(2)}, u32[]{:S(2)}) collective-permute-start(bf16[64,1536]{1,0:T(8,128)(2,1)} %select_bitcast_fusion), channel_id=1, source_target_pairs={{0,224},{32,0},{64,32},{96,64},{128,96},{160,128},{192,160},{224,1... | collective-permute-start | bytes 589832 | tf_op jit(solution)/shard_map/ppermute | solution.py:95
  23.8 0.0 collective-permute-start
  23.8 15.2 %collective-permute-done.1 = bf16[64,1536]{1,0:T(8,128)(2,1)} collective-permute-done((bf16[64,1536]{1,0:T(8,128)(2,1)}, bf16[64,1536]{1,0:T(8,128)(2,1)}, u32[]{:S(2)}, u32[]{:S(2)}) %collective-permute-start.1) | collective-permute-done | bytes 196640 | tf_op jit(solution)/shard_map/ppermute | solution.py:95
  39.0 0.0 collective-permute-done
  39.0 0.7 select_select_fusion
  39.8 5.6 %collective-permute-start.3 = (bf16[64,1536]{1,0:T(8,128)(2,1)}, bf16[64,1536]{1,0:T(8,128)(2,1)S(1)}, u32[]{:S(2)}, u32[]{:S(2)}) collective-permute-start(bf16[64,1536]{1,0:T(8,128)(2,1)} %select_select_fusion), channel_id=1, source_target_pairs={{0,160},{32,192},{64,224},{96,0},{128,32},{160,64},{192,96},{224,1... | collective-permute-start | bytes 589832 | tf_op jit(solution)/shard_map/ppermute | solution.py:95
  45.3 0.0 collective-permute-start.2
  45.3 6.7 %collective-permute-done.3 = bf16[64,1536]{1,0:T(8,128)(2,1)S(1)} collective-permute-done((bf16[64,1536]{1,0:T(8,128)(2,1)}, bf16[64,1536]{1,0:T(8,128)(2,1)S(1)}, u32[]{:S(2)}, u32[]{:S(2)}) %collective-permute-start.3) | collective-permute-done | bytes 196640 | tf_op jit(solution)/shard_map/ppermute | solution.py:95
  52.0 5.4 %collective-permute-done.2 = bf16[64,1536]{1,0:T(8,128)(2,1)S(1)} collective-permute-done((bf16[64,1536]{1,0:T(8,128)(2,1)}, bf16[64,1536]{1,0:T(8,128)(2,1)S(1)}, u32[]{:S(2)}, u32[]{:S(2)}) %collective-permute-start.2) | collective-permute-done | bytes 196640 | tf_op jit(solution)/shard_map/ppermute | solution.py:94
  57.3 5.5 %convolution_convert_fusion.1 = bf16[64,3072]{1,0:T(8,128)(2,1)S(1)} fusion(bf16[1536,3072]{1,0:T(8,128)(2,1)} %param.6, bf16[64,1536]{1,0:T(8,128)(2,1)S(1)} %collective-permute-done.2, bf16[64,1536]{1,0:T(8,128)(2,1)S(1)} %collective-permute-done.3, bf16[64,1536]{1,0:T(8,128)(2,1)} %select_select_fusion, pred[]{:T(512)S(6)} %and.35, pred[]{:T(512)S(6)} %and.31), kind=kOutput, calls=%fused_computation.1 | convolution fusion | flops 604372992 | bytes 10420226 | tf_op jit(solution)/shard_map/dot_general | solution.py:124
  62.9 0.1 copy.16
  63.0 0.0 all-to-all-done
  63.1 1.1 broadcast_in_dim.28
  64.2 10.8 %all-to-all-start.1 = ((bf16[32,64,256]{2,1,0:T(8,128)(2,1)}), bf16[32,64,256]{2,1,0:T(8,128)(2,1)}, u32[]{:S(2)}, u32[]{:S(2)}) async-start(bf16[32,64,256]{2,1,0:T(8,128)(2,1)} %bitcast.46), calls=%async_computation.1 | async-start | bytes 2097152 | tf_op jit(solution)/shard_map/all_to_all | solution.py:133
  75.0 2.3 %slice.9 = bf16[2048,256]{1,0:T(8,128)(2,1)} slice(bf16[2048,384]{1,0:T(8,128)(2,1)} %bitcast.7.q_ref.own_ref), slice={[0:2048], [128:384]} | slice | bytes 2097152 | tf_op jit(solution)/shard_map/slice | solution.py:136
  77.3 1.2 collective-permute-start.5
  78.5 2.9 %collective-permute-start.4 = (bf16[2048,256]{1,0:T(8,128)(2,1)}, bf16[2048,256]{1,0:T(8,128)(2,1)}, u32[]{:S(2)}, u32[]{:S(2)}) collective-permute-start(bf16[2048,256]{1,0:T(8,128)(2,1)} %slice.9), channel_id=1, source_target_pairs={{0,1},{1,0},{2,3},{3,2},{4,5},{5,4},{6,7},{7,6},{8,9},{9,8},{10,11... | collective-permute-start | bytes 3145736 | tf_op jit(solution)/shard_map/ppermute | solution.py:143
  81.4 0.1 constant_dynamic-slice_fusion
  81.5 0.7 copy.14
  82.2 0.6 pad_add_fusion.flag_ref
  82.8 20.3 %all-to-all-done.1 = bf16[32,64,256]{2,1,0:T(8,128)(2,1)} async-done(((bf16[32,64,256]{2,1,0:T(8,128)(2,1)}), bf16[32,64,256]{2,1,0:T(8,128)(2,1)}, u32[]{:S(2)}, u32[]{:S(2)}) %all-to-all-start.1) | async-done | bytes 1048608 | tf_op jit(solution)/shard_map/all_to_all | solution.py:133
  103.2 9.1 %collective-permute-done.5.rest_6_.rest_7_.rest_8_.rest_9_.rest_10_.rest_11_ = bf16[2048,256]{1,0:T(8,128)(2,1)} collective-permute-done((bf16[2048,256]{1,0:T(8,128)(2,1)}, bf16[2048,256]{1,0:T(8,128)(2,1)}, u32[]{:S(2)}, u32[]{:S(2)}) %collective-permute-start.5) | collective-permute-done | bytes 1048608 | tf_op jit(solution)/shard_map/ppermute | solution.py:149
  112.2 0.0 collective-permute-done.4.rest_0_.rest_1_.rest_2_.rest_3_.rest_4_.rest_5_
  112.2 18.5 %shard_map.55 = bf16[1024,128]{1,0:T(8,128)(2,1)} custom-call(s32[8,6]{1,0:T(8,128)} %bitcast.56, s32[2]{0:T(128)} %pad_add_fusion.flag_ref, bf16[2048,384]{1,0:T(8,128)(2,1)} %bitcast.7.q_ref.own_ref, bf16[2048,384]{1,0:T(8,128)(2,1)} %bitcast.7.q_ref.own_ref, bf16[2048,256]{1,0:T(8,128)(2,1)} %bitcast.13.anc_ref, ...), custom_call_target="tpu_custom_call" | custom-call | tf_op jit(solution)/shard_map/pallas_call | solution.py:69
  130.7 18.7 %all_to_all.15 = bf16[16,64,128]{2,1,0:T(8,128)(2,1)S(1)} all-to-all(bf16[16,64,128]{2,1,0:T(8,128)(2,1)} %bitcast.55), channel_id=1, replica_groups=mesh['view'=8,'zh'=2,'zl'=4,'yhi'=2,'core'=2] {'zl','yhi','core'}, dimensions={0} | all-to-all | bytes 524288 | tf_op jit(solution)/shard_map/all_to_all | solution.py:155
  149.4 1.3 fusion
  (9 shorter events, 0.1 us)
Async XLA Ops:
  0.0 149.4 %copy-start = (bf16[1024,1536]{1,0:T(8,128)(2,1)S(1)}, bf16[1024,1536]{1,0:T(8,128)(2,1)}, u32[]{:S(2)}) copy-start(bf16[1024,1536]{1,0:T(8,128)(2,1)} %param.7) | copy-start | bytes 9437188
  0.0 20.5 %copy-start.1 = (bf16[2,64,1536]{2,1,0:T(8,128)(2,1)S(1)}, bf16[2,64,1536]{2,1,0:T(8,128)(2,1)}, u32[]{:S(2)}) copy-start(bf16[2,64,1536]{2,1,0:T(8,128)(2,1)} %param.5) | copy-start | bytes 1179652
  7.0 56.0 %all-to-all-start = ((bf16[32,64,384]{2,1,0:T(8,128)(2,1)}), bf16[32,64,384]{2,1,0:T(8,128)(2,1)}, u32[]{:S(2)}, u32[]{:S(2)}) async-start(bf16[32,64,384]{2,1,0:T(8,128)(2,1)} %bitcast.45), calls=%async_computation | async-start | bytes 3145728 | tf_op jit(solution)/shard_map/all_to_all | solution.py:133
  21.2 17.8 %collective-permute-start.1 = (bf16[64,1536]{1,0:T(8,128)(2,1)}, bf16[64,1536]{1,0:T(8,128)(2,1)}, u32[]{:S(2)}, u32[]{:S(2)}) collective-permute-start(bf16[64,1536]{1,0:T(8,128)(2,1)} %select_bitcast_fusion), channel_id=1, source_target_pairs={{0,224},{32,0},{64,32},{96,64},{128,96},{160,128},{192,160},{224,1... | collective-permute-start | bytes 589832 | tf_op jit(solution)/shard_map/ppermute | solution.py:95
  23.8 15.2 %collective-permute-start = (bf16[64,1536]{1,0:T(8,128)(2,1)}, bf16[64,1536]{1,0:T(8,128)(2,1)}, u32[]{:S(2)}, u32[]{:S(2)}) collective-permute-start(bf16[64,1536]{1,0:T(8,128)(2,1)} %select_bitcast_fusion), channel_id=1, source_target_pairs={{0,32},{32,64},{64,96},{96,128},{128,160},{160,192},{192,224},{224... | collective-permute-start | bytes 589832 | tf_op jit(solution)/shard_map/ppermute | solution.py:94
  39.8 12.2 %collective-permute-start.3 = (bf16[64,1536]{1,0:T(8,128)(2,1)}, bf16[64,1536]{1,0:T(8,128)(2,1)S(1)}, u32[]{:S(2)}, u32[]{:S(2)}) collective-permute-start(bf16[64,1536]{1,0:T(8,128)(2,1)} %select_select_fusion), channel_id=1, source_target_pairs={{0,160},{32,192},{64,224},{96,0},{128,32},{160,64},{192,96},{224,1... | collective-permute-start | bytes 589832 | tf_op jit(solution)/shard_map/ppermute | solution.py:95
  45.3 12.0 %collective-permute-start.2 = (bf16[64,1536]{1,0:T(8,128)(2,1)}, bf16[64,1536]{1,0:T(8,128)(2,1)S(1)}, u32[]{:S(2)}, u32[]{:S(2)}) collective-permute-start(bf16[64,1536]{1,0:T(8,128)(2,1)} %select_select_fusion), channel_id=1, source_target_pairs={{0,96},{32,128},{64,160},{96,192},{128,224},{160,0},{192,32},{224,... | collective-permute-start | bytes 589832 | tf_op jit(solution)/shard_map/ppermute | solution.py:94
  45.3 36.1 %copy-start.2 = (s32[2,16,6]{1,0,2:T(2,128)S(1)}, s32[2,16,6]{1,0,2:T(2,128)}, u32[]{:S(2)}) copy-start(s32[2,16,6]{1,0,2:T(2,128)} %param.9) | copy-start | bytes 2308
  64.2 39.0 %all-to-all-start.1 = ((bf16[32,64,256]{2,1,0:T(8,128)(2,1)}), bf16[32,64,256]{2,1,0:T(8,128)(2,1)}, u32[]{:S(2)}, u32[]{:S(2)}) async-start(bf16[32,64,256]{2,1,0:T(8,128)(2,1)} %bitcast.46), calls=%async_computation.1 | async-start | bytes 2097152 | tf_op jit(solution)/shard_map/all_to_all | solution.py:133
  77.3 34.9 %collective-permute-start.5 = (bf16[2048,256]{1,0:T(8,128)(2,1)}, bf16[2048,256]{1,0:T(8,128)(2,1)}, u32[]{:S(2)}, u32[]{:S(2)}) collective-permute-start(bf16[2048,256]{1,0:T(8,128)(2,1)} %slice.9), channel_id=1, source_target_pairs={{0,225},{1,32},{32,1},{33,64},{64,33},{65,96},{96,65},{97,128},{12... | collective-permute-start | bytes 3145736 | tf_op jit(solution)/shard_map/ppermute | solution.py:149
  78.5 33.7 %collective-permute-start.4 = (bf16[2048,256]{1,0:T(8,128)(2,1)}, bf16[2048,256]{1,0:T(8,128)(2,1)}, u32[]{:S(2)}, u32[]{:S(2)}) collective-permute-start(bf16[2048,256]{1,0:T(8,128)(2,1)} %slice.9), channel_id=1, source_target_pairs={{0,1},{1,0},{2,3},{3,2},{4,5},{5,4},{6,7},{7,6},{8,9},{9,8},{10,11... | collective-permute-start | bytes 3145736 | tf_op jit(solution)/shard_map/ppermute | solution.py:143

commit v6 on v5

--- a/solution.py
+++ b/solution.py
@@ -15,7 +15,7 @@
 NBLK = 16
 
 SUB = ("zh", "zl", "yhi", "core")
-HALF = ("zl", "yhi", "core")
+CHIPS = ("zh", "zl", "yhi")
 
 
 def attention_kernel(epi_ref, flag_ref, q_ref, own_ref, anc_ref, *rest):
@@ -34,7 +34,7 @@
     own = own_ref[...]
     anc = anc_ref[...]
     parts = [
-        (scores_of(own[:, HD : 2 * HD]), own[:, 2 * HD :]),
+        (scores_of(own[:, :HD]), own[:, HD:]),
         (scores_of(anc[:, :HD]), anc[:, HD:]),
     ]
     for slot in range(slots):
@@ -57,8 +57,10 @@
     o_ref[...] = (summed / total).astype(o_ref.dtype)
 
 
-def attention(epi_rows, flags, resident, anchored, other, far, rows):
+def attention(epi_rows, flags, resident, own, anchored, other, far, q_rows):
     slots = epi_rows.shape[1]
+    blocks = epi_rows.shape[0]
+    parts = BLK // q_rows
 
     def spec_slot(slot):
         return pl.BlockSpec(
@@ -68,20 +70,20 @@
 
     return pl.pallas_call(
         attention_kernel,
-        out_shape=jax.ShapeDtypeStruct((rows, HD), jnp.bfloat16),
+        out_shape=jax.ShapeDtypeStruct((blocks * q_rows, HD), jnp.bfloat16),
         grid_spec=pltpu.PrefetchScalarGridSpec(
             num_scalar_prefetch=2,
-            grid=(rows // BLK,),
+            grid=(blocks,),
             in_specs=[
-                pl.BlockSpec((BLK, HD), lambda b, epi, flag: (flag[1] + b, 0)),
-                pl.BlockSpec(resident.shape, lambda b, epi, flag: (0, 0)),
+                pl.BlockSpec((q_rows, HD), lambda b, epi, flag: (parts * b + flag[1], 0)),
+                pl.BlockSpec(own.shape, lambda b, epi, flag: (0, 0)),
                 pl.BlockSpec(anchored.shape, lambda b, epi, flag: (0, 0)),
             ]
             + [spec_slot(e) for e in range(slots)]
             + [spec_slot(e) for e in range(slots)],
-            out_specs=pl.BlockSpec((BLK, HD), lambda b, epi, flag: (b, 0)),
+            out_specs=pl.BlockSpec((q_rows, HD), lambda b, epi, flag: (b, 0)),
         ),
-    )(epi_rows, flags, resident, resident, anchored, *([other] * slots), *([far] * slots))
+    )(epi_rows, flags, resident, own, anchored, *([other] * slots), *([far] * slots))
 
 
 def broadcast_view(value, root, count):
@@ -103,12 +105,10 @@
 def layer(latents, qkv_weight, out_weight, anchor, epi_list):
     per_dev, tile_tokens, model_width = latents.shape
     views_n = lax.axis_size("view")
-    half_n = lax.axis_size(HALF)
     tile_n = lax.axis_size(SUB)
-    part_rows = tile_tokens * half_n
-    core_n = lax.axis_size("core")
-    slot = lax.axis_index("core")
-    half = lax.axis_index("zh")
+    zl_n = lax.axis_size("zl")
+    part = lax.axis_index("core")
+    slot = lax.axis_index("zl") % 2
 
     target = anchor[0]
     anchor_latents = lax.dynamic_index_in_dim(latents, target % per_dev, 0, keepdims=False)
@@ -119,40 +119,39 @@
         preferred_element_type=jnp.float32,
     ).astype(jnp.bfloat16)
     projected = flat.reshape(per_dev, tile_tokens, HEADS, 3 * HD).transpose(2, 0, 1, 3)
-    key_values = projected[..., HD:]
 
     anchor_tile = jnp.dot(
         anchor_latents, qkv_weight, preferred_element_type=jnp.float32
     ).astype(jnp.bfloat16)
     anchor_tile = anchor_tile.reshape(tile_tokens, HEADS, 3 * HD)[..., HD:].transpose(1, 0, 2)
 
-    def to_units(source):
-        width = source.shape[-1]
-        wide = jnp.broadcast_to(source[None], (tile_n // (HEADS * per_dev),) + source.shape)
-        wide = wide.reshape(tile_n, tile_tokens, width)
-        return lax.all_to_all(wide, SUB, 0, 0, tiled=True).reshape(tile_n * tile_tokens, width)
+    by_unit = projected.reshape(2, 2, 2, per_dev, tile_tokens, 3 * HD).transpose(0, 1, 3, 2, 4, 5)
+    anchor_by = jnp.broadcast_to(
+        anchor_tile.reshape(2, 2, 1, 2, tile_tokens, 2 * HD), by_unit.shape[:-1] + (2 * HD,)
+    )
+    with_anchor = jnp.concatenate([by_unit[..., :HD], anchor_by], axis=-1)
+    send = jnp.stack([by_unit, with_anchor], axis=4).reshape(tile_n, tile_tokens, 3 * HD)
+    received = lax.all_to_all(send, SUB, 0, 0, tiled=True).reshape(tile_n * tile_tokens, 3 * HD)
+    mine = received[:, HD:]
+    swapped = lax.ppermute(mine, "core", [(0, 1), (1, 0)])
+    own_kv = jnp.where(part == 0, mine, swapped)
+    anchored = jnp.where(part == 0, swapped, mine)
 
-    resident = to_units(projected.reshape(HEADS * per_dev, tile_tokens, 3 * HD))
-    own_kv = resident[:, HD:]
-    anchored = to_units(
-        jnp.broadcast_to(anchor_tile[:, None], key_values.shape).reshape(
-            HEADS * per_dev, tile_tokens, 2 * HD
-        )
-    )
-
-    other = lax.ppermute(own_kv, "core", [(0, 1), (1, 0)])
+    other = lax.ppermute(own_kv, "zl", [(z, z ^ 1) for z in range(zl_n)])
     pairs = []
     for v in range(views_n):
-        for c in range(core_n):
-            dest_view = (v + 1) % views_n if c == 1 else (v - 1) % views_n
-            pairs.append((v * core_n + c, dest_view * core_n + (1 - c)))
-    far = lax.ppermute(own_kv, ("view", "core"), pairs)
+        for z in range(zl_n):
+            dest_view = (v + 1) % views_n if z % 2 == 1 else (v - 1) % views_n
+            pairs.append((v * zl_n + z, dest_view * zl_n + (z ^ 1)))
+    far = lax.ppermute(own_kv, ("view", "zl"), pairs)
+
     epi_rows = lax.dynamic_index_in_dim(epi_list, slot, 0, keepdims=False)
-    epi_rows = lax.dynamic_slice_in_dim(epi_rows, half * (part_rows // BLK), part_rows // BLK, 0)
-    flags = jnp.stack([slot, half * (part_rows // BLK)]).astype(jnp.int32)
-    attended = attention(epi_rows, flags, resident, anchored, other, far, part_rows)
-    attended = attended.reshape(half_n, tile_tokens, HD)
-    returned = lax.all_to_all(attended, HALF, 0, 0, tiled=True)
+    flags = jnp.stack([slot, part]).astype(jnp.int32)
+    attended = attention(epi_rows, flags, received, own_kv, anchored, other, far, tile_tokens)
+    chips_n = tile_n // 2
+    attended = attended.reshape(chips_n, tile_tokens, HD)
+    returned = lax.all_to_all(attended, CHIPS, 0, 0, tiled=True)
+    returned = returned.reshape(2, 2, per_dev, 2, tile_tokens, HD).transpose(0, 1, 3, 2, 4, 5)
     returned = returned.reshape(HEADS, per_dev, tile_tokens, HD)
     projected_out = jnp.einsum(
         "hvtc,hcd->vtd",

time: 151 us -> 194 us (1.28)
  blocking collectives: 18.7 us -> 70.6 us
  starting transfers between devices: 35.9 us -> 13.7 us
  Pallas kernels: 18.5 us -> 29.1 us
  waiting for transfers between devices: 56.7 us -> 46.8 us
  local copies, waits for them, and re-layouts: 6.01 us -> 13.2 us
  other arithmetic: 2.05 us -> 6.36 us
    all_to_all x1 -> x2, blocking collectives: 18.7 us -> 70.6 us  [the longest x1 53.2 us: layer(): lax.all_to_all(send, SUB, 0, 0, tiled=True)]
    ppermute x2 -> x3, waiting for transfers between devices: 9.07 us -> 46.3 us  [the longest x1 22.1 us: layer(): far = lax.ppermute(own_kv, ('view', 'zl'), pairs)]
    all_to_all x2 -> x0, starting transfers between devices: 23.6 us -> none  [to_units(): lax.all_to_all(wide, SUB, 0, 0, tiled=True)]
    ppermute x2, waiting for transfers between devices: 21.9 us -> 0.01 us  [broadcast_view(): lax.ppermute(held, 'view', [(i, (i - step) % count) for i in range(count)])]
    all_to_all x2 -> x0, waiting for transfers between devices: 20.3 us -> none  [to_units(): lax.all_to_all(wide, SUB, 0, 0, tiled=True)]
    pallas_call x1, Pallas kernels: 18.5 us -> 29.1 us  [attention(): pl.pallas_call(attention_kernel, out_shape=jax.ShapeDtypeStruct((blocks *...]
    ppermute x2, waiting for transfers between devices: 5.38 us -> 0.49 us  [broadcast_view(): lax.ppermute(held, 'view', [(i, (i + step) % count) for i in range(count)])]
    unnamed x9 -> x14, local copies, waits for them, and re-layouts: 0.87 us -> 5.08 us
  transfers between devices with their start and end apart: 8 -> 7, of which waited for: 5 -> 4; matrix products, arithmetic and copies ran while one was open for 7% -> 8% of each run, Pallas kernels for 0% -> 0%
where the time goes in v6:
time: 194 us
  blocking collectives  70.6 us (36%)
  waiting for transfers between devices  46.8 us (24%)
  Pallas kernels  29.1 us (15%)
  starting transfers between devices  13.7 us (7%)
  local copies, waits for them, and re-layouts  13.2 us (7%)
  matrix products  13.1 us (7%)
  other arithmetic  6.36 us (3%)
    all_to_all x1, blocking collectives, layer(): lax.all_to_all(send, SUB, 0, 0, tiled=True)  53.2 us
    pallas_call x1, Pallas kernels, attention(): pl.pallas_call(attention_kernel, out_shape=jax.ShapeDtypeStruct((blocks *...  29.1 us
    ppermute x1, waiting for transfers between devices, layer(): far = lax.ppermute(own_kv, ('view', 'zl'), pairs)  22.1 us
    ppermute x1, waiting for transfers between devices, layer(): other = lax.ppermute(own_kv, 'zl', [(z, z ^ 1) for z in range(zl_n)])  21.6 us
    all_to_all x1, blocking collectives, layer(): returned = lax.all_to_all(attended, CHIPS, 0, 0, tiled=True)  17.4 us
    ppermute x2, starting transfers between devices, broadcast_view(): lax.ppermute(held, 'view', [(i, (i - step) % count) for i in range(count)])  7.92 us
    dot_general x1, matrix products, layer(): jnp.dot(latents.reshape(per_dev * tile_tokens, model_width), qkv_weight,...  6.18 us
    dot_general x1, matrix products, layer(): jnp.dot(anchor_latents, qkv_weight, preferred_element_type=jnp.float32)  5.63 us
  transfers between devices with their start and end apart: 7, of which 4 were waited for; matrix products, arithmetic and copies ran while one was open for 8% of the time, Pallas kernels for 0%

profile of v6, /device:TPU:1, one launch (start us, length us, event | category | flops | bytes accessed | tf_op | source)
XLA Modules:
  0.0 193.8 jit_solution(1861045685784543606)
XLA Ops:
  0.9 1.7 select_bitcast_fusion
  2.6 4.3 %collective-permute-start.1 = (bf16[64,1536]{1,0:T(8,128)(2,1)}, bf16[64,1536]{1,0:T(8,128)(2,1)}, u32[]{:S(2)}, u32[]{:S(2)}) collective-permute-start(bf16[64,1536]{1,0:T(8,128)(2,1)} %select_bitcast_fusion), channel_id=1, source_target_pairs={{0,224},{32,0},{64,32},{96,64},{128,96},{160,128},{192,160},{224,1... | collective-permute-start | bytes 589832 | tf_op jit(solution)/shard_map/ppermute | solution.py:97
  6.9 0.0 collective-permute-start
  6.9 6.2 %convolution_convert_fusion = bf16[128,3072]{1,0:T(8,128)(2,1)} fusion(bf16[128,1536]{1,0:T(8,128)(2,1)} %bitcast.69, bf16[1536,3072]{1,0:T(8,128)(2,1)} %param.6), kind=kOutput, calls=%fused_computation | convolution fusion | flops 1208352768 | bytes 10616832 | tf_op jit(solution)/shard_map/dot_general | solution.py:117
  13.1 2.2 %copy.16 = bf16[16,8,8,384]{3,2,1,0:T(8,128)(2,1)} copy(bf16[16,8,8,384]{3,1,2,0:T(8,128)(2,1)} %bitcast.67) | data formatting | bytes 1572864
  15.2 0.0 collective-permute-done.1
  15.2 0.0 collective-permute-done
  15.2 0.7 select_select_fusion
  16.0 3.6 %collective-permute-start.3 = (bf16[64,1536]{1,0:T(8,128)(2,1)}, bf16[64,1536]{1,0:T(8,128)(2,1)}, u32[]{:S(2)}, u32[]{:S(2)}) collective-permute-start(bf16[64,1536]{1,0:T(8,128)(2,1)} %select_select_fusion), channel_id=1, source_target_pairs={{0,160},{32,192},{64,224},{96,0},{128,32},{160,64},{192,96},{224,1... | collective-permute-start | bytes 589832 | tf_op jit(solution)/shard_map/ppermute | solution.py:97
  19.6 2.1 %bitcast_bitcast_fusion = bf16[8,2,64,384]{3,0,2,1:T(8,128)(2,1)} fusion(bf16[2,64,8,384]{3,2,1,0:T(8,128)(2,1)} %bitcast.68), kind=kLoop, calls=%fused_computation.7 | loop fusion | bytes 1572864 | tf_op jit(solution)/shard_map/transpose | solution.py:121
  21.7 2.8 %reshape.37 = bf16[2,2,2,2,64,384]{5,2,1,0,4,3:T(2,128)(2,1)} reshape(bf16[8,2,64,384]{3,0,2,1:T(8,128)(2,1)} %bitcast_bitcast_fusion) | data formatting | bytes 1572864 | tf_op jit(solution)/shard_map/reshape | solution.py:128
  24.6 1.3 copy.20
  25.8 0.9 copy-done.2
  26.8 0.5 collective-permute-done.2
  27.3 5.6 %convolution_convert_fusion.1 = bf16[64,3072]{1,0:T(8,128)(2,1)S(1)} fusion(bf16[1536,3072]{1,0:T(8,128)(2,1)} %param.6, bf16[64,1536]{1,0:T(8,128)(2,1)} %collective-permute-done.2, bf16[64,1536]{1,0:T(8,128)(2,1)} %collective-permute-done.3, bf16[64,1536]{1,0:T(8,128)(2,1)} %select_select_fusion, pred[]{:T(512)S(6)} %and.40, pred[]{:T(512)S(6)} %and.36), kind=kOutput, calls=%fused_computation.1 | convolution fusion | flops 604372992 | bytes 10420226 | tf_op jit(solution)/shard_map/dot_general | solution.py:123
  33.1 0.1 maximum_bitcast_fusion
  33.3 0.8 copy-done.3
  34.1 0.2 pad_maximum_fusion
  34.2 53.2 %all_to_all.10 = bf16[32,64,384]{2,1,0:T(8,128)(2,1)S(1)} all-to-all(bf16[32,64,384]{2,1,0:T(8,128)(2,1)S(1)} %bitcast.64), channel_id=1, replica_groups=mesh['view'=8,'zh'=2,'zl'=4,'yhi'=2,'core'=2] {'zh','zl','yhi','core'}, dimensions={0} | all-to-all | bytes 3145728 | tf_op jit(solution)/shard_map/all_to_all | solution.py:134
  87.5 1.2 copy-done.1
  88.6 1.0 slice.14
  89.7 1.4 collective-permute-start.4
  91.1 2.6 %collective-permute-done.4 = bf16[2048,256]{1,0:T(8,128)(2,1)} collective-permute-done((bf16[2048,256]{1,0:T(8,128)(2,1)}, bf16[2048,256]{1,0:T(8,128)(2,1)}, u32[]{:S(2)}, u32[]{:S(2)}) %collective-permute-start.4) | collective-permute-done | bytes 1048608 | tf_op jit(solution)/shard_map/ppermute | solution.py:136
  93.7 3.0 %broadcast_select_fusion = (bf16[2048,256]{1,0:T(8,128)(2,1)}, bf16[2048,256]{1,0:T(8,128)(2,1)}) fusion(bf16[2048,256]{1,0:T(8,128)(2,1)} %collective-permute-done.4, pred[]{:T(512)S(6)} %eq.12, bf16[2048,384]{1,0:T(8,128)(2,1)} %bitcast.62), kind=kLoop, calls=%fused_computation.5 | loop fusion | flops 1048576 | bytes 4194305 | tf_op jit(solution)/shard_map/jit(_where)/select_n | solution.py:138
  96.7 4.3 %collective-permute-start.6 = (bf16[2048,256]{1,0:T(8,128)(2,1)}, bf16[2048,256]{1,0:T(8,128)(2,1)}, u32[]{:S(2)}, u32[]{:S(2)}) collective-permute-start(bf16[2048,256]{1,0:T(8,128)(2,1)} %get-tuple-element.6.own_ref), channel_id=1, source_target_pairs={{0,228},{4,32},{8,236},{12,40},{32,4},{36,64},{40,12},{44,72},{64,... | collective-permute-start | bytes 3145736 | tf_op jit(solution)/shard_map/ppermute | solution.py:146
  101.1 0.7 copy.15
  101.7 0.6 pad_add_fusion.flag_ref
  102.3 22.1 %collective-permute-done.6.rest_6_.rest_7_.rest_8_.rest_9_.rest_10_.rest_11_ = bf16[2048,256]{1,0:T(8,128)(2,1)} collective-permute-done((bf16[2048,256]{1,0:T(8,128)(2,1)}, bf16[2048,256]{1,0:T(8,128)(2,1)}, u32[]{:S(2)}, u32[]{:S(2)}) %collective-permute-start.6) | collective-permute-done | bytes 1048608 | tf_op jit(solution)/shard_map/ppermute | solution.py:146
  124.4 21.6 %collective-permute-done.5.rest_0_.rest_1_.rest_2_.rest_3_.rest_4_.rest_5_ = bf16[2048,256]{1,0:T(8,128)(2,1)} collective-permute-done((bf16[2048,256]{1,0:T(8,128)(2,1)}, bf16[2048,256]{1,0:T(8,128)(2,1)}, u32[]{:S(2)}, u32[]{:S(2)}) %collective-permute-start.5) | collective-permute-done | bytes 1048608 | tf_op jit(solution)/shard_map/ppermute | solution.py:140
  146.0 29.1 %shard_map.55 = bf16[1024,128]{1,0:T(8,128)(2,1)} custom-call(s32[16,6]{1,0:T(8,128)} %bitcast.76, s32[2]{0:T(128)} %pad_add_fusion.flag_ref, bf16[2048,384]{1,0:T(8,128)(2,1)} %bitcast.63, bf16[2048,256]{1,0:T(8,128)(2,1)} %get-tuple-element.6.own_ref, bf16[2048,256]{1,0:T(8,128)(2,1)} %get-tuple-element.5.anc_ref, ...), custom_call_target="tpu_custom_call" | custom-call | tf_op jit(solution)/shard_map/pallas_call | solution.py:71
  175.0 17.4 %all_to_all.11 = bf16[16,64,128]{2,1,0:T(8,128)(2,1)S(1)} all-to-all(bf16[16,64,128]{2,1,0:T(8,128)(2,1)} %bitcast.73), channel_id=1, replica_groups=mesh['view'=8,'zh'=2,'zl'=4,'yhi'=2,'core'=2] {'zh','zl','yhi'}, dimensions={0} | all-to-all | bytes 524288 | tf_op jit(solution)/shard_map/all_to_all | solution.py:153
  192.5 1.3 fusion
  (19 shorter events, 0.3 us)
Async XLA Ops:
  0.0 192.5 %copy-start = (bf16[1024,1536]{1,0:T(8,128)(2,1)S(1)}, bf16[1024,1536]{1,0:T(8,128)(2,1)}, u32[]{:S(2)}) copy-start(bf16[1024,1536]{1,0:T(8,128)(2,1)} %param.7) | copy-start | bytes 9437188
  2.6 12.7 %collective-permute-start.1 = (bf16[64,1536]{1,0:T(8,128)(2,1)}, bf16[64,1536]{1,0:T(8,128)(2,1)}, u32[]{:S(2)}, u32[]{:S(2)}) collective-permute-start(bf16[64,1536]{1,0:T(8,128)(2,1)} %select_bitcast_fusion), channel_id=1, source_target_pairs={{0,224},{32,0},{64,32},{96,64},{128,96},{160,128},{192,160},{224,1... | collective-permute-start | bytes 589832 | tf_op jit(solution)/shard_map/ppermute | solution.py:97
  6.9 8.4 %collective-permute-start = (bf16[64,1536]{1,0:T(8,128)(2,1)}, bf16[64,1536]{1,0:T(8,128)(2,1)}, u32[]{:S(2)}, u32[]{:S(2)}) collective-permute-start(bf16[64,1536]{1,0:T(8,128)(2,1)} %select_bitcast_fusion), channel_id=1, source_target_pairs={{0,32},{32,64},{64,96},{96,128},{128,160},{160,192},{192,224},{224... | collective-permute-start | bytes 589832 | tf_op jit(solution)/shard_map/ppermute | solution.py:96
  6.9 8.4 %copy-start.4 = (bf16[2,64,1536]{2,1,0:T(8,128)(2,1)S(1)}, bf16[2,64,1536]{2,1,0:T(8,128)(2,1)}, u32[]{:S(2)}) copy-start(bf16[2,64,1536]{2,1,0:T(8,128)(2,1)} %param.5) | copy-start | bytes 1179652
  16.0 10.8 %collective-permute-start.3 = (bf16[64,1536]{1,0:T(8,128)(2,1)}, bf16[64,1536]{1,0:T(8,128)(2,1)}, u32[]{:S(2)}, u32[]{:S(2)}) collective-permute-start(bf16[64,1536]{1,0:T(8,128)(2,1)} %select_select_fusion), channel_id=1, source_target_pairs={{0,160},{32,192},{64,224},{96,0},{128,32},{160,64},{192,96},{224,1... | collective-permute-start | bytes 589832 | tf_op jit(solution)/shard_map/ppermute | solution.py:97
  19.6 7.7 %collective-permute-start.2 = (bf16[64,1536]{1,0:T(8,128)(2,1)}, bf16[64,1536]{1,0:T(8,128)(2,1)}, u32[]{:S(2)}, u32[]{:S(2)}) collective-permute-start(bf16[64,1536]{1,0:T(8,128)(2,1)} %select_select_fusion), channel_id=1, source_target_pairs={{0,96},{32,128},{64,160},{96,192},{128,224},{160,0},{192,32},{224,... | collective-permute-start | bytes 589832 | tf_op jit(solution)/shard_map/ppermute | solution.py:96
  25.8 0.9 copy-start.2
  32.9 1.1 copy-start.3
  87.5 1.2 copy-start.1
  88.6 12.4 %copy-start.5 = (s32[2,16,6]{1,0,2:T(2,128)S(1)}, s32[2,16,6]{1,0,2:T(2,128)}, u32[]{:S(2)}) copy-start(s32[2,16,6]{1,0,2:T(2,128)} %param.9) | copy-start | bytes 2308
  89.7 4.0 %collective-permute-start.4 = (bf16[2048,256]{1,0:T(8,128)(2,1)}, bf16[2048,256]{1,0:T(8,128)(2,1)}, u32[]{:S(2)}, u32[]{:S(2)}) collective-permute-start(bf16[2048,256]{1,0:T(8,128)(2,1)} %slice.14), channel_id=1, source_target_pairs={{0,1},{1,0},{2,3},{3,2},{4,5},{5,4},{6,7},{7,6},{8,9},{9,8},{10,11... | collective-permute-start | bytes 3145736 | tf_op jit(solution)/shard_map/ppermute | solution.py:136
  96.7 27.7 %collective-permute-start.6 = (bf16[2048,256]{1,0:T(8,128)(2,1)}, bf16[2048,256]{1,0:T(8,128)(2,1)}, u32[]{:S(2)}, u32[]{:S(2)}) collective-permute-start(bf16[2048,256]{1,0:T(8,128)(2,1)} %get-tuple-element.6.own_ref), channel_id=1, source_target_pairs={{0,228},{4,32},{8,236},{12,40},{32,4},{36,64},{40,12},{44,72},{64,... | collective-permute-start | bytes 3145736 | tf_op jit(solution)/shard_map/ppermute | solution.py:146
  101.0 44.9 %collective-permute-start.5 = (bf16[2048,256]{1,0:T(8,128)(2,1)}, bf16[2048,256]{1,0:T(8,128)(2,1)}, u32[]{:S(2)}, u32[]{:S(2)}) collective-permute-start(bf16[2048,256]{1,0:T(8,128)(2,1)} %get-tuple-element.6.own_ref), channel_id=1, source_target_pairs={{0,4},{4,0},{8,12},{12,8},{1,5},{5,1},{9,13},{13,9},{2,6},{6,2},{1... | collective-permute-start | bytes 3145736 | tf_op jit(solution)/shard_map/ppermute | solution.py:140

commit v7 on v5

--- a/solution.py
+++ b/solution.py
@@ -18,7 +18,7 @@
 HALF = ("zl", "yhi", "core")
 
 
-def attention_kernel(epi_ref, flag_ref, q_ref, own_ref, anc_ref, *rest):
+def attention_kernel(epi_ref, flag_ref, q_ref, own_ref, anc_ref, anc2_ref, *rest):
     block = pl.program_id(0)
     slots = epi_ref.shape[1]
     other_refs, far_refs, o_ref = rest[:slots], rest[slots:-1], rest[-1]
@@ -33,9 +33,11 @@
 
     own = own_ref[...]
     anc = anc_ref[...]
+    anc2 = anc2_ref[...]
     parts = [
         (scores_of(own[:, HD : 2 * HD]), own[:, 2 * HD :]),
         (scores_of(anc[:, :HD]), anc[:, HD:]),
+        (scores_of(anc2[:, :HD]), anc2[:, HD:]),
     ]
     for slot in range(slots):
         index = epi_ref[block, slot]
@@ -57,14 +59,16 @@
     o_ref[...] = (summed / total).astype(o_ref.dtype)
 
 
-def attention(epi_rows, flags, resident, anchored, other, far, rows):
+def attention(epi_rows, flags, resident, anchored, anchored2, other, far, rows):
     slots = epi_rows.shape[1]
 
-    def spec_slot(slot):
-        return pl.BlockSpec(
-            (BLK, 2 * HD),
-            lambda b, epi, flag: (jnp.clip(epi[b, slot], 0, 2 * NBLK - 1) % NBLK, 0),
-        )
+    def spec_slot(slot, want_other):
+        def index_map(b, epi, flag):
+            index = epi[b, slot]
+            used = (index >= 0) & ((index < NBLK) == ((flag[0] == 1) == want_other))
+            return (jnp.where(used, jnp.clip(index, 0, 2 * NBLK - 1) % NBLK, 0), 0)
+
+        return pl.BlockSpec((BLK, 2 * HD), index_map)
 
     return pl.pallas_call(
         attention_kernel,
@@ -76,12 +80,13 @@
                 pl.BlockSpec((BLK, HD), lambda b, epi, flag: (flag[1] + b, 0)),
                 pl.BlockSpec(resident.shape, lambda b, epi, flag: (0, 0)),
                 pl.BlockSpec(anchored.shape, lambda b, epi, flag: (0, 0)),
+                pl.BlockSpec(anchored2.shape, lambda b, epi, flag: (0, 0)),
             ]
-            + [spec_slot(e) for e in range(slots)]
-            + [spec_slot(e) for e in range(slots)],
+            + [spec_slot(e, True) for e in range(slots)]
+            + [spec_slot(e, False) for e in range(slots)],
             out_specs=pl.BlockSpec((BLK, HD), lambda b, epi, flag: (b, 0)),
         ),
-    )(epi_rows, flags, resident, resident, anchored, *([other] * slots), *([far] * slots))
+    )(epi_rows, flags, resident, resident, anchored, anchored2, *([other] * slots), *([far] * slots))
 
 
 def broadcast_view(value, root, count):
@@ -119,7 +124,6 @@
         preferred_element_type=jnp.float32,
     ).astype(jnp.bfloat16)
     projected = flat.reshape(per_dev, tile_tokens, HEADS, 3 * HD).transpose(2, 0, 1, 3)
-    key_values = projected[..., HD:]
 
     anchor_tile = jnp.dot(
         anchor_latents, qkv_weight, preferred_element_type=jnp.float32
@@ -134,11 +138,11 @@
 
     resident = to_units(projected.reshape(HEADS * per_dev, tile_tokens, 3 * HD))
     own_kv = resident[:, HD:]
-    anchored = to_units(
-        jnp.broadcast_to(anchor_tile[:, None], key_values.shape).reshape(
-            HEADS * per_dev, tile_tokens, 2 * HD
-        )
-    )
+    halves = anchor_tile.reshape(HEADS * core_n, tile_tokens // core_n, 2 * HD)
+    wide = jnp.broadcast_to(halves[None], (tile_n // (HEADS * core_n),) + halves.shape)
+    wide = wide.reshape(tile_n, tile_tokens // core_n, 2 * HD)
+    anchored = lax.all_to_all(wide, SUB, 0, 0, tiled=True).reshape(-1, 2 * HD)
+    anchored2 = lax.ppermute(anchored, "core", [(0, 1), (1, 0)])
 
     other = lax.ppermute(own_kv, "core", [(0, 1), (1, 0)])
     pairs = []
@@ -150,7 +154,7 @@
     epi_rows = lax.dynamic_index_in_dim(epi_list, slot, 0, keepdims=False)
     epi_rows = lax.dynamic_slice_in_dim(epi_rows, half * (part_rows // BLK), part_rows // BLK, 0)
     flags = jnp.stack([slot, half * (part_rows // BLK)]).astype(jnp.int32)
-    attended = attention(epi_rows, flags, resident, anchored, other, far, part_rows)
+    attended = attention(epi_rows, flags, resident, anchored, anchored2, other, far, part_rows)
     attended = attended.reshape(half_n, tile_tokens, HD)
     returned = lax.all_to_all(attended, HALF, 0, 0, tiled=True)
     returned = returned.reshape(HEADS, per_dev, tile_tokens, HD)

time: 151 us -> 147 us (0.974)
  waiting for transfers between devices: 56.7 us -> 50.8 us
    all_to_all x2 -> x1, waiting for transfers between devices: 20.3 us -> 0.01 us  [to_units(): lax.all_to_all(wide, SUB, 0, 0, tiled=True)]
    all_to_all x0 -> x1, waiting for transfers between devices: none -> 10.9 us  [layer(): anchored = lax.all_to_all(wide, SUB, 0, 0, tiled=True).reshape(-1, 2 * HD)]
    all_to_all x2 -> x1, starting transfers between devices: 23.6 us -> 12.8 us  [to_units(): lax.all_to_all(wide, SUB, 0, 0, tiled=True)]
    all_to_all x0 -> x1, starting transfers between devices: none -> 10.8 us  [layer(): anchored = lax.all_to_all(wide, SUB, 0, 0, tiled=True).reshape(-1, 2 * HD)]
    ppermute x1, waiting for transfers between devices: 9.07 us -> 12.2 us  [layer(): far = lax.ppermute(own_kv, ('view', 'core'), pairs)]
  transfers between devices with their start and end apart: 8 -> 9, of which waited for: 5 -> 6; matrix products, arithmetic and copies ran while one was open for 7% -> 7% of each run, Pallas kernels for 0% -> 0%
where the time goes in v7:
time: 147 us; the launch traced here: 146 us
  waiting for transfers between devices  50.8 us (35%)
  starting transfers between devices  37.1 us (25%)
  Pallas kernels  19.8 us (13%)
  blocking collectives  18 us (12%)
  matrix products  12.2 us (8%)
  local copies, waits for them, and re-layouts  5.7 us (4%)
  other arithmetic  2.03 us (1%)
    ppermute x2, waiting for transfers between devices, broadcast_view(): lax.ppermute(held, 'view', [(i, (i - step) % count) for i in range(count)])  21.9 us
    pallas_call x1, Pallas kernels, attention(): pl.pallas_call(attention_kernel, out_shape=jax.ShapeDtypeStruct((rows, HD...  19.8 us
    all_to_all x1, blocking collectives, layer(): returned = lax.all_to_all(attended, HALF, 0, 0, tiled=True)  18 us
    all_to_all x1, starting transfers between devices, to_units(): lax.all_to_all(wide, SUB, 0, 0, tiled=True)  12.8 us
    ppermute x1, waiting for transfers between devices, layer(): far = lax.ppermute(own_kv, ('view', 'core'), pairs)  12.2 us
    all_to_all x1, waiting for transfers between devices, layer(): anchored = lax.all_to_all(wide, SUB, 0, 0, tiled=True).reshape(-1, 2 * HD)  10.9 us
    all_to_all x1, starting transfers between devices, layer(): anchored = lax.all_to_all(wide, SUB, 0, 0, tiled=True).reshape(-1, 2 * HD)  10.8 us
    ppermute x2, starting transfers between devices, broadcast_view(): lax.ppermute(held, 'view', [(i, (i - step) % count) for i in range(count)])  8.14 us
  transfers between devices with their start and end apart: 9, of which 6 were waited for; matrix products, arithmetic and copies ran while one was open for 7% of the time, Pallas kernels for 0%

profile of v7, /device:TPU:1, one launch (start us, length us, event | category | flops | bytes accessed | tf_op | source)
XLA Modules:
  0.0 146.4 jit_solution(16825541911335080649)
XLA Ops:
  0.0 5.3 %convolution_convert_fusion = bf16[128,3072]{1,0:T(8,128)(2,1)S(1)} fusion(bf16[128,1536]{1,0:T(8,128)(2,1)} %bitcast.49, bf16[1536,3072]{1,0:T(8,128)(2,1)} %param.6), kind=kOutput, calls=%fused_computation | convolution fusion | flops 1208352768 | bytes 10616832 | tf_op jit(solution)/shard_map/dot_general | solution.py:122
  5.4 0.1 copy.15
  5.5 0.1 copy.8
  5.6 1.4 broadcast_in_dim.18
  7.0 12.8 %all-to-all-start = ((bf16[32,64,384]{2,1,0:T(8,128)(2,1)}), bf16[32,64,384]{2,1,0:T(8,128)(2,1)}, u32[]{:S(2)}, u32[]{:S(2)}) async-start(bf16[32,64,384]{2,1,0:T(8,128)(2,1)} %bitcast.45), calls=%async_computation | async-start | bytes 3145728 | tf_op jit(solution)/shard_map/all_to_all | solution.py:137
  20.5 0.7 select_bitcast_fusion
  21.2 2.6 %collective-permute-start.1 = (bf16[64,1536]{1,0:T(8,128)(2,1)}, bf16[64,1536]{1,0:T(8,128)(2,1)}, u32[]{:S(2)}, u32[]{:S(2)}) collective-permute-start(bf16[64,1536]{1,0:T(8,128)(2,1)} %select_bitcast_fusion), channel_id=1, source_target_pairs={{0,224},{32,0},{64,32},{96,64},{128,96},{160,128},{192,160},{224,1... | collective-permute-start | bytes 589832 | tf_op jit(solution)/shard_map/ppermute | solution.py:100
  23.8 0.0 collective-permute-start
  23.8 15.2 %collective-permute-done.1 = bf16[64,1536]{1,0:T(8,128)(2,1)} collective-permute-done((bf16[64,1536]{1,0:T(8,128)(2,1)}, bf16[64,1536]{1,0:T(8,128)(2,1)}, u32[]{:S(2)}, u32[]{:S(2)}) %collective-permute-start.1) | collective-permute-done | bytes 196640 | tf_op jit(solution)/shard_map/ppermute | solution.py:100
  39.0 0.0 collective-permute-done
  39.0 0.7 select_select_fusion
  39.7 5.6 %collective-permute-start.3 = (bf16[64,1536]{1,0:T(8,128)(2,1)}, bf16[64,1536]{1,0:T(8,128)(2,1)S(1)}, u32[]{:S(2)}, u32[]{:S(2)}) collective-permute-start(bf16[64,1536]{1,0:T(8,128)(2,1)} %select_select_fusion), channel_id=1, source_target_pairs={{0,160},{32,192},{64,224},{96,0},{128,32},{160,64},{192,96},{224,1... | collective-permute-start | bytes 589832 | tf_op jit(solution)/shard_map/ppermute | solution.py:100
  45.3 6.7 %collective-permute-done.3 = bf16[64,1536]{1,0:T(8,128)(2,1)S(1)} collective-permute-done((bf16[64,1536]{1,0:T(8,128)(2,1)}, bf16[64,1536]{1,0:T(8,128)(2,1)S(1)}, u32[]{:S(2)}, u32[]{:S(2)}) %collective-permute-start.3) | collective-permute-done | bytes 196640 | tf_op jit(solution)/shard_map/ppermute | solution.py:100
  52.0 5.4 %collective-permute-done.2 = bf16[64,1536]{1,0:T(8,128)(2,1)S(1)} collective-permute-done((bf16[64,1536]{1,0:T(8,128)(2,1)}, bf16[64,1536]{1,0:T(8,128)(2,1)S(1)}, u32[]{:S(2)}, u32[]{:S(2)}) %collective-permute-start.2) | collective-permute-done | bytes 196640 | tf_op jit(solution)/shard_map/ppermute | solution.py:99
  57.3 5.5 %convolution_convert_fusion.1 = bf16[64,3072]{1,0:T(8,128)(2,1)S(1)} fusion(bf16[1536,3072]{1,0:T(8,128)(2,1)} %param.6, bf16[64,1536]{1,0:T(8,128)(2,1)S(1)} %collective-permute-done.2, bf16[64,1536]{1,0:T(8,128)(2,1)S(1)} %collective-permute-done.3, bf16[64,1536]{1,0:T(8,128)(2,1)} %select_select_fusion, pred[]{:T(512)S(6)} %and.35, pred[]{:T(512)S(6)} %and.31), kind=kOutput, calls=%fused_computation.1 | convolution fusion | flops 604372992 | bytes 10420226 | tf_op jit(solution)/shard_map/dot_general | solution.py:128
  62.9 0.1 copy.16
  63.0 0.0 all-to-all-done
  63.0 0.9 broadcast_in_dim.21
  63.9 10.8 %all-to-all-start.1 = ((bf16[32,32,256]{2,1,0:T(8,128)(2,1)}), bf16[32,32,256]{2,1,0:T(8,128)(2,1)}, u32[]{:S(2)}, u32[]{:S(2)}) async-start(bf16[32,32,256]{2,1,0:T(8,128)(2,1)} %bitcast.50), calls=%async_computation.1 | async-start | bytes 1048576 | tf_op jit(solution)/shard_map/all_to_all | solution.py:144
  74.8 2.3 %slice.9 = bf16[2048,256]{1,0:T(8,128)(2,1)} slice(bf16[2048,384]{1,0:T(8,128)(2,1)} %bitcast.7.q_ref.own_ref), slice={[0:2048], [128:384]} | slice | bytes 2097152 | tf_op jit(solution)/shard_map/slice | solution.py:140
  77.0 1.2 collective-permute-start.6
  78.2 2.9 %collective-permute-start.5 = (bf16[2048,256]{1,0:T(8,128)(2,1)}, bf16[2048,256]{1,0:T(8,128)(2,1)}, u32[]{:S(2)}, u32[]{:S(2)}) collective-permute-start(bf16[2048,256]{1,0:T(8,128)(2,1)} %slice.9), channel_id=1, source_target_pairs={{0,1},{1,0},{2,3},{3,2},{4,5},{5,4},{6,7},{7,6},{8,9},{9,8},{10,11... | collective-permute-start | bytes 3145736 | tf_op jit(solution)/shard_map/ppermute | solution.py:147
  81.1 10.9 %all-to-all-done.1 = bf16[32,32,256]{2,1,0:T(8,128)(2,1)} async-done(((bf16[32,32,256]{2,1,0:T(8,128)(2,1)}), bf16[32,32,256]{2,1,0:T(8,128)(2,1)}, u32[]{:S(2)}, u32[]{:S(2)}) %all-to-all-start.1) | async-done | bytes 524320 | tf_op jit(solution)/shard_map/all_to_all | solution.py:144
  92.0 1.2 collective-permute-start.4
  93.2 0.1 constant_dynamic-slice_fusion
  93.3 0.7 copy.13
  94.0 0.6 pad_add_fusion.flag_ref
  94.6 0.5 collective-permute-done.4.anc2_ref
  95.1 12.2 %collective-permute-done.6.rest_6_.rest_7_.rest_8_.rest_9_.rest_10_.rest_11_ = bf16[2048,256]{1,0:T(8,128)(2,1)} collective-permute-done((bf16[2048,256]{1,0:T(8,128)(2,1)}, bf16[2048,256]{1,0:T(8,128)(2,1)}, u32[]{:S(2)}, u32[]{:S(2)}) %collective-permute-start.6) | collective-permute-done | bytes 1048608 | tf_op jit(solution)/shard_map/ppermute | solution.py:153
  107.3 19.8 %shard_map.55 = bf16[1024,128]{1,0:T(8,128)(2,1)} custom-call(s32[8,6]{1,0:T(8,128)} %bitcast.56, s32[2]{0:T(128)} %pad_add_fusion.flag_ref, bf16[2048,384]{1,0:T(8,128)(2,1)} %bitcast.7.q_ref.own_ref, bf16[2048,384]{1,0:T(8,128)(2,1)} %bitcast.7.q_ref.own_ref, bf16[1024,256]{1,0:T(8,128)(2,1)} %bitcast.13.anc_ref, ...), custom_call_target="tpu_custom_call" | custom-call | tf_op jit(solution)/shard_map/pallas_call | solution.py:73
  127.1 18.0 %all_to_all.15 = bf16[16,64,128]{2,1,0:T(8,128)(2,1)S(1)} all-to-all(bf16[16,64,128]{2,1,0:T(8,128)(2,1)} %bitcast.54), channel_id=1, replica_groups=mesh['view'=8,'zh'=2,'zl'=4,'yhi'=2,'core'=2] {'zl','yhi','core'}, dimensions={0} | all-to-all | bytes 524288 | tf_op jit(solution)/shard_map/all_to_all | solution.py:159
  145.0 1.3 fusion
  (10 shorter events, 0.1 us)
Async XLA Ops:
  0.0 145.0 %copy-start = (bf16[1024,1536]{1,0:T(8,128)(2,1)S(1)}, bf16[1024,1536]{1,0:T(8,128)(2,1)}, u32[]{:S(2)}) copy-start(bf16[1024,1536]{1,0:T(8,128)(2,1)} %param.7) | copy-start | bytes 9437188
  0.0 20.5 %copy-start.1 = (bf16[2,64,1536]{2,1,0:T(8,128)(2,1)S(1)}, bf16[2,64,1536]{2,1,0:T(8,128)(2,1)}, u32[]{:S(2)}) copy-start(bf16[2,64,1536]{2,1,0:T(8,128)(2,1)} %param.5) | copy-start | bytes 1179652
  7.0 56.0 %all-to-all-start = ((bf16[32,64,384]{2,1,0:T(8,128)(2,1)}), bf16[32,64,384]{2,1,0:T(8,128)(2,1)}, u32[]{:S(2)}, u32[]{:S(2)}) async-start(bf16[32,64,384]{2,1,0:T(8,128)(2,1)} %bitcast.45), calls=%async_computation | async-start | bytes 3145728 | tf_op jit(solution)/shard_map/all_to_all | solution.py:137
  21.2 17.8 %collective-permute-start.1 = (bf16[64,1536]{1,0:T(8,128)(2,1)}, bf16[64,1536]{1,0:T(8,128)(2,1)}, u32[]{:S(2)}, u32[]{:S(2)}) collective-permute-start(bf16[64,1536]{1,0:T(8,128)(2,1)} %select_bitcast_fusion), channel_id=1, source_target_pairs={{0,224},{32,0},{64,32},{96,64},{128,96},{160,128},{192,160},{224,1... | collective-permute-start | bytes 589832 | tf_op jit(solution)/shard_map/ppermute | solution.py:100
  23.8 15.2 %collective-permute-start = (bf16[64,1536]{1,0:T(8,128)(2,1)}, bf16[64,1536]{1,0:T(8,128)(2,1)}, u32[]{:S(2)}, u32[]{:S(2)}) collective-permute-start(bf16[64,1536]{1,0:T(8,128)(2,1)} %select_bitcast_fusion), channel_id=1, source_target_pairs={{0,32},{32,64},{64,96},{96,128},{128,160},{160,192},{192,224},{224... | collective-permute-start | bytes 589832 | tf_op jit(solution)/shard_map/ppermute | solution.py:99
  39.7 12.2 %collective-permute-start.3 = (bf16[64,1536]{1,0:T(8,128)(2,1)}, bf16[64,1536]{1,0:T(8,128)(2,1)S(1)}, u32[]{:S(2)}, u32[]{:S(2)}) collective-permute-start(bf16[64,1536]{1,0:T(8,128)(2,1)} %select_select_fusion), channel_id=1, source_target_pairs={{0,160},{32,192},{64,224},{96,0},{128,32},{160,64},{192,96},{224,1... | collective-permute-start | bytes 589832 | tf_op jit(solution)/shard_map/ppermute | solution.py:100
  45.3 12.0 %collective-permute-start.2 = (bf16[64,1536]{1,0:T(8,128)(2,1)}, bf16[64,1536]{1,0:T(8,128)(2,1)S(1)}, u32[]{:S(2)}, u32[]{:S(2)}) collective-permute-start(bf16[64,1536]{1,0:T(8,128)(2,1)} %select_select_fusion), channel_id=1, source_target_pairs={{0,96},{32,128},{64,160},{96,192},{128,224},{160,0},{192,32},{224,... | collective-permute-start | bytes 589832 | tf_op jit(solution)/shard_map/ppermute | solution.py:99
  45.3 47.9 %copy-start.2 = (s32[2,16,6]{1,0,2:T(2,128)S(1)}, s32[2,16,6]{1,0,2:T(2,128)}, u32[]{:S(2)}) copy-start(s32[2,16,6]{1,0,2:T(2,128)} %param.9) | copy-start | bytes 2308
  63.9 28.1 %all-to-all-start.1 = ((bf16[32,32,256]{2,1,0:T(8,128)(2,1)}), bf16[32,32,256]{2,1,0:T(8,128)(2,1)}, u32[]{:S(2)}, u32[]{:S(2)}) async-start(bf16[32,32,256]{2,1,0:T(8,128)(2,1)} %bitcast.50), calls=%async_computation.1 | async-start | bytes 1048576 | tf_op jit(solution)/shard_map/all_to_all | solution.py:144
  77.0 30.3 %collective-permute-start.6 = (bf16[2048,256]{1,0:T(8,128)(2,1)}, bf16[2048,256]{1,0:T(8,128)(2,1)}, u32[]{:S(2)}, u32[]{:S(2)}) collective-permute-start(bf16[2048,256]{1,0:T(8,128)(2,1)} %slice.9), channel_id=1, source_target_pairs={{0,225},{1,32},{32,1},{33,64},{64,33},{65,96},{96,65},{97,128},{12... | collective-permute-start | bytes 3145736 | tf_op jit(solution)/shard_map/ppermute | solution.py:153
  78.2 29.1 %collective-permute-start.5 = (bf16[2048,256]{1,0:T(8,128)(2,1)}, bf16[2048,256]{1,0:T(8,128)(2,1)}, u32[]{:S(2)}, u32[]{:S(2)}) collective-permute-start(bf16[2048,256]{1,0:T(8,128)(2,1)} %slice.9), channel_id=1, source_target_pairs={{0,1},{1,0},{2,3},{3,2},{4,5},{5,4},{6,7},{7,6},{8,9},{9,8},{10,11... | collective-permute-start | bytes 3145736 | tf_op jit(solution)/shard_map/ppermute | solution.py:147
  92.0 3.1 %collective-permute-start.4 = (bf16[1024,256]{1,0:T(8,128)(2,1)}, bf16[1024,256]{1,0:T(8,128)(2,1)}, u32[]{:S(2)}, u32[]{:S(2)}) collective-permute-start(bf16[1024,256]{1,0:T(8,128)(2,1)} %bitcast.13.anc_ref), channel_id=1, source_target_pairs={{0,1},{1,0},{2,3},{3,2},{4,5},{5,4},{6,7},{7,6},{8,9},{9,8},{10,11... | collective-permute-start | bytes 1572872 | tf_op jit(solution)/shard_map/ppermute | solution.py:145

commit v8 on v7

--- a/solution.py
+++ b/solution.py
@@ -23,13 +23,13 @@
     slots = epi_ref.shape[1]
     other_refs, far_refs, o_ref = rest[:slots], rest[slots:-1], rest[-1]
     queries = q_ref[...]
-    scale = math.sqrt(HD)
+    inverse = 1.0 / math.sqrt(HD)
 
     def scores_of(keys):
         return lax.dot_general(
             queries, keys, (((1,), (1,)), ((), ())),
             preferred_element_type=jnp.float32,
-        ) / scale
+        ) * inverse
 
     own = own_ref[...]
     anc = anc_ref[...]
@@ -62,13 +62,11 @@
 def attention(epi_rows, flags, resident, anchored, anchored2, other, far, rows):
     slots = epi_rows.shape[1]
 
-    def spec_slot(slot, want_other):
-        def index_map(b, epi, flag):
-            index = epi[b, slot]
-            used = (index >= 0) & ((index < NBLK) == ((flag[0] == 1) == want_other))
-            return (jnp.where(used, jnp.clip(index, 0, 2 * NBLK - 1) % NBLK, 0), 0)
-
-        return pl.BlockSpec((BLK, 2 * HD), index_map)
+    def spec_slot(slot):
+        return pl.BlockSpec(
+            (BLK, 2 * HD),
+            lambda b, epi, flag: (jnp.clip(epi[b, slot], 0, 2 * NBLK - 1) % NBLK, 0),
+        )
 
     return pl.pallas_call(
         attention_kernel,
@@ -82,8 +80,8 @@
                 pl.BlockSpec(anchored.shape, lambda b, epi, flag: (0, 0)),
                 pl.BlockSpec(anchored2.shape, lambda b, epi, flag: (0, 0)),
             ]
-            + [spec_slot(e, True) for e in range(slots)]
-            + [spec_slot(e, False) for e in range(slots)],
+            + [spec_slot(e) for e in range(slots)]
+            + [spec_slot(e) for e in range(slots)],
             out_specs=pl.BlockSpec((BLK, HD), lambda b, epi, flag: (b, 0)),
         ),
     )(epi_rows, flags, resident, resident, anchored, anchored2, *([other] * slots), *([far] * slots))

time: 147 us -> 146 us (level)
  no operation moved by 1% of the time
where the time goes in v8:
time: 146 us; the launch traced here: 145 us
  waiting for transfers between devices  50.8 us (35%)
  starting transfers between devices  37.1 us (25%)
  Pallas kernels  18.6 us (13%)
  blocking collectives  18 us (12%)
  matrix products  12.2 us (8%)
  local copies, waits for them, and re-layouts  5.7 us (4%)
  other arithmetic  2.03 us (1%)
    ppermute x2, waiting for transfers between devices, broadcast_view(): lax.ppermute(held, 'view', [(i, (i - step) % count) for i in range(count)])  21.9 us
    pallas_call x1, Pallas kernels, attention(): pl.pallas_call(attention_kernel, out_shape=jax.ShapeDtypeStruct((rows, HD...  18.6 us
    all_to_all x1, blocking collectives, layer(): returned = lax.all_to_all(attended, HALF, 0, 0, tiled=True)  18 us
    all_to_all x1, starting transfers between devices, to_units(): lax.all_to_all(wide, SUB, 0, 0, tiled=True)  12.8 us
    ppermute x1, waiting for transfers between devices, layer(): far = lax.ppermute(own_kv, ('view', 'core'), pairs)  12.2 us
    all_to_all x1, waiting for transfers between devices, layer(): anchored = lax.all_to_all(wide, SUB, 0, 0, tiled=True).reshape(-1, 2 * HD)  10.9 us
    all_to_all x1, starting transfers between devices, layer(): anchored = lax.all_to_all(wide, SUB, 0, 0, tiled=True).reshape(-1, 2 * HD)  10.8 us
    ppermute x2, starting transfers between devices, broadcast_view(): lax.ppermute(held, 'view', [(i, (i - step) % count) for i in range(count)])  8.14 us
  transfers between devices with their start and end apart: 9, of which 6 were waited for; matrix products, arithmetic and copies ran while one was open for 7% of the time, Pallas kernels for 0%

profile of v8, /device:TPU:1, one launch (start us, length us, event | category | flops | bytes accessed | tf_op | source)
XLA Modules:
  0.0 145.2 jit_solution(8498457189409331377)
XLA Ops:
  0.0 5.3 %convolution_convert_fusion = bf16[128,3072]{1,0:T(8,128)(2,1)S(1)} fusion(bf16[128,1536]{1,0:T(8,128)(2,1)} %bitcast.49, bf16[1536,3072]{1,0:T(8,128)(2,1)} %param.6), kind=kOutput, calls=%fused_computation | convolution fusion | flops 1208352768 | bytes 10616832 | tf_op jit(solution)/shard_map/dot_general | solution.py:120
  5.4 0.1 copy.15
  5.5 0.1 copy.8
  5.6 1.4 broadcast_in_dim.18
  7.0 12.8 %all-to-all-start = ((bf16[32,64,384]{2,1,0:T(8,128)(2,1)}), bf16[32,64,384]{2,1,0:T(8,128)(2,1)}, u32[]{:S(2)}, u32[]{:S(2)}) async-start(bf16[32,64,384]{2,1,0:T(8,128)(2,1)} %bitcast.45), calls=%async_computation | async-start | bytes 3145728 | tf_op jit(solution)/shard_map/all_to_all | solution.py:135
  20.5 0.7 select_bitcast_fusion
  21.2 2.6 %collective-permute-start.1 = (bf16[64,1536]{1,0:T(8,128)(2,1)}, bf16[64,1536]{1,0:T(8,128)(2,1)}, u32[]{:S(2)}, u32[]{:S(2)}) collective-permute-start(bf16[64,1536]{1,0:T(8,128)(2,1)} %select_bitcast_fusion), channel_id=1, source_target_pairs={{0,224},{32,0},{64,32},{96,64},{128,96},{160,128},{192,160},{224,1... | collective-permute-start | bytes 589832 | tf_op jit(solution)/shard_map/ppermute | solution.py:98
  23.8 0.0 collective-permute-start
  23.8 15.2 %collective-permute-done.1 = bf16[64,1536]{1,0:T(8,128)(2,1)} collective-permute-done((bf16[64,1536]{1,0:T(8,128)(2,1)}, bf16[64,1536]{1,0:T(8,128)(2,1)}, u32[]{:S(2)}, u32[]{:S(2)}) %collective-permute-start.1) | collective-permute-done | bytes 196640 | tf_op jit(solution)/shard_map/ppermute | solution.py:98
  39.0 0.0 collective-permute-done
  39.0 0.7 select_select_fusion
  39.7 5.6 %collective-permute-start.3 = (bf16[64,1536]{1,0:T(8,128)(2,1)}, bf16[64,1536]{1,0:T(8,128)(2,1)S(1)}, u32[]{:S(2)}, u32[]{:S(2)}) collective-permute-start(bf16[64,1536]{1,0:T(8,128)(2,1)} %select_select_fusion), channel_id=1, source_target_pairs={{0,160},{32,192},{64,224},{96,0},{128,32},{160,64},{192,96},{224,1... | collective-permute-start | bytes 589832 | tf_op jit(solution)/shard_map/ppermute | solution.py:98
  45.3 6.7 %collective-permute-done.3 = bf16[64,1536]{1,0:T(8,128)(2,1)S(1)} collective-permute-done((bf16[64,1536]{1,0:T(8,128)(2,1)}, bf16[64,1536]{1,0:T(8,128)(2,1)S(1)}, u32[]{:S(2)}, u32[]{:S(2)}) %collective-permute-start.3) | collective-permute-done | bytes 196640 | tf_op jit(solution)/shard_map/ppermute | solution.py:98
  52.0 5.4 %collective-permute-done.2 = bf16[64,1536]{1,0:T(8,128)(2,1)S(1)} collective-permute-done((bf16[64,1536]{1,0:T(8,128)(2,1)}, bf16[64,1536]{1,0:T(8,128)(2,1)S(1)}, u32[]{:S(2)}, u32[]{:S(2)}) %collective-permute-start.2) | collective-permute-done | bytes 196640 | tf_op jit(solution)/shard_map/ppermute | solution.py:97
  57.3 5.5 %convolution_convert_fusion.1 = bf16[64,3072]{1,0:T(8,128)(2,1)S(1)} fusion(bf16[1536,3072]{1,0:T(8,128)(2,1)} %param.6, bf16[64,1536]{1,0:T(8,128)(2,1)S(1)} %collective-permute-done.2, bf16[64,1536]{1,0:T(8,128)(2,1)S(1)} %collective-permute-done.3, bf16[64,1536]{1,0:T(8,128)(2,1)} %select_select_fusion, pred[]{:T(512)S(6)} %and.35, pred[]{:T(512)S(6)} %and.31), kind=kOutput, calls=%fused_computation.1 | convolution fusion | flops 604372992 | bytes 10420226 | tf_op jit(solution)/shard_map/dot_general | solution.py:126
  62.9 0.1 copy.16
  63.0 0.0 all-to-all-done
  63.0 0.9 broadcast_in_dim.21
  63.9 10.8 %all-to-all-start.1 = ((bf16[32,32,256]{2,1,0:T(8,128)(2,1)}), bf16[32,32,256]{2,1,0:T(8,128)(2,1)}, u32[]{:S(2)}, u32[]{:S(2)}) async-start(bf16[32,32,256]{2,1,0:T(8,128)(2,1)} %bitcast.50), calls=%async_computation.1 | async-start | bytes 1048576 | tf_op jit(solution)/shard_map/all_to_all | solution.py:142
  74.8 2.3 %slice.9 = bf16[2048,256]{1,0:T(8,128)(2,1)} slice(bf16[2048,384]{1,0:T(8,128)(2,1)} %bitcast.7.q_ref.own_ref), slice={[0:2048], [128:384]} | slice | bytes 2097152 | tf_op jit(solution)/shard_map/slice | solution.py:138
  77.0 1.2 collective-permute-start.6
  78.2 2.9 %collective-permute-start.5 = (bf16[2048,256]{1,0:T(8,128)(2,1)}, bf16[2048,256]{1,0:T(8,128)(2,1)}, u32[]{:S(2)}, u32[]{:S(2)}) collective-permute-start(bf16[2048,256]{1,0:T(8,128)(2,1)} %slice.9), channel_id=1, source_target_pairs={{0,1},{1,0},{2,3},{3,2},{4,5},{5,4},{6,7},{7,6},{8,9},{9,8},{10,11... | collective-permute-start | bytes 3145736 | tf_op jit(solution)/shard_map/ppermute | solution.py:145
  81.1 10.9 %all-to-all-done.1 = bf16[32,32,256]{2,1,0:T(8,128)(2,1)} async-done(((bf16[32,32,256]{2,1,0:T(8,128)(2,1)}), bf16[32,32,256]{2,1,0:T(8,128)(2,1)}, u32[]{:S(2)}, u32[]{:S(2)}) %all-to-all-start.1) | async-done | bytes 524320 | tf_op jit(solution)/shard_map/all_to_all | solution.py:142
  92.0 1.2 collective-permute-start.4
  93.2 0.1 constant_dynamic-slice_fusion
  93.3 0.7 copy.13
  94.0 0.6 pad_add_fusion.flag_ref
  94.6 0.5 collective-permute-done.4.anc2_ref
  95.1 12.2 %collective-permute-done.6.rest_6_.rest_7_.rest_8_.rest_9_.rest_10_.rest_11_ = bf16[2048,256]{1,0:T(8,128)(2,1)} collective-permute-done((bf16[2048,256]{1,0:T(8,128)(2,1)}, bf16[2048,256]{1,0:T(8,128)(2,1)}, u32[]{:S(2)}, u32[]{:S(2)}) %collective-permute-start.6) | collective-permute-done | bytes 1048608 | tf_op jit(solution)/shard_map/ppermute | solution.py:151
  107.3 18.6 %shard_map.55 = bf16[1024,128]{1,0:T(8,128)(2,1)} custom-call(s32[8,6]{1,0:T(8,128)} %bitcast.56, s32[2]{0:T(128)} %pad_add_fusion.flag_ref, bf16[2048,384]{1,0:T(8,128)(2,1)} %bitcast.7.q_ref.own_ref, bf16[2048,384]{1,0:T(8,128)(2,1)} %bitcast.7.q_ref.own_ref, bf16[1024,256]{1,0:T(8,128)(2,1)} %bitcast.13.anc_ref, ...), custom_call_target="tpu_custom_call" | custom-call | tf_op jit(solution)/shard_map/pallas_call | solution.py:71
  125.9 18.0 %all_to_all.15 = bf16[16,64,128]{2,1,0:T(8,128)(2,1)S(1)} all-to-all(bf16[16,64,128]{2,1,0:T(8,128)(2,1)} %bitcast.54), channel_id=1, replica_groups=mesh['view'=8,'zh'=2,'zl'=4,'yhi'=2,'core'=2] {'zl','yhi','core'}, dimensions={0} | all-to-all | bytes 524288 | tf_op jit(solution)/shard_map/all_to_all | solution.py:157
  143.9 1.3 fusion
  (10 shorter events, 0.1 us)
Async XLA Ops:
  0.0 143.9 %copy-start = (bf16[1024,1536]{1,0:T(8,128)(2,1)S(1)}, bf16[1024,1536]{1,0:T(8,128)(2,1)}, u32[]{:S(2)}) copy-start(bf16[1024,1536]{1,0:T(8,128)(2,1)} %param.7) | copy-start | bytes 9437188
  0.0 20.5 %copy-start.1 = (bf16[2,64,1536]{2,1,0:T(8,128)(2,1)S(1)}, bf16[2,64,1536]{2,1,0:T(8,128)(2,1)}, u32[]{:S(2)}) copy-start(bf16[2,64,1536]{2,1,0:T(8,128)(2,1)} %param.5) | copy-start | bytes 1179652
  7.0 56.0 %all-to-all-start = ((bf16[32,64,384]{2,1,0:T(8,128)(2,1)}), bf16[32,64,384]{2,1,0:T(8,128)(2,1)}, u32[]{:S(2)}, u32[]{:S(2)}) async-start(bf16[32,64,384]{2,1,0:T(8,128)(2,1)} %bitcast.45), calls=%async_computation | async-start | bytes 3145728 | tf_op jit(solution)/shard_map/all_to_all | solution.py:135
  21.2 17.8 %collective-permute-start.1 = (bf16[64,1536]{1,0:T(8,128)(2,1)}, bf16[64,1536]{1,0:T(8,128)(2,1)}, u32[]{:S(2)}, u32[]{:S(2)}) collective-permute-start(bf16[64,1536]{1,0:T(8,128)(2,1)} %select_bitcast_fusion), channel_id=1, source_target_pairs={{0,224},{32,0},{64,32},{96,64},{128,96},{160,128},{192,160},{224,1... | collective-permute-start | bytes 589832 | tf_op jit(solution)/shard_map/ppermute | solution.py:98
  23.8 15.2 %collective-permute-start = (bf16[64,1536]{1,0:T(8,128)(2,1)}, bf16[64,1536]{1,0:T(8,128)(2,1)}, u32[]{:S(2)}, u32[]{:S(2)}) collective-permute-start(bf16[64,1536]{1,0:T(8,128)(2,1)} %select_bitcast_fusion), channel_id=1, source_target_pairs={{0,32},{32,64},{64,96},{96,128},{128,160},{160,192},{192,224},{224... | collective-permute-start | bytes 589832 | tf_op jit(solution)/shard_map/ppermute | solution.py:97
  39.7 12.2 %collective-permute-start.3 = (bf16[64,1536]{1,0:T(8,128)(2,1)}, bf16[64,1536]{1,0:T(8,128)(2,1)S(1)}, u32[]{:S(2)}, u32[]{:S(2)}) collective-permute-start(bf16[64,1536]{1,0:T(8,128)(2,1)} %select_select_fusion), channel_id=1, source_target_pairs={{0,160},{32,192},{64,224},{96,0},{128,32},{160,64},{192,96},{224,1... | collective-permute-start | bytes 589832 | tf_op jit(solution)/shard_map/ppermute | solution.py:98
  45.3 12.0 %collective-permute-start.2 = (bf16[64,1536]{1,0:T(8,128)(2,1)}, bf16[64,1536]{1,0:T(8,128)(2,1)S(1)}, u32[]{:S(2)}, u32[]{:S(2)}) collective-permute-start(bf16[64,1536]{1,0:T(8,128)(2,1)} %select_select_fusion), channel_id=1, source_target_pairs={{0,96},{32,128},{64,160},{96,192},{128,224},{160,0},{192,32},{224,... | collective-permute-start | bytes 589832 | tf_op jit(solution)/shard_map/ppermute | solution.py:97
  45.3 47.9 %copy-start.2 = (s32[2,16,6]{1,0,2:T(2,128)S(1)}, s32[2,16,6]{1,0,2:T(2,128)}, u32[]{:S(2)}) copy-start(s32[2,16,6]{1,0,2:T(2,128)} %param.9) | copy-start | bytes 2308
  63.9 28.1 %all-to-all-start.1 = ((bf16[32,32,256]{2,1,0:T(8,128)(2,1)}), bf16[32,32,256]{2,1,0:T(8,128)(2,1)}, u32[]{:S(2)}, u32[]{:S(2)}) async-start(bf16[32,32,256]{2,1,0:T(8,128)(2,1)} %bitcast.50), calls=%async_computation.1 | async-start | bytes 1048576 | tf_op jit(solution)/shard_map/all_to_all | solution.py:142
  77.0 30.3 %collective-permute-start.6 = (bf16[2048,256]{1,0:T(8,128)(2,1)}, bf16[2048,256]{1,0:T(8,128)(2,1)}, u32[]{:S(2)}, u32[]{:S(2)}) collective-permute-start(bf16[2048,256]{1,0:T(8,128)(2,1)} %slice.9), channel_id=1, source_target_pairs={{0,225},{1,32},{32,1},{33,64},{64,33},{65,96},{96,65},{97,128},{12... | collective-permute-start | bytes 3145736 | tf_op jit(solution)/shard_map/ppermute | solution.py:151
  78.2 29.1 %collective-permute-start.5 = (bf16[2048,256]{1,0:T(8,128)(2,1)}, bf16[2048,256]{1,0:T(8,128)(2,1)}, u32[]{:S(2)}, u32[]{:S(2)}) collective-permute-start(bf16[2048,256]{1,0:T(8,128)(2,1)} %slice.9), channel_id=1, source_target_pairs={{0,1},{1,0},{2,3},{3,2},{4,5},{5,4},{6,7},{7,6},{8,9},{9,8},{10,11... | collective-permute-start | bytes 3145736 | tf_op jit(solution)/shard_map/ppermute | solution.py:145
  92.0 3.1 %collective-permute-start.4 = (bf16[1024,256]{1,0:T(8,128)(2,1)}, bf16[1024,256]{1,0:T(8,128)(2,1)}, u32[]{:S(2)}, u32[]{:S(2)}) collective-permute-start(bf16[1024,256]{1,0:T(8,128)(2,1)} %bitcast.13.anc_ref), channel_id=1, source_target_pairs={{0,1},{1,0},{2,3},{3,2},{4,5},{5,4},{6,7},{7,6},{8,9},{9,8},{10,11... | collective-permute-start | bytes 1572872 | tf_op jit(solution)/shard_map/ppermute | solution.py:143

commit v9 on v8

--- a/solution.py
+++ b/solution.py
@@ -23,19 +23,19 @@
     slots = epi_ref.shape[1]
     other_refs, far_refs, o_ref = rest[:slots], rest[slots:-1], rest[-1]
     queries = q_ref[...]
-    inverse = 1.0 / math.sqrt(HD)
+    scale = math.sqrt(HD)
 
     def scores_of(keys):
         return lax.dot_general(
             queries, keys, (((1,), (1,)), ((), ())),
             preferred_element_type=jnp.float32,
-        ) * inverse
+        ) / scale
 
     own = own_ref[...]
     anc = anc_ref[...]
     anc2 = anc2_ref[...]
     parts = [
-        (scores_of(own[:, HD : 2 * HD]), own[:, 2 * HD :]),
+        (scores_of(own[:, :HD]), own[:, HD : 2 * HD]),
         (scores_of(anc[:, :HD]), anc[:, HD:]),
         (scores_of(anc2[:, :HD]), anc2[:, HD:]),
     ]
@@ -75,7 +75,7 @@
             num_scalar_prefetch=2,
             grid=(rows // BLK,),
             in_specs=[
-                pl.BlockSpec((BLK, HD), lambda b, epi, flag: (flag[1] + b, 0)),
+                pl.BlockSpec((BLK, HD), lambda b, epi, flag: (flag[1] + b, 2)),
                 pl.BlockSpec(resident.shape, lambda b, epi, flag: (0, 0)),
                 pl.BlockSpec(anchored.shape, lambda b, epi, flag: (0, 0)),
                 pl.BlockSpec(anchored2.shape, lambda b, epi, flag: (0, 0)),
@@ -134,21 +134,24 @@
         wide = wide.reshape(tile_n, tile_tokens, width)
         return lax.all_to_all(wide, SUB, 0, 0, tiled=True).reshape(tile_n * tile_tokens, width)
 
-    resident = to_units(projected.reshape(HEADS * per_dev, tile_tokens, 3 * HD))
-    own_kv = resident[:, HD:]
+    resident = to_units(
+        jnp.concatenate([projected[..., HD:], projected[..., :HD]], axis=-1).reshape(
+            HEADS * per_dev, tile_tokens, 3 * HD
+        )
+    )
     halves = anchor_tile.reshape(HEADS * core_n, tile_tokens // core_n, 2 * HD)
     wide = jnp.broadcast_to(halves[None], (tile_n // (HEADS * core_n),) + halves.shape)
     wide = wide.reshape(tile_n, tile_tokens // core_n, 2 * HD)
     anchored = lax.all_to_all(wide, SUB, 0, 0, tiled=True).reshape(-1, 2 * HD)
     anchored2 = lax.ppermute(anchored, "core", [(0, 1), (1, 0)])
 
-    other = lax.ppermute(own_kv, "core", [(0, 1), (1, 0)])
+    other = lax.ppermute(resident, "core", [(0, 1), (1, 0)])
     pairs = []
     for v in range(views_n):
         for c in range(core_n):
             dest_view = (v + 1) % views_n if c == 1 else (v - 1) % views_n
             pairs.append((v * core_n + c, dest_view * core_n + (1 - c)))
-    far = lax.ppermute(own_kv, ("view", "core"), pairs)
+    far = lax.ppermute(resident, ("view", "core"), pairs)
     epi_rows = lax.dynamic_index_in_dim(epi_list, slot, 0, keepdims=False)
     epi_rows = lax.dynamic_slice_in_dim(epi_rows, half * (part_rows // BLK), part_rows // BLK, 0)
     flags = jnp.stack([slot, half * (part_rows // BLK)]).astype(jnp.int32)

time: 146 us -> 144 us (0.986)
  blocking collectives: 18 us -> 51.8 us
  waiting for transfers between devices: 50.8 us -> 29.7 us
  starting transfers between devices: 37.1 us -> 25.7 us
  local copies, waits for them, and re-layouts: 5.7 us -> 2.68 us
    all_to_all x0 -> x1, blocking collectives: none -> 34.5 us  [layer(): anchored = lax.all_to_all(wide, SUB, 0, 0, tiled=True).reshape(-1, 2 * HD)]
    all_to_all x1, waiting for transfers between devices: 0.01 us -> 13.9 us  [to_units(): lax.all_to_all(wide, SUB, 0, 0, tiled=True)]
    ppermute x2, waiting for transfers between devices: 12.2 us -> 0.01 us  [the longest x1 0.01 us: layer(): far = lax.ppermute(resident, ('view', 'core'), pairs)]
    all_to_all x1 -> x0, waiting for transfers between devices: 10.9 us -> none  [layer(): anchored = lax.all_to_all(wide, SUB, 0, 0, tiled=True).reshape(-1, 2 * HD)]
    all_to_all x1 -> x0, starting transfers between devices: 10.8 us -> none  [layer(): anchored = lax.all_to_all(wide, SUB, 0, 0, tiled=True).reshape(-1, 2 * HD)]
    ppermute x2, waiting for transfers between devices: 21.9 us -> 15.2 us  [broadcast_view(): lax.ppermute(held, 'view', [(i, (i - step) % count) for i in range(count)])]
    ppermute x2, waiting for transfers between devices: 5.38 us -> 0.03 us  [broadcast_view(): lax.ppermute(held, 'view', [(i, (i + step) % count) for i in range(count)])]
    slice x1 -> x2, local copies, waits for them, and re-layouts: 2.27 us -> 0.08 us  [the longest x1 0.05 us: layer(): projected[..., :HD]]
  transfers between devices with their start and end apart: 9 -> 8, of which waited for: 6 -> 3; matrix products, arithmetic and copies ran while one was open for 7% -> 6% of each run, Pallas kernels for 0% -> 0%
where the time goes in v9:
time: 144 us
  blocking collectives  51.8 us (36%)
  waiting for transfers between devices  29.7 us (21%)
  starting transfers between devices  25.7 us (18%)
  Pallas kernels  18.8 us (13%)
  matrix products  12.2 us (8%)
  local copies, waits for them, and re-layouts  2.68 us (2%)
  other arithmetic  2.09 us (1%)
    all_to_all x1, blocking collectives, layer(): anchored = lax.all_to_all(wide, SUB, 0, 0, tiled=True).reshape(-1, 2 * HD)  34.5 us
    pallas_call x1, Pallas kernels, attention(): pl.pallas_call(attention_kernel, out_shape=jax.ShapeDtypeStruct((rows, HD...  18.8 us
    all_to_all x1, blocking collectives, layer(): returned = lax.all_to_all(attended, HALF, 0, 0, tiled=True)  17.3 us
    ppermute x2, waiting for transfers between devices, broadcast_view(): lax.ppermute(held, 'view', [(i, (i - step) % count) for i in range(count)])  15.2 us
    all_to_all x1, waiting for transfers between devices, to_units(): lax.all_to_all(wide, SUB, 0, 0, tiled=True)  13.9 us
    all_to_all x1, starting transfers between devices, to_units(): lax.all_to_all(wide, SUB, 0, 0, tiled=True)  12.8 us
    ppermute x2, starting transfers between devices, broadcast_view(): lax.ppermute(held, 'view', [(i, (i - step) % count) for i in range(count)])  8.14 us
    dot_general x1, matrix products, layer(): jnp.dot(anchor_latents, qkv_weight, preferred_element_type=jnp.float32)  5.52 us
  transfers between devices with their start and end apart: 8, of which 3 were waited for; matrix products, arithmetic and copies ran while one was open for 6% of the time, Pallas kernels for 0%

profile of v9, /device:TPU:1, one launch (start us, length us, event | category | flops | bytes accessed | tf_op | source)
XLA Modules:
  0.0 143.8 jit_solution(16109348569422142093)
XLA Ops:
  0.0 5.3 %convolution_convert_fusion = bf16[128,3072]{1,0:T(8,128)(2,1)S(1)} fusion(bf16[128,1536]{1,0:T(8,128)(2,1)} %bitcast.52, bf16[1536,3072]{1,0:T(8,128)(2,1)} %param.6), kind=kOutput, calls=%fused_computation | convolution fusion | flops 1208352768 | bytes 10616832 | tf_op jit(solution)/shard_map/dot_general | solution.py:120
  5.4 0.1 copy.15
  5.5 0.1 copy.18
  5.7 0.1 pad_maximum_fusion
  5.8 0.0 copy-start.1
  5.8 1.4 broadcast_in_dim.18
  7.2 12.8 %all-to-all-start = ((bf16[32,64,384]{2,1,0:T(8,128)(2,1)}), bf16[32,64,384]{2,1,0:T(8,128)(2,1)}, u32[]{:S(2)}, u32[]{:S(2)}) async-start(bf16[32,64,384]{2,1,0:T(8,128)(2,1)} %bitcast.46), calls=%async_computation | async-start | bytes 3145728 | tf_op jit(solution)/shard_map/all_to_all | solution.py:135
  20.7 0.7 select_bitcast_fusion
  21.4 2.6 %collective-permute-start.1 = (bf16[64,1536]{1,0:T(8,128)(2,1)}, bf16[64,1536]{1,0:T(8,128)(2,1)}, u32[]{:S(2)}, u32[]{:S(2)}) collective-permute-start(bf16[64,1536]{1,0:T(8,128)(2,1)} %select_bitcast_fusion), channel_id=1, source_target_pairs={{0,224},{32,0},{64,32},{96,64},{128,96},{160,128},{192,160},{224,1... | collective-permute-start | bytes 589832 | tf_op jit(solution)/shard_map/ppermute | solution.py:98
  24.0 0.0 collective-permute-start
  24.0 15.2 %collective-permute-done.1 = bf16[64,1536]{1,0:T(8,128)(2,1)} collective-permute-done((bf16[64,1536]{1,0:T(8,128)(2,1)}, bf16[64,1536]{1,0:T(8,128)(2,1)}, u32[]{:S(2)}, u32[]{:S(2)}) %collective-permute-start.1) | collective-permute-done | bytes 196640 | tf_op jit(solution)/shard_map/ppermute | solution.py:98
  39.2 0.0 collective-permute-done
  39.2 0.7 select_select_fusion
  40.0 5.6 %collective-permute-start.3 = (bf16[64,1536]{1,0:T(8,128)(2,1)}, bf16[64,1536]{1,0:T(8,128)(2,1)S(1)}, u32[]{:S(2)}, u32[]{:S(2)}) collective-permute-start(bf16[64,1536]{1,0:T(8,128)(2,1)} %select_select_fusion), channel_id=1, source_target_pairs={{0,160},{32,192},{64,224},{96,0},{128,32},{160,64},{192,96},{224,1... | collective-permute-start | bytes 589832 | tf_op jit(solution)/shard_map/ppermute | solution.py:98
  45.5 0.0 collective-permute-start.2
  45.5 13.9 %all-to-all-done = bf16[32,64,384]{2,1,0:T(8,128)(2,1)} async-done(((bf16[32,64,384]{2,1,0:T(8,128)(2,1)}), bf16[32,64,384]{2,1,0:T(8,128)(2,1)}, u32[]{:S(2)}, u32[]{:S(2)}) %all-to-all-start) | async-done | bytes 1572896 | tf_op jit(solution)/shard_map/all_to_all | solution.py:135
  59.4 4.4 %collective-permute-start.6 = (bf16[2048,384]{1,0:T(8,128)(2,1)}, bf16[2048,384]{1,0:T(8,128)(2,1)}, u32[]{:S(2)}, u32[]{:S(2)}) collective-permute-start(bf16[2048,384]{1,0:T(8,128)(2,1)} %bitcast.7.q_ref.own_ref), channel_id=1, source_target_pairs={{0,225},{1,32},{32,1},{33,64},{64,33},{65,96},{96,65},{97,128},{12... | collective-permute-start | bytes 4718600 | tf_op jit(solution)/shard_map/ppermute | solution.py:154
  63.8 0.0 collective-permute-start.5
  63.8 0.0 collective-permute-done.3
  63.8 0.0 collective-permute-done.2
  63.8 5.5 %convolution_convert_fusion.1 = bf16[64,3072]{1,0:T(8,128)(2,1)S(1)} fusion(bf16[1536,3072]{1,0:T(8,128)(2,1)} %param.6, bf16[64,1536]{1,0:T(8,128)(2,1)S(1)} %collective-permute-done.2, bf16[64,1536]{1,0:T(8,128)(2,1)S(1)} %collective-permute-done.3, bf16[64,1536]{1,0:T(8,128)(2,1)} %select_select_fusion, pred[]{:T(512)S(6)} %and.35, pred[]{:T(512)S(6)} %and.31), kind=kOutput, calls=%fused_computation.1 | convolution fusion | flops 604372992 | bytes 10420226 | tf_op jit(solution)/shard_map/dot_general | solution.py:126
  69.4 0.0 copy-start.2
  69.5 0.1 broadcast_in_dim.21
  69.6 34.5 %all_to_all.15 = bf16[32,32,256]{2,1,0:T(8,128)(2,1)} all-to-all(bf16[32,32,256]{2,1,0:T(8,128)(2,1)S(1)} %bitcast.53), channel_id=1, replica_groups=mesh['view'=8,'zh'=2,'zl'=4,'yhi'=2,'core'=2] {'zh','zl','yhi','core'}, dimensions={0} | all-to-all | bytes 1048576 | tf_op jit(solution)/shard_map/all_to_all | solution.py:145
  104.1 0.4 collective-permute-start.4
  104.5 0.1 constant_dynamic-slice_fusion
  104.6 0.7 copy.13
  105.2 0.6 pad_add_fusion.flag_ref
  105.8 0.5 collective-permute-done.4.anc2_ref
  106.4 18.8 %shard_map.55 = bf16[1024,128]{1,0:T(8,128)(2,1)} custom-call(s32[8,6]{1,0:T(8,128)} %bitcast.59, s32[2]{0:T(128)} %pad_add_fusion.flag_ref, bf16[2048,384]{1,0:T(8,128)(2,1)} %bitcast.7.q_ref.own_ref, bf16[2048,384]{1,0:T(8,128)(2,1)} %bitcast.7.q_ref.own_ref, bf16[1024,256]{1,0:T(8,128)(2,1)} %bitcast.13.anc_ref, ...), custom_call_target="tpu_custom_call" | custom-call | tf_op jit(solution)/shard_map/pallas_call | solution.py:71
  125.1 17.3 %all_to_all.16 = bf16[16,64,128]{2,1,0:T(8,128)(2,1)S(1)} all-to-all(bf16[16,64,128]{2,1,0:T(8,128)(2,1)} %bitcast.57), channel_id=1, replica_groups=mesh['view'=8,'zh'=2,'zl'=4,'yhi'=2,'core'=2] {'zl','yhi','core'}, dimensions={0} | all-to-all | bytes 524288 | tf_op jit(solution)/shard_map/all_to_all | solution.py:160
  142.5 1.3 fusion
  (11 shorter events, 0.2 us)
Async XLA Ops:
  0.0 142.5 %copy-start = (bf16[1024,1536]{1,0:T(8,128)(2,1)S(1)}, bf16[1024,1536]{1,0:T(8,128)(2,1)}, u32[]{:S(2)}) copy-start(bf16[1024,1536]{1,0:T(8,128)(2,1)} %param.7) | copy-start | bytes 9437188
  5.8 14.9 %copy-start.1 = (bf16[2,64,1536]{2,1,0:T(8,128)(2,1)S(1)}, bf16[2,64,1536]{2,1,0:T(8,128)(2,1)}, u32[]{:S(2)}) copy-start(bf16[2,64,1536]{2,1,0:T(8,128)(2,1)} %param.5) | copy-start | bytes 1179652
  7.2 52.2 %all-to-all-start = ((bf16[32,64,384]{2,1,0:T(8,128)(2,1)}), bf16[32,64,384]{2,1,0:T(8,128)(2,1)}, u32[]{:S(2)}, u32[]{:S(2)}) async-start(bf16[32,64,384]{2,1,0:T(8,128)(2,1)} %bitcast.46), calls=%async_computation | async-start | bytes 3145728 | tf_op jit(solution)/shard_map/all_to_all | solution.py:135
  21.4 17.8 %collective-permute-start.1 = (bf16[64,1536]{1,0:T(8,128)(2,1)}, bf16[64,1536]{1,0:T(8,128)(2,1)}, u32[]{:S(2)}, u32[]{:S(2)}) collective-permute-start(bf16[64,1536]{1,0:T(8,128)(2,1)} %select_bitcast_fusion), channel_id=1, source_target_pairs={{0,224},{32,0},{64,32},{96,64},{128,96},{160,128},{192,160},{224,1... | collective-permute-start | bytes 589832 | tf_op jit(solution)/shard_map/ppermute | solution.py:98
  24.0 15.2 %collective-permute-start = (bf16[64,1536]{1,0:T(8,128)(2,1)}, bf16[64,1536]{1,0:T(8,128)(2,1)}, u32[]{:S(2)}, u32[]{:S(2)}) collective-permute-start(bf16[64,1536]{1,0:T(8,128)(2,1)} %select_bitcast_fusion), channel_id=1, source_target_pairs={{0,32},{32,64},{64,96},{96,128},{128,160},{160,192},{192,224},{224... | collective-permute-start | bytes 589832 | tf_op jit(solution)/shard_map/ppermute | solution.py:97
  40.0 23.9 %collective-permute-start.3 = (bf16[64,1536]{1,0:T(8,128)(2,1)}, bf16[64,1536]{1,0:T(8,128)(2,1)S(1)}, u32[]{:S(2)}, u32[]{:S(2)}) collective-permute-start(bf16[64,1536]{1,0:T(8,128)(2,1)} %select_select_fusion), channel_id=1, source_target_pairs={{0,160},{32,192},{64,224},{96,0},{128,32},{160,64},{192,96},{224,1... | collective-permute-start | bytes 589832 | tf_op jit(solution)/shard_map/ppermute | solution.py:98
  45.5 18.3 %collective-permute-start.2 = (bf16[64,1536]{1,0:T(8,128)(2,1)}, bf16[64,1536]{1,0:T(8,128)(2,1)S(1)}, u32[]{:S(2)}, u32[]{:S(2)}) collective-permute-start(bf16[64,1536]{1,0:T(8,128)(2,1)} %select_select_fusion), channel_id=1, source_target_pairs={{0,96},{32,128},{64,160},{96,192},{128,224},{160,0},{192,32},{224,... | collective-permute-start | bytes 589832 | tf_op jit(solution)/shard_map/ppermute | solution.py:97
  59.4 46.9 %collective-permute-start.6 = (bf16[2048,384]{1,0:T(8,128)(2,1)}, bf16[2048,384]{1,0:T(8,128)(2,1)}, u32[]{:S(2)}, u32[]{:S(2)}) collective-permute-start(bf16[2048,384]{1,0:T(8,128)(2,1)} %bitcast.7.q_ref.own_ref), channel_id=1, source_target_pairs={{0,225},{1,32},{32,1},{33,64},{64,33},{65,96},{96,65},{97,128},{12... | collective-permute-start | bytes 4718600 | tf_op jit(solution)/shard_map/ppermute | solution.py:154
  63.8 42.5 %collective-permute-start.5 = (bf16[2048,384]{1,0:T(8,128)(2,1)}, bf16[2048,384]{1,0:T(8,128)(2,1)}, u32[]{:S(2)}, u32[]{:S(2)}) collective-permute-start(bf16[2048,384]{1,0:T(8,128)(2,1)} %bitcast.7.q_ref.own_ref), channel_id=1, source_target_pairs={{0,1},{1,0},{2,3},{3,2},{4,5},{5,4},{6,7},{7,6},{8,9},{9,8},{10,11... | collective-permute-start | bytes 4718600 | tf_op jit(solution)/shard_map/ppermute | solution.py:148
  69.4 35.1 %copy-start.2 = (s32[2,16,6]{1,0,2:T(2,128)S(1)}, s32[2,16,6]{1,0,2:T(2,128)}, u32[]{:S(2)}) copy-start(s32[2,16,6]{1,0,2:T(2,128)} %param.9) | copy-start | bytes 2308
  104.1 2.3 %collective-permute-start.4 = (bf16[1024,256]{1,0:T(8,128)(2,1)}, bf16[1024,256]{1,0:T(8,128)(2,1)}, u32[]{:S(2)}, u32[]{:S(2)}) collective-permute-start(bf16[1024,256]{1,0:T(8,128)(2,1)} %bitcast.13.anc_ref), channel_id=1, source_target_pairs={{0,1},{1,0},{2,3},{3,2},{4,5},{5,4},{6,7},{7,6},{8,9},{9,8},{10,11... | collective-permute-start | bytes 1572872 | tf_op jit(solution)/shard_map/ppermute | solution.py:146

commit v10 on v8

--- a/solution.py
+++ b/solution.py
@@ -23,13 +23,13 @@
     slots = epi_ref.shape[1]
     other_refs, far_refs, o_ref = rest[:slots], rest[slots:-1], rest[-1]
     queries = q_ref[...]
-    inverse = 1.0 / math.sqrt(HD)
+    scale = math.sqrt(HD)
 
     def scores_of(keys):
         return lax.dot_general(
             queries, keys, (((1,), (1,)), ((), ())),
             preferred_element_type=jnp.float32,
-        ) * inverse
+        ) / scale
 
     own = own_ref[...]
     anc = anc_ref[...]
@@ -39,14 +39,23 @@
         (scores_of(anc[:, :HD]), anc[:, HD:]),
         (scores_of(anc2[:, :HD]), anc2[:, HD:]),
     ]
+    rows = queries.shape[0]
+    nearby = []
     for slot in range(slots):
         index = epi_ref[block, slot]
-        use_other = (index < NBLK) == (flag_ref[0] == 1)
-        keyvals = jnp.where(use_other, other_refs[slot][...], far_refs[slot][...])
-        scores = jnp.where(index >= 0, scores_of(keyvals[:, :HD]), -jnp.inf)
-        parts.append((scores, keyvals[:, HD:]))
+        valid = index >= 0
+
+        def slot_scores(slot=slot, index=index):
+            use_other = (index < NBLK) == (flag_ref[0] == 1)
+            keyvals = jnp.where(use_other, other_refs[slot][...], far_refs[slot][...])
+            return scores_of(keyvals[:, :HD]), keyvals
+
+        scores, keyvals = slot_scores()
+        nearby.append((valid, jnp.where(valid, scores, -jnp.inf), keyvals))
     peak = parts[0][0].max(axis=1, keepdims=True)
     for scores, _ in parts[1:]:
+        peak = jnp.maximum(peak, scores.max(axis=1, keepdims=True))
+    for _, scores, _ in nearby:
         peak = jnp.maximum(peak, scores.max(axis=1, keepdims=True))
     total = None
     summed = None
@@ -56,6 +65,20 @@
         prod = jnp.dot(raised.astype(jnp.bfloat16), values, preferred_element_type=jnp.float32)
         total = row if total is None else total + row
         summed = prod if summed is None else summed + prod
+    for valid, scores, values in nearby:
+        def slot_sums(scores=scores, values=values):
+            raised = jnp.exp(scores - peak)
+            return (
+                raised.sum(axis=1, keepdims=True),
+                jnp.dot(raised.astype(jnp.bfloat16), values[:, HD:], preferred_element_type=jnp.float32),
+            )
+
+        def no_sums():
+            return jnp.zeros((rows, 1), jnp.float32), jnp.zeros((rows, HD), jnp.float32)
+
+        row, prod = lax.cond(valid, slot_sums, no_sums)
+        total = total + row
+        summed = summed + prod
     o_ref[...] = (summed / total).astype(o_ref.dtype)
 
 

time: 146 us -> 148 us (1.014)
  no operation moved by 1% of the time
where the time goes in v10:
time: 148 us; the launch traced here: 147 us
  waiting for transfers between devices  50.8 us (34%)
  starting transfers between devices  37.1 us (25%)
  Pallas kernels  19.9 us (13%)
  blocking collectives  18 us (12%)
  matrix products  12.2 us (8%)
  local copies, waits for them, and re-layouts  5.7 us (4%)
  other arithmetic  2.03 us (1%)
    ppermute x2, waiting for transfers between devices, broadcast_view(): lax.ppermute(held, 'view', [(i, (i - step) % count) for i in range(count)])  21.9 us
    pallas_call x1, Pallas kernels, attention(): pl.pallas_call(attention_kernel, out_shape=jax.ShapeDtypeStruct((rows, HD...  19.9 us
    all_to_all x1, blocking collectives, layer(): returned = lax.all_to_all(attended, HALF, 0, 0, tiled=True)  18 us
    all_to_all x1, starting transfers between devices, to_units(): lax.all_to_all(wide, SUB, 0, 0, tiled=True)  12.8 us
    ppermute x1, waiting for transfers between devices, layer(): far = lax.ppermute(own_kv, ('view', 'core'), pairs)  12.2 us
    all_to_all x1, waiting for transfers between devices, layer(): anchored = lax.all_to_all(wide, SUB, 0, 0, tiled=True).reshape(-1, 2 * HD)  10.9 us
    all_to_all x1, starting transfers between devices, layer(): anchored = lax.all_to_all(wide, SUB, 0, 0, tiled=True).reshape(-1, 2 * HD)  10.8 us
    ppermute x2, starting transfers between devices, broadcast_view(): lax.ppermute(held, 'view', [(i, (i - step) % count) for i in range(count)])  8.14 us
  transfers between devices with their start and end apart: 9, of which 6 were waited for; matrix products, arithmetic and copies ran while one was open for 7% of the time, Pallas kernels for 0%

profile of v10, /device:TPU:1, one launch (start us, length us, event | category | flops | bytes accessed | tf_op | source)
XLA Modules:
  0.0 146.6 jit_solution(2173657720474206439)
XLA Ops:
  0.0 5.3 %convolution_convert_fusion = bf16[128,3072]{1,0:T(8,128)(2,1)S(1)} fusion(bf16[128,1536]{1,0:T(8,128)(2,1)} %bitcast.49, bf16[1536,3072]{1,0:T(8,128)(2,1)} %param.6), kind=kOutput, calls=%fused_computation | convolution fusion | flops 1208352768 | bytes 10616832 | tf_op jit(solution)/shard_map/dot_general | solution.py:143
  5.4 0.1 copy.15
  5.5 0.1 copy.8
  5.6 1.4 broadcast_in_dim.18
  7.0 12.8 %all-to-all-start = ((bf16[32,64,384]{2,1,0:T(8,128)(2,1)}), bf16[32,64,384]{2,1,0:T(8,128)(2,1)}, u32[]{:S(2)}, u32[]{:S(2)}) async-start(bf16[32,64,384]{2,1,0:T(8,128)(2,1)} %bitcast.45), calls=%async_computation | async-start | bytes 3145728 | tf_op jit(solution)/shard_map/all_to_all | solution.py:158
  20.5 0.7 select_bitcast_fusion
  21.2 2.6 %collective-permute-start.1 = (bf16[64,1536]{1,0:T(8,128)(2,1)}, bf16[64,1536]{1,0:T(8,128)(2,1)}, u32[]{:S(2)}, u32[]{:S(2)}) collective-permute-start(bf16[64,1536]{1,0:T(8,128)(2,1)} %select_bitcast_fusion), channel_id=1, source_target_pairs={{0,224},{32,0},{64,32},{96,64},{128,96},{160,128},{192,160},{224,1... | collective-permute-start | bytes 589832 | tf_op jit(solution)/shard_map/ppermute | solution.py:121
  23.8 0.0 collective-permute-start
  23.8 15.2 %collective-permute-done.1 = bf16[64,1536]{1,0:T(8,128)(2,1)} collective-permute-done((bf16[64,1536]{1,0:T(8,128)(2,1)}, bf16[64,1536]{1,0:T(8,128)(2,1)}, u32[]{:S(2)}, u32[]{:S(2)}) %collective-permute-start.1) | collective-permute-done | bytes 196640 | tf_op jit(solution)/shard_map/ppermute | solution.py:121
  39.0 0.0 collective-permute-done
  39.0 0.7 select_select_fusion
  39.7 5.6 %collective-permute-start.3 = (bf16[64,1536]{1,0:T(8,128)(2,1)}, bf16[64,1536]{1,0:T(8,128)(2,1)S(1)}, u32[]{:S(2)}, u32[]{:S(2)}) collective-permute-start(bf16[64,1536]{1,0:T(8,128)(2,1)} %select_select_fusion), channel_id=1, source_target_pairs={{0,160},{32,192},{64,224},{96,0},{128,32},{160,64},{192,96},{224,1... | collective-permute-start | bytes 589832 | tf_op jit(solution)/shard_map/ppermute | solution.py:121
  45.3 6.7 %collective-permute-done.3 = bf16[64,1536]{1,0:T(8,128)(2,1)S(1)} collective-permute-done((bf16[64,1536]{1,0:T(8,128)(2,1)}, bf16[64,1536]{1,0:T(8,128)(2,1)S(1)}, u32[]{:S(2)}, u32[]{:S(2)}) %collective-permute-start.3) | collective-permute-done | bytes 196640 | tf_op jit(solution)/shard_map/ppermute | solution.py:121
  52.0 5.4 %collective-permute-done.2 = bf16[64,1536]{1,0:T(8,128)(2,1)S(1)} collective-permute-done((bf16[64,1536]{1,0:T(8,128)(2,1)}, bf16[64,1536]{1,0:T(8,128)(2,1)S(1)}, u32[]{:S(2)}, u32[]{:S(2)}) %collective-permute-start.2) | collective-permute-done | bytes 196640 | tf_op jit(solution)/shard_map/ppermute | solution.py:120
  57.3 5.5 %convolution_convert_fusion.1 = bf16[64,3072]{1,0:T(8,128)(2,1)S(1)} fusion(bf16[1536,3072]{1,0:T(8,128)(2,1)} %param.6, bf16[64,1536]{1,0:T(8,128)(2,1)S(1)} %collective-permute-done.2, bf16[64,1536]{1,0:T(8,128)(2,1)S(1)} %collective-permute-done.3, bf16[64,1536]{1,0:T(8,128)(2,1)} %select_select_fusion, pred[]{:T(512)S(6)} %and.35, pred[]{:T(512)S(6)} %and.31), kind=kOutput, calls=%fused_computation.1 | convolution fusion | flops 604372992 | bytes 10420226 | tf_op jit(solution)/shard_map/dot_general | solution.py:149
  62.9 0.1 copy.16
  63.0 0.0 all-to-all-done
  63.0 0.9 broadcast_in_dim.21
  63.9 10.8 %all-to-all-start.1 = ((bf16[32,32,256]{2,1,0:T(8,128)(2,1)}), bf16[32,32,256]{2,1,0:T(8,128)(2,1)}, u32[]{:S(2)}, u32[]{:S(2)}) async-start(bf16[32,32,256]{2,1,0:T(8,128)(2,1)} %bitcast.50), calls=%async_computation.1 | async-start | bytes 1048576 | tf_op jit(solution)/shard_map/all_to_all | solution.py:165
  74.8 2.3 %slice.9 = bf16[2048,256]{1,0:T(8,128)(2,1)} slice(bf16[2048,384]{1,0:T(8,128)(2,1)} %bitcast.7.q_ref.own_ref), slice={[0:2048], [128:384]} | slice | bytes 2097152 | tf_op jit(solution)/shard_map/slice | solution.py:161
  77.0 1.2 collective-permute-start.6
  78.2 2.9 %collective-permute-start.5 = (bf16[2048,256]{1,0:T(8,128)(2,1)}, bf16[2048,256]{1,0:T(8,128)(2,1)}, u32[]{:S(2)}, u32[]{:S(2)}) collective-permute-start(bf16[2048,256]{1,0:T(8,128)(2,1)} %slice.9), channel_id=1, source_target_pairs={{0,1},{1,0},{2,3},{3,2},{4,5},{5,4},{6,7},{7,6},{8,9},{9,8},{10,11... | collective-permute-start | bytes 3145736 | tf_op jit(solution)/shard_map/ppermute | solution.py:168
  81.1 10.9 %all-to-all-done.1 = bf16[32,32,256]{2,1,0:T(8,128)(2,1)} async-done(((bf16[32,32,256]{2,1,0:T(8,128)(2,1)}), bf16[32,32,256]{2,1,0:T(8,128)(2,1)}, u32[]{:S(2)}, u32[]{:S(2)}) %all-to-all-start.1) | async-done | bytes 524320 | tf_op jit(solution)/shard_map/all_to_all | solution.py:165
  92.0 1.2 collective-permute-start.4
  93.2 0.1 constant_dynamic-slice_fusion
  93.3 0.7 copy.13
  94.0 0.6 pad_add_fusion.flag_ref
  94.6 0.5 collective-permute-done.4.anc2_ref
  95.1 12.2 %collective-permute-done.6.rest_6_.rest_7_.rest_8_.rest_9_.rest_10_.rest_11_ = bf16[2048,256]{1,0:T(8,128)(2,1)} collective-permute-done((bf16[2048,256]{1,0:T(8,128)(2,1)}, bf16[2048,256]{1,0:T(8,128)(2,1)}, u32[]{:S(2)}, u32[]{:S(2)}) %collective-permute-start.6) | collective-permute-done | bytes 1048608 | tf_op jit(solution)/shard_map/ppermute | solution.py:174
  107.3 19.9 %shard_map.55 = bf16[1024,128]{1,0:T(8,128)(2,1)} custom-call(s32[8,6]{1,0:T(8,128)} %bitcast.56, s32[2]{0:T(128)} %pad_add_fusion.flag_ref, bf16[2048,384]{1,0:T(8,128)(2,1)} %bitcast.7.q_ref.own_ref, bf16[2048,384]{1,0:T(8,128)(2,1)} %bitcast.7.q_ref.own_ref, bf16[1024,256]{1,0:T(8,128)(2,1)} %bitcast.13.anc_ref, ...), custom_call_target="tpu_custom_call" | custom-call | tf_op jit(solution)/shard_map/pallas_call | solution.py:94
  127.2 18.0 %all_to_all.15 = bf16[16,64,128]{2,1,0:T(8,128)(2,1)S(1)} all-to-all(bf16[16,64,128]{2,1,0:T(8,128)(2,1)} %bitcast.54), channel_id=1, replica_groups=mesh['view'=8,'zh'=2,'zl'=4,'yhi'=2,'core'=2] {'zl','yhi','core'}, dimensions={0} | all-to-all | bytes 524288 | tf_op jit(solution)/shard_map/all_to_all | solution.py:180
  145.2 1.3 fusion
  (10 shorter events, 0.1 us)
Async XLA Ops:
  0.0 145.2 %copy-start = (bf16[1024,1536]{1,0:T(8,128)(2,1)S(1)}, bf16[1024,1536]{1,0:T(8,128)(2,1)}, u32[]{:S(2)}) copy-start(bf16[1024,1536]{1,0:T(8,128)(2,1)} %param.7) | copy-start | bytes 9437188
  0.0 20.5 %copy-start.1 = (bf16[2,64,1536]{2,1,0:T(8,128)(2,1)S(1)}, bf16[2,64,1536]{2,1,0:T(8,128)(2,1)}, u32[]{:S(2)}) copy-start(bf16[2,64,1536]{2,1,0:T(8,128)(2,1)} %param.5) | copy-start | bytes 1179652
  7.0 56.0 %all-to-all-start = ((bf16[32,64,384]{2,1,0:T(8,128)(2,1)}), bf16[32,64,384]{2,1,0:T(8,128)(2,1)}, u32[]{:S(2)}, u32[]{:S(2)}) async-start(bf16[32,64,384]{2,1,0:T(8,128)(2,1)} %bitcast.45), calls=%async_computation | async-start | bytes 3145728 | tf_op jit(solution)/shard_map/all_to_all | solution.py:158
  21.2 17.8 %collective-permute-start.1 = (bf16[64,1536]{1,0:T(8,128)(2,1)}, bf16[64,1536]{1,0:T(8,128)(2,1)}, u32[]{:S(2)}, u32[]{:S(2)}) collective-permute-start(bf16[64,1536]{1,0:T(8,128)(2,1)} %select_bitcast_fusion), channel_id=1, source_target_pairs={{0,224},{32,0},{64,32},{96,64},{128,96},{160,128},{192,160},{224,1... | collective-permute-start | bytes 589832 | tf_op jit(solution)/shard_map/ppermute | solution.py:121
  23.8 15.2 %collective-permute-start = (bf16[64,1536]{1,0:T(8,128)(2,1)}, bf16[64,1536]{1,0:T(8,128)(2,1)}, u32[]{:S(2)}, u32[]{:S(2)}) collective-permute-start(bf16[64,1536]{1,0:T(8,128)(2,1)} %select_bitcast_fusion), channel_id=1, source_target_pairs={{0,32},{32,64},{64,96},{96,128},{128,160},{160,192},{192,224},{224... | collective-permute-start | bytes 589832 | tf_op jit(solution)/shard_map/ppermute | solution.py:120
  39.7 12.2 %collective-permute-start.3 = (bf16[64,1536]{1,0:T(8,128)(2,1)}, bf16[64,1536]{1,0:T(8,128)(2,1)S(1)}, u32[]{:S(2)}, u32[]{:S(2)}) collective-permute-start(bf16[64,1536]{1,0:T(8,128)(2,1)} %select_select_fusion), channel_id=1, source_target_pairs={{0,160},{32,192},{64,224},{96,0},{128,32},{160,64},{192,96},{224,1... | collective-permute-start | bytes 589832 | tf_op jit(solution)/shard_map/ppermute | solution.py:121
  45.3 12.0 %collective-permute-start.2 = (bf16[64,1536]{1,0:T(8,128)(2,1)}, bf16[64,1536]{1,0:T(8,128)(2,1)S(1)}, u32[]{:S(2)}, u32[]{:S(2)}) collective-permute-start(bf16[64,1536]{1,0:T(8,128)(2,1)} %select_select_fusion), channel_id=1, source_target_pairs={{0,96},{32,128},{64,160},{96,192},{128,224},{160,0},{192,32},{224,... | collective-permute-start | bytes 589832 | tf_op jit(solution)/shard_map/ppermute | solution.py:120
  45.3 47.9 %copy-start.2 = (s32[2,16,6]{1,0,2:T(2,128)S(1)}, s32[2,16,6]{1,0,2:T(2,128)}, u32[]{:S(2)}) copy-start(s32[2,16,6]{1,0,2:T(2,128)} %param.9) | copy-start | bytes 2308
  63.9 28.1 %all-to-all-start.1 = ((bf16[32,32,256]{2,1,0:T(8,128)(2,1)}), bf16[32,32,256]{2,1,0:T(8,128)(2,1)}, u32[]{:S(2)}, u32[]{:S(2)}) async-start(bf16[32,32,256]{2,1,0:T(8,128)(2,1)} %bitcast.50), calls=%async_computation.1 | async-start | bytes 1048576 | tf_op jit(solution)/shard_map/all_to_all | solution.py:165
  77.0 30.3 %collective-permute-start.6 = (bf16[2048,256]{1,0:T(8,128)(2,1)}, bf16[2048,256]{1,0:T(8,128)(2,1)}, u32[]{:S(2)}, u32[]{:S(2)}) collective-permute-start(bf16[2048,256]{1,0:T(8,128)(2,1)} %slice.9), channel_id=1, source_target_pairs={{0,225},{1,32},{32,1},{33,64},{64,33},{65,96},{96,65},{97,128},{12... | collective-permute-start | bytes 3145736 | tf_op jit(solution)/shard_map/ppermute | solution.py:174
  78.2 29.1 %collective-permute-start.5 = (bf16[2048,256]{1,0:T(8,128)(2,1)}, bf16[2048,256]{1,0:T(8,128)(2,1)}, u32[]{:S(2)}, u32[]{:S(2)}) collective-permute-start(bf16[2048,256]{1,0:T(8,128)(2,1)} %slice.9), channel_id=1, source_target_pairs={{0,1},{1,0},{2,3},{3,2},{4,5},{5,4},{6,7},{7,6},{8,9},{9,8},{10,11... | collective-permute-start | bytes 3145736 | tf_op jit(solution)/shard_map/ppermute | solution.py:168
  92.0 3.1 %collective-permute-start.4 = (bf16[1024,256]{1,0:T(8,128)(2,1)}, bf16[1024,256]{1,0:T(8,128)(2,1)}, u32[]{:S(2)}, u32[]{:S(2)}) collective-permute-start(bf16[1024,256]{1,0:T(8,128)(2,1)} %bitcast.13.anc_ref), channel_id=1, source_target_pairs={{0,1},{1,0},{2,3},{3,2},{4,5},{5,4},{6,7},{7,6},{8,9},{9,8},{10,11... | collective-permute-start | bytes 1572872 | tf_op jit(solution)/shard_map/ppermute | solution.py:166
